TPU v7x, 128 devices: a whole 4x4x4 slice. The times are simulated.
128 devices in a mesh: req: 16 (over y, x), kv: 8 (over z, core).
Axes of the slice: x: 4, y: 4, z: 4, core: 2. Of those that a mesh axis runs over, the one named last changes fastest.
Arguments:
- hidden: bfloat16 [1024, 1536], P('req', 'kv'), may hold values from -6 to 6
- perm: int32 [1024], replicated, may hold values from 0 to 1023, as said below
- seq_lens: int32 [1024], P('req'), may hold values from 1 to 4096, as said below
- page_table: int32 [1024, 32], P('req'), may hold values from 0 to 319, as said below
- kv_cache: bfloat16 [5120, 8, 128, 128], P('req', 'kv'), may hold values from -52 to 52
- attn_gain: float32 [1536], replicated, may hold values from 0.1 to 1.9
- qkv_weight: bfloat16 [8, 1536, 320], P('kv'), may hold values from -0.15625 to 0.15625
- out_weight: bfloat16 [8, 192, 1536], P('kv'), may hold values from -1 to 1
- ffn_gain: float32 [1536], replicated, may hold values from 0.1 to 1.9
- router: bfloat16 [1536, 16], replicated, may hold values from -0.15625 to 0.15625
- routes: int32 [1024, 2], P(('req', 'kv')), may hold values from 0 to 15, all different within a row; in each aligned block of 8 rows (0 to 7, 8 to 15, ...) at most 2 rows name the same one
- gate_up: bfloat16 [16, 1536, 2048], P('req'), may hold values from -0.15625 to 0.15625
- down: bfloat16 [16, 1024, 1536], P('req'), may hold values from -0.1875 to 0.1875
Outputs:
- mixed: bfloat16 [1024, 1536], P(('req', 'kv'))
Inputs may be any that keep to these rules, and one draw needn't show every extreme that they name: A permutation of the 1024 requests: slot s holds request perm[s]. The 64 slots of each index of req hold exactly 4 requests from each block of 64 consecutive requests. `seq_lens`: the length 4096 is reached on every index of req. `page_table`: entries 0 to (seq_lens[s] + 127) // 128 - 1 of row s are used; no page of one index of req is used by two of its slots; later entries name arbitrary pages.
All inputs are finite; a program needn't handle non-finite values.
Results may differ from a plain program's by a relative error of at most 0.017.
Values may be sent and summed in bfloat16 or wider, within the bound.
No kernel may reach another device: no remote copies, remote signals or barrier semaphores. Data moves between devices by JAX's collectives and lax.ppermute only.
A program may use at most 128 MiB of HBM per device.

v0:
```python
import jax
import jax.numpy as jnp
from jax import lax
from jax.sharding import PartitionSpec as P

REQ_DEV = 64


NEG_FILL = -1e30
EPS_NORM = 1e-05


def rms_norm(values, gain_vec):
    values = values.astype(jnp.float32)
    factor = lax.rsqrt(jnp.mean(values * values, axis=-1, keepdims=True) + EPS_NORM)
    return (values * factor * gain_vec).astype(jnp.bfloat16)


def attend(normed, seq_lens, page_table, kv_cache, qkv_weight):
    pool_pages, local_heads, twice_hd, page_len = kv_cache.shape
    head_dim = twice_hd // 2
    slot_count = normed.shape[0]
    groups = qkv_weight.shape[2] // head_dim - 2
    max_pages = page_table.shape[1]
    projected = jnp.einsum("sd,hdc->shc", normed, qkv_weight, preferred_element_type=jnp.float32)
    queries = (
        projected[:, :, : groups * head_dim]
        .reshape(slot_count, local_heads, groups, head_dim)
        .astype(jnp.bfloat16)
    )
    key_new = projected[:, :, groups * head_dim : (groups + 1) * head_dim].astype(jnp.bfloat16)
    value_new = projected[:, :, (groups + 1) * head_dim :].astype(jnp.bfloat16)
    page_need = (seq_lens + page_len - 1) // page_len
    page_ids = jnp.arange(max_pages, dtype=jnp.int32)
    in_use = page_ids[None, :] < page_need[:, None]
    target_page = jnp.where(in_use, page_table, pool_pages).reshape(-1)
    slot_ids = jnp.broadcast_to(
        jnp.arange(slot_count, dtype=jnp.int32)[:, None], (slot_count, max_pages)
    ).reshape(-1)
    order_ids = jnp.broadcast_to(page_ids[None, :], (slot_count, max_pages)).reshape(-1)
    owner = (
        jnp.full((pool_pages,), slot_count, jnp.int32).at[target_page].set(slot_ids, mode="drop")
    )
    page_order = jnp.zeros((pool_pages,), jnp.int32).at[target_page].set(order_ids, mode="drop")
    owner_safe = jnp.minimum(owner, slot_count - 1)
    position = page_order[:, None] * page_len + jnp.arange(page_len, dtype=jnp.int32)[None, :]
    live = (owner[:, None] < slot_count) & (position < jnp.take(seq_lens, owner_safe)[:, None])
    scale_factor = head_dim ** (-0.5)
    page_queries = jnp.take(queries, owner_safe, axis=0)
    scores = (
        jnp.einsum(
            "pkgd,pkdt->pkgt",
            page_queries,
            kv_cache[:, :, :head_dim, :],
            preferred_element_type=jnp.float32,
        )
        * scale_factor
    )
    scores = jnp.where(live[:, None, None, :], scores, NEG_FILL)
    score_new = (
        jnp.einsum("skgd,skd->skg", queries, key_new, preferred_element_type=jnp.float32)
        * scale_factor
    )
    page_peak = jnp.max(scores, axis=3)
    belongs = owner[None, :] == jnp.arange(slot_count, dtype=jnp.int32)[:, None]
    slot_peak = jnp.max(jnp.where(belongs[:, :, None, None], page_peak[None], NEG_FILL), axis=1)
    slot_peak = jnp.maximum(slot_peak, score_new)
    weights = jnp.where(
        live[:, None, None, :],
        jnp.exp(scores - jnp.take(slot_peak, owner_safe, axis=0)[..., None]),
        0.0,
    )
    page_total = jnp.sum(weights, axis=3)
    page_value = jnp.einsum(
        "pkgt,pkdt->pkgd",
        weights.astype(jnp.bfloat16),
        kv_cache[:, :, head_dim:, :],
        preferred_element_type=jnp.float32,
    )
    belongs_f = belongs.astype(jnp.float32)
    total_sum = jnp.dot(
        belongs_f, page_total.reshape(pool_pages, -1), precision=lax.Precision.HIGHEST
    ).reshape(slot_count, local_heads, groups)
    value_sum = jnp.dot(
        belongs_f, page_value.reshape(pool_pages, -1), precision=lax.Precision.HIGHEST
    ).reshape(slot_count, local_heads, groups, head_dim)
    weight_new = jnp.exp(score_new - slot_peak)
    total_sum = total_sum + weight_new
    rounded_new = lax.optimization_barrier(weight_new.astype(jnp.bfloat16)).astype(jnp.float32)
    value_sum = value_sum + rounded_new[..., None] * value_new.astype(jnp.float32)[:, :, None, :]
    return (value_sum / total_sum[..., None]).astype(jnp.bfloat16).reshape(slot_count, -1)


def expert_apply(piece, gate_up, down):
    n_source, slot_num, local_experts, width = piece.shape
    rows_in = piece.transpose(2, 0, 1, 3).reshape(local_experts, n_source * slot_num, width)
    projected_up = jnp.einsum("erd,edf->erf", rows_in, gate_up, preferred_element_type=jnp.float32)
    hidden_units = gate_up.shape[2] // 2
    acts = (
        jax.nn.silu(projected_up[..., :hidden_units]) * projected_up[..., hidden_units:]
    ).astype(jnp.bfloat16)
    result = jnp.einsum("erf,efd->erd", acts, down, preferred_element_type=jnp.float32).astype(
        jnp.bfloat16
    )
    return result.reshape(local_experts, n_source, slot_num, width).transpose(1, 2, 0, 3)


def shards(
    hidden,
    perm,
    seq_lens,
    page_table,
    kv_cache,
    attn_gain,
    qkv_weight,
    out_weight,
    ffn_gain,
    router,
    routes,
    gate_up,
    down,
):
    req_index = lax.axis_index("req")
    kv_index = lax.axis_index("kv")
    every_row = lax.all_gather(hidden, "req", axis=0, tiled=True)
    my_perm = lax.dynamic_slice_in_dim(perm, req_index * REQ_DEV, REQ_DEV)
    picked_rows = jnp.take(every_row, my_perm, axis=0)
    tokens = lax.all_gather(picked_rows, "kv", axis=1, tiled=True)
    normed = rms_norm(tokens, attn_gain)
    head_out = attend(normed, seq_lens, page_table, kv_cache, qkv_weight)
    sub_rows = routes.shape[0]
    width = tokens.shape[1]
    out_flat = out_weight.reshape(-1, out_weight.shape[2])
    attn_rows = lax.psum_scatter(
        jnp.dot(head_out, out_flat, preferred_element_type=jnp.float32).astype(jnp.bfloat16),
        "kv",
        scatter_dimension=0,
        tiled=True,
    ).astype(jnp.float32)
    own_tokens = lax.dynamic_slice_in_dim(tokens, kv_index * sub_rows, sub_rows, 0)
    residual = (own_tokens.astype(jnp.float32) + attn_rows).astype(jnp.bfloat16)
    normed_ffn = rms_norm(residual, ffn_gain)
    logits = jnp.dot(normed_ffn, router, preferred_element_type=jnp.float32)
    chosen = jnp.take_along_axis(logits, routes, axis=1)
    sigmoid_vals = jax.nn.sigmoid(chosen)
    gates = sigmoid_vals / jnp.sum(sigmoid_vals, axis=1, keepdims=True)
    experts_all = router.shape[1]
    n_req = lax.axis_size("req")
    local_experts = gate_up.shape[0]
    capacity = max(2, 2 * sub_rows // experts_all + 1)
    flat_routes = routes.reshape(-1)
    onehot_int = (flat_routes[:, None] == jnp.arange(experts_all, dtype=jnp.int32)[None, :]).astype(
        jnp.int32
    )
    earlier = jnp.cumsum(onehot_int, axis=0) - onehot_int
    rank_in = jnp.sum(earlier * onehot_int, axis=1)
    place_at = (
        flat_routes // local_experts * capacity * local_experts
        + rank_in * local_experts
        + flat_routes % local_experts
    )
    placement_plan = (
        place_at[:, None] == jnp.arange(experts_all * capacity, dtype=jnp.int32)[None, :]
    ).astype(jnp.bfloat16)
    paired_rows = jnp.repeat(normed_ffn, 2, axis=0)
    outgoing = jnp.einsum(
        "qe,qd->ed", placement_plan, paired_rows, preferred_element_type=jnp.float32
    )
    outgoing = outgoing.astype(jnp.bfloat16).reshape(n_req, capacity, local_experts, width)
    arrived = lax.all_to_all(outgoing, "req", split_axis=0, concat_axis=0, tiled=True)
    returned = lax.all_to_all(
        expert_apply(arrived, gate_up, down), "req", split_axis=0, concat_axis=0, tiled=True
    )
    back_rows = returned.reshape(experts_all * capacity, width)
    paired_output = jnp.dot(placement_plan, back_rows, preferred_element_type=jnp.float32).reshape(
        sub_rows, 2, width
    )
    mixed = residual.astype(jnp.float32) + jnp.sum(gates[:, :, None] * paired_output, axis=1)
    return mixed.astype(jnp.bfloat16)


def solution(mesh):
    in_specs = (
        P("req", "kv"),
        P(),
        P("req"),
        P("req", None),
        P("req", "kv", None, None),
        P(),
        P("kv", None, None),
        P("kv", None, None),
        P(),
        P(),
        P(("req", "kv"), None),
        P("req", None, None),
        P("req", None, None),
    )
    out_specs = P(("req", "kv"), None)
    return jax.shard_map(shards, mesh=mesh, in_specs=in_specs, out_specs=out_specs, check_vma=False)
```

profile of v0, /device:TPU:0, one launch (start us, length us, event | category | flops | bytes accessed | tf_op | source)
XLA Modules:
  0.0 223.6 jit_solution(11353303705725707446)
XLA Ops:
  6.5 2.1 fusion.66
  8.6 2.1 fusion.67
  10.7 2.1 fusion.68
  13.4 1.6 fusion.69
  16.0 8.0 %scatter_custom_fusion = s32[320]{0:T(512)S(1)} fusion(s32[2048]{0:T(1024)S(1)} %bitcast.180, s32[2048]{0:T(1024)S(1)} %reshape.468, s32[]{:T(128)} %constant.102.clone.1), kind=kCustom, calls=%fused_computation.112 | custom fusion | bytes 1284 | tf_op jit(solution)/shard_map/scatter | solution.py:42
  26.0 26.8 %all_gather.6 = bf16[1024,192]{1,0:T(8,128)(2,1)} all-gather(bf16[64,192]{1,0:T(8,128)(2,1)} %param.13), channel_id=1, replica_groups=mesh['req'=16,'kv'=8] {'req'}, dimensions={0}, use_global_device_ids=true | all-gather | bytes 417792 | tf_op jit(solution)/shard_map/all_gather | solution.py:125
  52.8 1.8 gather_fusion
  54.7 14.0 %all-gather = bf16[8,192,64]{1,2,0:T(8,128)(2,1)S(1)} all-gather(bf16[1,192,64]{1,2,0:T(8,128)(2,1)S(1)} %select_bitcast_fusion), channel_id=1, replica_groups=mesh['req'=16,'kv'=8] {'kv'}, dimensions={0}, use_global_device_ids=true | all-gather | bytes 221184 | tf_op jit(solution)/shard_map/all_gather | solution.py:128
  69.6 1.2 reshape.494
  70.9 1.7 convolution_bitcast_fusion
  73.3 8.2 %scatter_custom_fusion.1 = s32[320]{0:T(512)S(1)} fusion(s32[2048]{0:T(1024)S(1)} %bitcast.181, s32[2048]{0:T(1024)S(1)} %reshape.476, s32[]{:T(128)} %constant.106.clone.1), kind=kCustom, calls=%fused_computation.109 | custom fusion | bytes 1284 | tf_op jit(solution)/shard_map/scatter | solution.py:44
  83.1 2.5 %gather_fusion.1 = bf16[320,3,64]{2,1,0:T(4,128)(2,1)} fusion(bf16[64,3,64]{2,1,0:T(4,128)(2,1)S(1)} %copy.107, s32[1024]{0:T(1024)S(1)} %pad_clamp_fusion), kind=kCustom, calls=%fused_computation.1 | custom fusion | bytes 247040 | tf_op jit(solution)/shard_map/jit(_take)/gather | solution.py:49
  85.5 39.8 %select_select_fusion = s32[320]{0:T(512)S(1)} fusion(s32[]{:T(128)} %bitcast.5, s32[]{:T(128)} %bitcast.6, s32[]{:T(128)} %bitcast.7, s32[]{:T(128)} %bitcast.8, s32[]{:T(128)} %bitcast.9, s32[]{:T(128)} %bitcast.10, s32[]{:T(128)} %bitcast.11, s32[]{:T(128)} %bitcast.12, s32[]{:T(128)} %bitcast.13, s32[]{:T(128)} %bitcast.14, s32[]{:T(128)} %bitcast.15, ...), kind=kLoop, calls=%fused_computation.96 | loop fusion | flops 42880 | bytes 2816 | tf_op jit(solution)/shard_map/jit(_take)/select_n | solution.py:47
  125.4 0.9 fusion.36
  126.3 5.7 %fusion.70 = (f32[320,3]{1,0:T(8,128)}, f32[320,3,128]{2,1,0:T(4,128)}) fusion(bf16[320,1,128,128]{3,2,0,1:T(8,128)(2,1)} %bitcast.182, bf16[320,3,64]{2,1,0:T(4,128)(2,1)} %gather_fusion.1, pred[320]{0:T(512)(128)(4,1)} %get-tuple-element.16, pred[320,128]{1,0:T(8,128)(4,1)S(1)} %fusion.36), kind=kOutput, calls=%fused_computation.124 | convolution fusion | flops 16157760 | bytes 6107392 | tf_op jit(solution)/shard_map/pkgd,pkdt->pkgt/dot_general | solution.py:51
  131.9 1.0 copy.109
  132.9 0.9 fusion.48
  134.2 1.6 gather_fusion.2
  135.8 1.0 broadcast_select_fusion
  136.9 1.9 fusion.19
  138.8 6.5 %fusion.2 = f32[320,3,64]{2,1,0:T(4,128)} fusion(bf16[320,1,128,128]{3,2,0,1:T(8,128)(2,1)} %bitcast.183, f32[320,3,128]{2,1,0:T(4,128)} %get-tuple-element.82, f32[320,3]{1,0:T(8,128)S(1)} %broadcast_select_fusion, pred[320,128]{1,0:T(8,128)(4,1)S(1)} %fusion.36), kind=kOutput, calls=%fused_computation.9 | convolution fusion | flops 16097280 | bytes 6188800 | tf_op jit(solution)/shard_map/pkgt,pkdt->pkgd/dot_general | solution.py:74
  145.5 2.1 copy.112
  147.5 2.0 fusion.15
  149.5 0.9 copy.113
  150.4 2.0 convolution_convert_fusion
  153.3 28.5 %reduce-scatter.2.cloned.1.call-done = bf16[8,1536]{1,0:T(8,128)(2,1)} async-done(((bf16[64,1536]{1,0:T(8,128)(2,1)}), bf16[8,1536]{1,0:T(8,128)(2,1)}) %reduce-scatter.2.cloned.1.call-update) | async-done | bytes 24592 | tf_op jit(solution)/shard_map/reduce_scatter | solution.py:134
  181.9 0.9 fusion.41
  184.7 6.8 %all-to-all-start = ((bf16[16,2,1,1536]{3,1,2,0:T(2,128)(2,1)}), bf16[16,2,1,1536]{3,1,2,0:T(2,128)(2,1)S(1)}, u32[]{:S(2)}, u32[]{:S(2)}) async-start(bf16[16,2,1,1536]{3,1,2,0:T(2,128)(2,1)} %bitcast.90), calls=%async_computation.1 | async-start | bytes 196608 | tf_op jit(solution)/shard_map/all_to_all | solution.py:170
  191.7 7.7 %all-to-all-done = bf16[16,2,1,1536]{3,1,2,0:T(2,128)(2,1)S(1)} async-done(((bf16[16,2,1,1536]{3,1,2,0:T(2,128)(2,1)}), bf16[16,2,1,1536]{3,1,2,0:T(2,128)(2,1)S(1)}, u32[]{:S(2)}, u32[]{:S(2)}) %all-to-all-start) | async-done | bytes 98336 | tf_op jit(solution)/shard_map/all_to_all | solution.py:170
  199.4 4.0 %fusion.6 = f32[1,32,2048]{2,1,0:T(8,128)S(1)} fusion(bf16[32,1536]{1,0:T(8,128)(2,1)S(1)} %reshape.352, bf16[1,1536,2048]{2,1,0:T(8,128)(2,1)} %param.24), kind=kOutput, calls=%fused_computation.15 | convolution fusion | flops 201326592 | bytes 6651904 | tf_op jit(solution)/shard_map/erd,edf->erf/dot_general | solution.py:97
  204.6 3.5 %all-to-all-start.1 = ((bf16[16,2,1,1536]{3,1,2,0:T(2,128)(2,1)}), bf16[16,2,1,1536]{3,1,2,0:T(2,128)(2,1)S(1)}, u32[]{:S(2)}, u32[]{:S(2)}) async-start(bf16[16,2,1,1536]{3,1,2,0:T(2,128)(2,1)} %bitcast.95), calls=%async_computation.2 | async-start | bytes 196608 | tf_op jit(solution)/shard_map/all_to_all | solution.py:171
  208.3 7.6 %all-to-all-done.1 = bf16[16,2,1,1536]{3,1,2,0:T(2,128)(2,1)S(1)} async-done(((bf16[16,2,1,1536]{3,1,2,0:T(2,128)(2,1)}), bf16[16,2,1,1536]{3,1,2,0:T(2,128)(2,1)S(1)}, u32[]{:S(2)}, u32[]{:S(2)}) %all-to-all-start.1) | async-done | bytes 98336 | tf_op jit(solution)/shard_map/all_to_all | solution.py:171
  (71 shorter events, 12.8 us)
Async XLA Ops:
  6.5 196.8 %copy-start = (bf16[1,1024,1536]{2,1,0:T(8,128)(2,1)S(1)}, bf16[1,1024,1536]{2,1,0:T(8,128)(2,1)}, u32[]{:S(2)}) copy-start(bf16[1,1024,1536]{2,1,0:T(8,128)(2,1)} %param.25) | copy-start | bytes 9437188
  6.5 175.3 %reduce-scatter.2.cloned.1.call-start = ((), (), s32[]{:S(2)}) async-start(), calls=%async_computation.3 | async-start | bytes 221184 | tf_op jit(solution)/shard_map/reduce_scatter | solution.py:134
  134.2 18.2 %copy-start.3 = (s32[8,2]{0,1:T(2,128)S(1)}, s32[8,2]{0,1:T(2,128)}, u32[]{:S(2)}) copy-start(s32[8,2]{0,1:T(2,128)} %param.23) | copy-start | bytes 196
  134.2 48.5 %copy-start.2 = (f32[1536]{0:T(1024)S(1)}, f32[1536]{0:T(1024)}, u32[]{:S(2)}) copy-start(f32[1536]{0:T(1024)} %param.21) | copy-start | bytes 18436
  134.2 48.6 %copy-start.1 = (bf16[1536,16]{0,1:T(8,128)(2,1)S(1)}, bf16[1536,16]{0,1:T(8,128)(2,1)}, u32[]{:S(2)}) copy-start(bf16[1536,16]{0,1:T(8,128)(2,1)} %param.22) | copy-start | bytes 147460
  184.7 14.6 %all-to-all-start = ((bf16[16,2,1,1536]{3,1,2,0:T(2,128)(2,1)}), bf16[16,2,1,1536]{3,1,2,0:T(2,128)(2,1)S(1)}, u32[]{:S(2)}, u32[]{:S(2)}) async-start(bf16[16,2,1,1536]{3,1,2,0:T(2,128)(2,1)} %bitcast.90), calls=%async_computation.1 | async-start | bytes 196608 | tf_op jit(solution)/shard_map/all_to_all | solution.py:170
  204.6 11.3 %all-to-all-start.1 = ((bf16[16,2,1,1536]{3,1,2,0:T(2,128)(2,1)}), bf16[16,2,1,1536]{3,1,2,0:T(2,128)(2,1)S(1)}, u32[]{:S(2)}, u32[]{:S(2)}) async-start(bf16[16,2,1,1536]{3,1,2,0:T(2,128)(2,1)} %bitcast.95), calls=%async_computation.2 | async-start | bytes 196608 | tf_op jit(solution)/shard_map/all_to_all | solution.py:171
Sparse Core Ops, SparseCore 0:
  152.5 29.2 reduce-scatter.1
where the time goes:
time: 225 us; the launch traced here: 224 us
  other arithmetic  51.4 us (23%)
  waiting for transfers between devices  43.9 us (20%)
  blocking collectives  40.8 us (18%)
  local copies, waits for them, and re-layouts  39.5 us (18%)
  matrix products  24.1 us (11%)
  between operations  13.6 us (6%)
  starting transfers between devices  10.3 us (5%)
    select_n x2, other arithmetic, attend(): jnp.take(seq_lens, owner_safe)[:, None]  40.4 us
    reduce_scatter x1, waiting for transfers between devices, shards(): lax.psum_scatter(jnp.dot(head_out, out_flat, preferred_element_type=jnp.f...  28.5 us
    all_gather x1, blocking collectives, shards(): every_row = lax.all_gather(hidden, 'req', axis=0, tiled=True)  26.8 us
    all_gather x1, blocking collectives, shards(): tokens = lax.all_gather(picked_rows, 'kv', axis=1, tiled=True)  14 us
    scatter x1, local copies, waits for them, and re-layouts, attend(): jnp.zeros((pool_pages,), jnp.int32).at[target_page]  8.21 us
    scatter x1, local copies, waits for them, and re-layouts, attend(): jnp.full((pool_pages,), slot_count, jnp.int32).at[target_page]  8.03 us
    gather x4, local copies, waits for them, and re-layouts, attend(): jnp.take(seq_lens, owner_safe)[:, None]  7.79 us
    all_to_all x1, waiting for transfers between devices, shards(): lax.all_to_all(outgoing, 'req', split_axis=0, concat_axis=0, tiled=True)  7.69 us
  transfers between devices with their start and end apart: 3, of which 3 were waited for; matrix products, arithmetic and copies ran while one was open for 1% of the time, Pallas kernels for 0%

commit v1 on v0

--- a/solution.py
+++ b/solution.py
@@ -33,20 +33,19 @@
     page_need = (seq_lens + page_len - 1) // page_len
     page_ids = jnp.arange(max_pages, dtype=jnp.int32)
     in_use = page_ids[None, :] < page_need[:, None]
-    target_page = jnp.where(in_use, page_table, pool_pages).reshape(-1)
-    slot_ids = jnp.broadcast_to(
-        jnp.arange(slot_count, dtype=jnp.int32)[:, None], (slot_count, max_pages)
-    ).reshape(-1)
-    order_ids = jnp.broadcast_to(page_ids[None, :], (slot_count, max_pages)).reshape(-1)
-    owner = (
-        jnp.full((pool_pages,), slot_count, jnp.int32).at[target_page].set(slot_ids, mode="drop")
-    )
-    page_order = jnp.zeros((pool_pages,), jnp.int32).at[target_page].set(order_ids, mode="drop")
-    owner_safe = jnp.minimum(owner, slot_count - 1)
+    pool_ids = jnp.arange(pool_pages, dtype=jnp.int32)
+    match = (page_table[:, :, None] == pool_ids[None, None, :]) & in_use[:, :, None]
+    belongs = jnp.any(match, axis=1)
+    page_order = jnp.sum(jnp.where(match, page_ids[None, :, None], 0), axis=(0, 1))
+    owner_len = jnp.sum(jnp.where(belongs, seq_lens[:, None], 0), axis=0)
     position = page_order[:, None] * page_len + jnp.arange(page_len, dtype=jnp.int32)[None, :]
-    live = (owner[:, None] < slot_count) & (position < jnp.take(seq_lens, owner_safe)[:, None])
+    live = position < owner_len[:, None]
     scale_factor = head_dim ** (-0.5)
-    page_queries = jnp.take(queries, owner_safe, axis=0)
+    page_queries = jnp.dot(
+        belongs.T.astype(jnp.bfloat16),
+        queries.reshape(slot_count, -1),
+        preferred_element_type=jnp.float32,
+    ).astype(jnp.bfloat16).reshape(pool_pages, local_heads, groups, head_dim)
     scores = (
         jnp.einsum(
             "pkgd,pkdt->pkgt",
@@ -62,12 +61,14 @@
         * scale_factor
     )
     page_peak = jnp.max(scores, axis=3)
-    belongs = owner[None, :] == jnp.arange(slot_count, dtype=jnp.int32)[:, None]
     slot_peak = jnp.max(jnp.where(belongs[:, :, None, None], page_peak[None], NEG_FILL), axis=1)
     slot_peak = jnp.maximum(slot_peak, score_new)
+    page_peak_of_owner = jnp.max(
+        jnp.where(belongs[:, :, None, None], slot_peak[:, None], NEG_FILL), axis=0
+    )
     weights = jnp.where(
         live[:, None, None, :],
-        jnp.exp(scores - jnp.take(slot_peak, owner_safe, axis=0)[..., None]),
+        jnp.exp(scores - page_peak_of_owner[..., None]),
         0.0,
     )
     page_total = jnp.sum(weights, axis=3)
@@ -124,7 +125,12 @@
     kv_index = lax.axis_index("kv")
     every_row = lax.all_gather(hidden, "req", axis=0, tiled=True)
     my_perm = lax.dynamic_slice_in_dim(perm, req_index * REQ_DEV, REQ_DEV)
-    picked_rows = jnp.take(every_row, my_perm, axis=0)
+    pick = (
+        my_perm[:, None] == jnp.arange(every_row.shape[0], dtype=jnp.int32)[None, :]
+    ).astype(every_row.dtype)
+    picked_rows = jnp.dot(pick, every_row, preferred_element_type=jnp.float32).astype(
+        every_row.dtype
+    )
     tokens = lax.all_gather(picked_rows, "kv", axis=1, tiled=True)
     normed = rms_norm(tokens, attn_gain)
     head_out = attend(normed, seq_lens, page_table, kv_cache, qkv_weight)

time: 225 us -> 154 us (0.68)
  other arithmetic: 51.4 us -> 8.5 us
  local copies, waits for them, and re-layouts: 39.5 us -> 11.7 us
    select_n x5 -> x0, other arithmetic: 42.2 us -> none  [the longest x2 40.4 us: attend(): jnp.take(seq_lens, owner_safe)[:, None]]
    scatter x2 -> x0, local copies, waits for them, and re-layouts: 16.2 us -> none  [the longest x1 8.21 us: attend(): jnp.zeros((pool_pages,), jnp.int32).at[target_page]]
    gather x7 -> x0, local copies, waits for them, and re-layouts: 13.6 us -> none  [the longest x4 7.79 us: attend(): jnp.take(seq_lens, owner_safe)[:, None]]
where the time goes in v1:
time: 154 us; the launch traced here: 153 us
  waiting for transfers between devices  43.2 us (28%)
  blocking collectives  40.8 us (26%)
  matrix products  24.8 us (16%)
  between operations  13.6 us (9%)
  local copies, waits for them, and re-layouts  11.7 us (8%)
  starting transfers between devices  10.3 us (7%)
  other arithmetic  8.5 us (6%)
    reduce_scatter x1, waiting for transfers between devices, shards(): lax.psum_scatter(jnp.dot(head_out, out_flat, preferred_element_type=jnp.f...  27.9 us
    all_gather x1, blocking collectives, shards(): every_row = lax.all_gather(hidden, 'req', axis=0, tiled=True)  26.8 us
    all_gather x1, blocking collectives, shards(): tokens = lax.all_gather(picked_rows, 'kv', axis=1, tiled=True)  14 us
    all_to_all x1, waiting for transfers between devices, shards(): lax.all_to_all(outgoing, 'req', split_axis=0, concat_axis=0, tiled=True)  7.69 us
    all_to_all x1, waiting for transfers between devices, shards(): lax.all_to_all(expert_apply(arrived, gate_up, down), 'req', split_axis=0,...  7.62 us
    all_to_all x1, starting transfers between devices, shards(): lax.all_to_all(outgoing, 'req', split_axis=0, concat_axis=0, tiled=True)  6.8 us
    dot_general x1, matrix products, attend(): jnp.einsum('pkgt,pkdt->pkgd', weights.astype(jnp.bfloat16), kv_cache[:, :...  6.5 us
    dot_general x1, matrix products, attend(): jnp.einsum('pkgd,pkdt->pkgt', page_queries, kv_cache[:, :, :head_dim, :],...  5.63 us
  transfers between devices with their start and end apart: 3, of which 3 were waited for; matrix products, arithmetic and copies ran while one was open for 1% of the time, Pallas kernels for 0%

profile of v1, /device:TPU:0, one launch (start us, length us, event | category | flops | bytes accessed | tf_op | source)
XLA Modules:
  0.0 153.1 jit_solution(15035684609703527632)
XLA Ops:
  6.5 0.9 copy.88
  7.5 0.7 and_select_fusion
  8.2 0.9 fusion.7
  9.1 0.8 select_reduce_fusion
  10.0 26.8 %all_gather.6 = bf16[1024,192]{1,0:T(8,128)(2,1)} all-gather(bf16[64,192]{1,0:T(8,128)(2,1)} %param.13), channel_id=1, replica_groups=mesh['req'=16,'kv'=8] {'req'}, dimensions={0}, use_global_device_ids=true | all-gather | bytes 417792 | tf_op jit(solution)/shard_map/all_gather | solution.py:126
  36.8 0.8 dynamic_slice.6
  37.6 1.3 fusion.19
  38.9 14.0 %all-gather = bf16[8,192,64]{1,2,0:T(8,128)(2,1)S(1)} all-gather(bf16[1,192,64]{1,2,0:T(8,128)(2,1)S(1)} %fusion.19), channel_id=1, replica_groups=mesh['req'=16,'kv'=8] {'kv'}, dimensions={0}, use_global_device_ids=true | all-gather | bytes 221184 | tf_op jit(solution)/shard_map/all_gather | solution.py:134
  52.9 0.8 copy.87
  53.7 1.2 reshape.301
  55.1 0.8 select_reduce_fusion.3
  55.8 1.6 %convolution_bitcast_fusion = bf16[64,1,320]{2,0,1:T(8,128)(2,1)S(1)} fusion(bf16[1,1536,320]{1,2,0:T(8,128)(2,1)} %param.19, bf16[1536,64]{0,1:T(8,128)(2,1)S(1)} %reshape.301, f32[1536]{0:T(1024)} %param.18, f32[64]{0:T(128)S(1)} %add_rsqrt_fusion.1), kind=kOutput, calls=%fused_computation.20 | convolution fusion | flops 63307776 | bytes 1227008 | tf_op jit(solution)/shard_map/sd,hdc->shc/dot_general | solution.py:25
  57.7 0.7 fusion.47
  58.4 0.9 copy.90
  59.5 5.6 %fusion.57 = (f32[320,3]{1,0:T(8,128)}, f32[320,3,128]{2,1,0:T(4,128)}) fusion(bf16[320,3,64]{2,1,0:T(4,128)(2,1)} %copy.90, bf16[320,1,128,128]{3,2,0,1:T(8,128)(2,1)} %bitcast.113, pred[320,128]{1,0:T(8,128)(4,1)S(1)} %add_compare_fusion), kind=kOutput, calls=%fused_computation.102 | convolution fusion | flops 16096320 | bytes 6106880 | tf_op jit(solution)/shard_map/pkgd,pkdt->pkgt/dot_general | solution.py:50
  65.2 1.0 copy.91
  66.9 1.9 %fusion.22 = f32[320,3]{1,0:T(8,128)S(1)} fusion(f32[320,3,128]{2,1,0:T(4,128)} %get-tuple-element.14, f32[320,3]{1,0:T(8,128)S(1)} %copy.93, pred[320,128]{1,0:T(8,128)(4,1)} %copy-done.2), kind=kLoop, calls=%fused_computation.34 | loop fusion | flops 367680 | bytes 540160 | tf_op jit(solution)/shard_map/reduce_sum | solution.py:74
  68.8 6.5 %fusion.2 = f32[320,3,64]{2,1,0:T(4,128)} fusion(bf16[320,1,128,128]{3,2,0,1:T(8,128)(2,1)} %bitcast.114, f32[320,3,128]{2,1,0:T(4,128)} %get-tuple-element.14, f32[320,3]{1,0:T(8,128)S(1)} %copy.93, pred[320,128]{1,0:T(8,128)(4,1)} %copy-done.2), kind=kOutput, calls=%fused_computation.4 | convolution fusion | flops 16097280 | bytes 6188800 | tf_op jit(solution)/shard_map/pkgt,pkdt->pkgd/dot_general | solution.py:75
  75.5 2.1 %copy.95 = f32[320,3,64]{0,2,1:T(8,128)} copy(f32[320,3,64]{2,1,0:T(4,128)} %fusion.2) | data formatting | bytes 491520 | tf_op jit(solution)/shard_map/pkgt,pkdt->pkgd/dot_general | solution.py:75
  77.6 1.3 fusion.17
  79.0 2.0 %convolution_convert_fusion = bf16[64,1536]{1,0:T(8,128)(2,1)} fusion(bf16[64,192]{0,1:T(8,128)(2,1)S(1)} %bitcast.111, bf16[1,192,1536]{2,1,0:T(8,128)(2,1)} %param.20), kind=kOutput, calls=%fused_computation.13 | convolution fusion | flops 37847040 | bytes 811008 | tf_op jit(solution)/shard_map/dot_general | solution.py:141
  81.0 0.8 copy.97
  82.6 27.9 %reduce-scatter.2.cloned.1.call-done = bf16[8,1536]{1,0:T(8,128)(2,1)} async-done(((bf16[64,1536]{1,0:T(8,128)(2,1)}), bf16[8,1536]{1,0:T(8,128)(2,1)}) %reduce-scatter.2.cloned.1.call-update) | async-done | bytes 24592 | tf_op jit(solution)/shard_map/reduce_scatter | solution.py:140
  110.5 0.9 fusion.41
  111.5 0.9 fusion.59
  113.5 0.7 reshape.281
  114.1 6.8 %all-to-all-start = ((bf16[16,2,1,1536]{3,1,2,0:T(2,128)(2,1)}), bf16[16,2,1,1536]{3,1,2,0:T(2,128)(2,1)S(1)}, u32[]{:S(2)}, u32[]{:S(2)}) async-start(bf16[16,2,1,1536]{3,1,2,0:T(2,128)(2,1)} %bitcast.28), calls=%async_computation.1 | async-start | bytes 196608 | tf_op jit(solution)/shard_map/all_to_all | solution.py:176
  121.1 7.7 %all-to-all-done = bf16[16,2,1,1536]{3,1,2,0:T(2,128)(2,1)S(1)} async-done(((bf16[16,2,1,1536]{3,1,2,0:T(2,128)(2,1)}), bf16[16,2,1,1536]{3,1,2,0:T(2,128)(2,1)S(1)}, u32[]{:S(2)}, u32[]{:S(2)}) %all-to-all-start) | async-done | bytes 98336 | tf_op jit(solution)/shard_map/all_to_all | solution.py:176
  128.8 4.0 %fusion.8 = f32[1,32,2048]{2,1,0:T(8,128)S(1)} fusion(bf16[32,1536]{1,0:T(8,128)(2,1)S(1)} %reshape.282, bf16[1,1536,2048]{2,1,0:T(8,128)(2,1)} %param.24), kind=kOutput, calls=%fused_computation.14 | convolution fusion | flops 201326592 | bytes 6651904 | tf_op jit(solution)/shard_map/erd,edf->erf/dot_general | solution.py:98
  133.4 0.7 transpose_reshape.3
  134.1 3.5 %all-to-all-start.1 = ((bf16[16,2,1,1536]{3,1,2,0:T(2,128)(2,1)}), bf16[16,2,1,1536]{3,1,2,0:T(2,128)(2,1)S(1)}, u32[]{:S(2)}, u32[]{:S(2)}) async-start(bf16[16,2,1,1536]{3,1,2,0:T(2,128)(2,1)} %bitcast.33), calls=%async_computation.2 | async-start | bytes 196608 | tf_op jit(solution)/shard_map/all_to_all | solution.py:177
  137.7 7.6 %all-to-all-done.1 = bf16[16,2,1,1536]{3,1,2,0:T(2,128)(2,1)S(1)} async-done(((bf16[16,2,1,1536]{3,1,2,0:T(2,128)(2,1)}), bf16[16,2,1,1536]{3,1,2,0:T(2,128)(2,1)S(1)}, u32[]{:S(2)}, u32[]{:S(2)}) %all-to-all-start.1) | async-done | bytes 98336 | tf_op jit(solution)/shard_map/all_to_all | solution.py:177
  (57 shorter events, 5.4 us)
Async XLA Ops:
  6.5 126.2 %copy-start = (bf16[1,1024,1536]{2,1,0:T(8,128)(2,1)S(1)}, bf16[1,1024,1536]{2,1,0:T(8,128)(2,1)}, u32[]{:S(2)}) copy-start(bf16[1,1024,1536]{2,1,0:T(8,128)(2,1)} %param.25) | copy-start | bytes 9437188
  6.5 104.0 %reduce-scatter.2.cloned.1.call-start = ((), (), s32[]{:S(2)}) async-start(), calls=%async_computation.3 | async-start | bytes 221184 | tf_op jit(solution)/shard_map/reduce_scatter | solution.py:140
  57.5 0.9 copy-start.1
  58.4 8.0 %slice-start = ((bf16[64,1,320]{2,0,1:T(8,128)(2,1)}), bf16[64,1,192]{2,0,1:T(8,128)(2,1)S(1)}, s32[]{:S(2)}) async-start(bf16[64,1,320]{2,0,1:T(8,128)(2,1)} %copy-done.1), calls=%async_computation.4 | async-start | bytes 65536 | tf_op jit(solution)/shard_map/slice | solution.py:27
  59.4 7.0 %copy-start.3 = (f32[64,64]{1,0:T(8,128)S(1)}, f32[64,64]{1,0:T(8,128)}, u32[]{:S(2)}) copy-start(f32[64,64]{1,0:T(8,128)} %get-tuple-element.8) | copy-start | bytes 49156
  59.5 6.8 %copy-start.2 = (pred[320,128]{1,0:T(8,128)(4,1)}, pred[320,128]{1,0:T(8,128)(4,1)S(1)}, u32[]{:S(2)}) copy-start(pred[320,128]{1,0:T(8,128)(4,1)S(1)} %add_compare_fusion) | copy-start | bytes 122884
  68.7 42.6 %copy-start.4 = (f32[1536]{0:T(1024)S(1)}, f32[1536]{0:T(1024)}, u32[]{:S(2)}) copy-start(f32[1536]{0:T(1024)} %param.21) | copy-start | bytes 18436
  114.1 14.6 %all-to-all-start = ((bf16[16,2,1,1536]{3,1,2,0:T(2,128)(2,1)}), bf16[16,2,1,1536]{3,1,2,0:T(2,128)(2,1)S(1)}, u32[]{:S(2)}, u32[]{:S(2)}) async-start(bf16[16,2,1,1536]{3,1,2,0:T(2,128)(2,1)} %bitcast.28), calls=%async_computation.1 | async-start | bytes 196608 | tf_op jit(solution)/shard_map/all_to_all | solution.py:176
  134.1 11.3 %all-to-all-start.1 = ((bf16[16,2,1,1536]{3,1,2,0:T(2,128)(2,1)}), bf16[16,2,1,1536]{3,1,2,0:T(2,128)(2,1)S(1)}, u32[]{:S(2)}, u32[]{:S(2)}) async-start(bf16[16,2,1,1536]{3,1,2,0:T(2,128)(2,1)} %bitcast.33), calls=%async_computation.2 | async-start | bytes 196608 | tf_op jit(solution)/shard_map/all_to_all | solution.py:177
Sparse Core Ops, SparseCore 0:
  81.1 29.3 reduce-scatter.1

commit v2 on v1

--- a/solution.py
+++ b/solution.py
@@ -137,12 +137,12 @@
     sub_rows = routes.shape[0]
     width = tokens.shape[1]
     out_flat = out_weight.reshape(-1, out_weight.shape[2])
-    attn_rows = lax.psum_scatter(
-        jnp.dot(head_out, out_flat, preferred_element_type=jnp.float32).astype(jnp.bfloat16),
-        "kv",
-        scatter_dimension=0,
-        tiled=True,
-    ).astype(jnp.float32)
+    n_kv = lax.axis_size("kv")
+    partial = jnp.dot(head_out, out_flat, preferred_element_type=jnp.float32).astype(jnp.bfloat16)
+    partial_parts = lax.all_to_all(
+        partial.reshape(n_kv, sub_rows, partial.shape[1]), "kv", split_axis=0, concat_axis=0, tiled=True
+    )
+    attn_rows = jnp.sum(partial_parts.astype(jnp.float32), axis=0)
     own_tokens = lax.dynamic_slice_in_dim(tokens, kv_index * sub_rows, sub_rows, 0)
     residual = (own_tokens.astype(jnp.float32) + attn_rows).astype(jnp.bfloat16)
     normed_ffn = rms_norm(residual, ffn_gain)

time: 154 us -> 120 us (0.78)
  waiting for transfers between devices: 43.2 us -> 17.4 us
  between operations: 13.6 us -> 0.21 us
  other arithmetic: 8.5 us -> 11 us
  starting transfers between devices: 10.3 us -> 12.1 us
    reduce_scatter x1 -> x0, waiting for transfers between devices: 27.9 us -> none  [shards(): lax.psum_scatter(jnp.dot(head_out, out_flat, preferred_element_type=jnp.f...]
    all_to_all x0 -> x1, starting transfers between devices: none -> 4.11 us  [shards(): lax.all_to_all(partial.reshape(n_kv, sub_rows, partial.shape[1]), 'kv', s...]
    all_to_all x1, starting transfers between devices: 6.8 us -> 4.48 us  [shards(): lax.all_to_all(outgoing, 'req', split_axis=0, concat_axis=0, tiled=True)]
    all_to_all x0 -> x1, waiting for transfers between devices: none -> 2.12 us  [shards(): lax.all_to_all(partial.reshape(n_kv, sub_rows, partial.shape[1]), 'kv', s...]
  transfers between devices with their start and end apart: 3 -> 3, of which waited for: 3 -> 3; matrix products, arithmetic and copies ran while one was open for 1% -> 4% of each run, Pallas kernels for 0% -> 0%
where the time goes in v2:
time: 120 us; the launch traced here: 119 us
  blocking collectives  40.8 us (34%)
  matrix products  24.8 us (21%)
  waiting for transfers between devices  17.4 us (14%)
  local copies, waits for them, and re-layouts  12.4 us (10%)
  starting transfers between devices  12.1 us (10%)
  other arithmetic  11 us (9%)
    all_gather x1, blocking collectives, shards(): every_row = lax.all_gather(hidden, 'req', axis=0, tiled=True)  26.8 us
    all_gather x1, blocking collectives, shards(): tokens = lax.all_gather(picked_rows, 'kv', axis=1, tiled=True)  14 us
    all_to_all x1, waiting for transfers between devices, shards(): lax.all_to_all(outgoing, 'req', split_axis=0, concat_axis=0, tiled=True)  7.69 us
    all_to_all x1, waiting for transfers between devices, shards(): lax.all_to_all(expert_apply(arrived, gate_up, down), 'req', split_axis=0,...  7.62 us
    dot_general x1, matrix products, attend(): jnp.einsum('pkgt,pkdt->pkgd', weights.astype(jnp.bfloat16), kv_cache[:, :...  6.5 us
    dot_general x1, matrix products, attend(): jnp.einsum('pkgd,pkdt->pkgt', page_queries, kv_cache[:, :, :head_dim, :],...  5.63 us
    all_to_all x1, starting transfers between devices, shards(): lax.all_to_all(outgoing, 'req', split_axis=0, concat_axis=0, tiled=True)  4.48 us
    all_to_all x1, starting transfers between devices, shards(): lax.all_to_all(partial.reshape(n_kv, sub_rows, partial.shape[1]), 'kv', s...  4.11 us
  transfers between devices with their start and end apart: 3, of which 3 were waited for; matrix products, arithmetic and copies ran while one was open for 4% of the time, Pallas kernels for 0%

profile of v2, /device:TPU:0, one launch (start us, length us, event | category | flops | bytes accessed | tf_op | source)
XLA Modules:
  0.0 118.8 jit_solution(6768713367886617896)
XLA Ops:
  0.0 0.9 copy.88
  1.7 0.9 fusion.7
  2.6 0.8 select_reduce_fusion
  3.5 26.8 %all_gather.6 = bf16[1024,192]{1,0:T(8,128)(2,1)} all-gather(bf16[64,192]{1,0:T(8,128)(2,1)} %param.13), channel_id=1, replica_groups=mesh['req'=16,'kv'=8] {'req'}, dimensions={0}, use_global_device_ids=true | all-gather | bytes 417792 | tf_op jit(solution)/shard_map/all_gather | solution.py:126
  30.3 0.8 dynamic_slice.6
  31.0 1.3 %fusion.20 = bf16[1,192,64]{1,2,0:T(8,128)(2,1)S(1)} fusion(bf16[1024,192]{1,0:T(8,128)(2,1)} %all_gather.6, s32[64]{0:T(128)S(1)} %dynamic_slice.6), kind=kOutput, calls=%fused_computation.28 | convolution fusion | flops 25243648 | bytes 418048 | tf_op jit(solution)/shard_map/dot_general | solution.py:131
  32.3 14.0 %all-gather = bf16[8,192,64]{1,2,0:T(8,128)(2,1)S(1)} all-gather(bf16[1,192,64]{1,2,0:T(8,128)(2,1)S(1)} %fusion.20), channel_id=1, replica_groups=mesh['req'=16,'kv'=8] {'kv'}, dimensions={0}, use_global_device_ids=true | all-gather | bytes 221184 | tf_op jit(solution)/shard_map/all_gather | solution.py:134
  46.4 0.8 copy.87
  47.2 1.2 reshape.305
  48.5 0.8 select_reduce_fusion.3
  49.3 1.6 %convolution_bitcast_fusion = bf16[64,1,320]{2,0,1:T(8,128)(2,1)S(1)} fusion(bf16[1,1536,320]{1,2,0:T(8,128)(2,1)} %param.19, bf16[1536,64]{0,1:T(8,128)(2,1)S(1)} %reshape.305, f32[1536]{0:T(1024)} %param.18, f32[64]{0:T(128)S(1)} %add_rsqrt_fusion.1), kind=kOutput, calls=%fused_computation.21 | convolution fusion | flops 63307776 | bytes 1227008 | tf_op jit(solution)/shard_map/sd,hdc->shc/dot_general | solution.py:25
  51.9 0.9 copy.90
  53.0 5.6 %fusion.58 = (f32[320,3]{1,0:T(8,128)}, f32[320,3,128]{2,1,0:T(4,128)}) fusion(bf16[320,3,64]{2,1,0:T(4,128)(2,1)} %copy.90, bf16[320,1,128,128]{3,2,0,1:T(8,128)(2,1)} %bitcast.115, pred[320,128]{1,0:T(8,128)(4,1)S(1)} %add_compare_fusion), kind=kOutput, calls=%fused_computation.104 | convolution fusion | flops 16096320 | bytes 6106880 | tf_op jit(solution)/shard_map/pkgd,pkdt->pkgt/dot_general | solution.py:50
  58.6 1.0 copy.91
  60.3 1.9 %fusion.23 = f32[320,3]{1,0:T(8,128)S(1)} fusion(f32[320,3,128]{2,1,0:T(4,128)} %get-tuple-element.14, f32[320,3]{1,0:T(8,128)S(1)} %copy.93, pred[320,128]{1,0:T(8,128)(4,1)} %copy-done.2), kind=kLoop, calls=%fused_computation.35 | loop fusion | flops 367680 | bytes 540160 | tf_op jit(solution)/shard_map/reduce_sum | solution.py:74
  62.2 6.5 %fusion.2 = f32[320,3,64]{2,1,0:T(4,128)} fusion(bf16[320,1,128,128]{3,2,0,1:T(8,128)(2,1)} %bitcast.116, f32[320,3,128]{2,1,0:T(4,128)} %get-tuple-element.14, f32[320,3]{1,0:T(8,128)S(1)} %copy.93, pred[320,128]{1,0:T(8,128)(4,1)} %copy-done.2), kind=kOutput, calls=%fused_computation.4 | convolution fusion | flops 16097280 | bytes 6188800 | tf_op jit(solution)/shard_map/pkgt,pkdt->pkgd/dot_general | solution.py:75
  68.9 2.1 %copy.95 = f32[320,3,64]{0,2,1:T(8,128)} copy(f32[320,3,64]{2,1,0:T(4,128)} %fusion.2) | data formatting | bytes 491520 | tf_op jit(solution)/shard_map/pkgt,pkdt->pkgd/dot_general | solution.py:75
  71.0 1.3 %fusion.18 = bf16[64,3,64]{2,0,1:T(8,128)(2,1)S(1)} fusion(f32[320,3,64]{0,2,1:T(8,128)} %copy.95, pred[64,320]{1,0:T(8,128)(4,1)S(1)} %fusion.7, f32[64,3]{0,1:T(4,128)S(1)} %convolution_add_fusion.1, f32[64,64]{1,0:T(8,128)} %get-tuple-element.7, f32[64,3]{0,1:T(4,128)S(1)} %bitcast_convert_fusion), kind=kOutput, calls=%fused_computation.25 | convolution fusion | flops 47235072 | bytes 308736 | tf_op jit(solution)/shard_map/dot_general | solution.py:85
  72.5 2.0 %fusion.8 = bf16[8,8,1536]{2,1,0:T(8,128)(2,1)} fusion(bf16[64,192]{0,1:T(8,128)(2,1)S(1)} %bitcast.113, bf16[1,192,1536]{2,1,0:T(8,128)(2,1)} %param.20), kind=kOutput, calls=%fused_computation.14 | convolution fusion | flops 37847040 | bytes 811008 | tf_op jit(solution)/shard_map/dot_general | solution.py:141
  74.4 4.1 %all-to-all-start = ((bf16[8,8,1536]{2,1,0:T(8,128)(2,1)}), bf16[8,8,1536]{2,1,0:T(8,128)(2,1)S(1)}, u32[]{:S(2)}, u32[]{:S(2)}) async-start(bf16[8,8,1536]{2,1,0:T(8,128)(2,1)} %fusion.8), calls=%async_computation | async-start | bytes 393216 | tf_op jit(solution)/shard_map/all_to_all | solution.py:142
  78.6 0.8 copy.97
  80.1 0.7 reduce_window_sum.11
  80.8 0.7 select_reduce_fusion.4
  81.5 0.7 reduce_sum.91
  83.3 2.1 %all-to-all-done = bf16[8,8,1536]{2,1,0:T(8,128)(2,1)S(1)} async-done(((bf16[8,8,1536]{2,1,0:T(8,128)(2,1)}), bf16[8,8,1536]{2,1,0:T(8,128)(2,1)S(1)}, u32[]{:S(2)}, u32[]{:S(2)}) %all-to-all-start) | async-done | bytes 196640 | tf_op jit(solution)/shard_map/all_to_all | solution.py:142
  85.6 0.8 fusion.44
  86.4 0.9 fusion.60
  89.0 4.5 %all-to-all-start.1 = ((bf16[16,2,1,1536]{3,1,2,0:T(2,128)(2,1)}), bf16[16,2,1,1536]{3,1,2,0:T(2,128)(2,1)S(1)}, u32[]{:S(2)}, u32[]{:S(2)}) async-start(bf16[16,2,1,1536]{3,1,2,0:T(2,128)(2,1)} %bitcast.29), calls=%async_computation.1 | async-start | bytes 196608 | tf_op jit(solution)/shard_map/all_to_all | solution.py:176
  93.6 7.7 %all-to-all-done.1 = bf16[16,2,1,1536]{3,1,2,0:T(2,128)(2,1)S(1)} async-done(((bf16[16,2,1,1536]{3,1,2,0:T(2,128)(2,1)}), bf16[16,2,1,1536]{3,1,2,0:T(2,128)(2,1)S(1)}, u32[]{:S(2)}, u32[]{:S(2)}) %all-to-all-start.1) | async-done | bytes 98336 | tf_op jit(solution)/shard_map/all_to_all | solution.py:176
  101.4 4.0 %fusion.9 = f32[1,32,2048]{2,1,0:T(8,128)S(1)} fusion(bf16[32,1536]{1,0:T(8,128)(2,1)S(1)} %reshape.286, bf16[1,1536,2048]{2,1,0:T(8,128)(2,1)} %param.24), kind=kOutput, calls=%fused_computation.15 | convolution fusion | flops 201326592 | bytes 6651904 | tf_op jit(solution)/shard_map/erd,edf->erf/dot_general | solution.py:98
  106.6 3.5 %all-to-all-start.2 = ((bf16[16,2,1,1536]{3,1,2,0:T(2,128)(2,1)}), bf16[16,2,1,1536]{3,1,2,0:T(2,128)(2,1)S(1)}, u32[]{:S(2)}, u32[]{:S(2)}) async-start(bf16[16,2,1,1536]{3,1,2,0:T(2,128)(2,1)} %bitcast.34), calls=%async_computation.2 | async-start | bytes 196608 | tf_op jit(solution)/shard_map/all_to_all | solution.py:177
  110.3 7.6 %all-to-all-done.2 = bf16[16,2,1,1536]{3,1,2,0:T(2,128)(2,1)S(1)} async-done(((bf16[16,2,1,1536]{3,1,2,0:T(2,128)(2,1)}), bf16[16,2,1,1536]{3,1,2,0:T(2,128)(2,1)S(1)}, u32[]{:S(2)}, u32[]{:S(2)}) %all-to-all-start.2) | async-done | bytes 98336 | tf_op jit(solution)/shard_map/all_to_all | solution.py:177
  (57 shorter events, 9.2 us)
Async XLA Ops:
  0.0 105.3 %copy-start = (bf16[1,1024,1536]{2,1,0:T(8,128)(2,1)S(1)}, bf16[1,1024,1536]{2,1,0:T(8,128)(2,1)}, u32[]{:S(2)}) copy-start(bf16[1,1024,1536]{2,1,0:T(8,128)(2,1)} %param.25) | copy-start | bytes 9437188
  51.0 0.9 copy-start.1
  51.9 8.0 %slice-start = ((bf16[64,1,320]{2,0,1:T(8,128)(2,1)}), bf16[64,1,192]{2,0,1:T(8,128)(2,1)S(1)}, s32[]{:S(2)}) async-start(bf16[64,1,320]{2,0,1:T(8,128)(2,1)} %copy-done.1), calls=%async_computation.3 | async-start | bytes 65536 | tf_op jit(solution)/shard_map/slice | solution.py:27
  52.8 7.0 %copy-start.3 = (f32[64,64]{1,0:T(8,128)S(1)}, f32[64,64]{1,0:T(8,128)}, u32[]{:S(2)}) copy-start(f32[64,64]{1,0:T(8,128)} %get-tuple-element.8) | copy-start | bytes 49156
  53.0 6.8 %copy-start.2 = (pred[320,128]{1,0:T(8,128)(4,1)}, pred[320,128]{1,0:T(8,128)(4,1)S(1)}, u32[]{:S(2)}) copy-start(pred[320,128]{1,0:T(8,128)(4,1)S(1)} %add_compare_fusion) | copy-start | bytes 122884
  74.4 10.9 %all-to-all-start = ((bf16[8,8,1536]{2,1,0:T(8,128)(2,1)}), bf16[8,8,1536]{2,1,0:T(8,128)(2,1)S(1)}, u32[]{:S(2)}, u32[]{:S(2)}) async-start(bf16[8,8,1536]{2,1,0:T(8,128)(2,1)} %fusion.8), calls=%async_computation | async-start | bytes 393216 | tf_op jit(solution)/shard_map/all_to_all | solution.py:142
  79.4 2.1 %copy-start.4 = (s32[16]{0:T(128)}, s32[16]{0:T(128)S(1)}, u32[]{:S(2)}) copy-start(s32[16]{0:T(128)S(1)} %eq.84) | copy-start | bytes 196
  89.0 12.3 %all-to-all-start.1 = ((bf16[16,2,1,1536]{3,1,2,0:T(2,128)(2,1)}), bf16[16,2,1,1536]{3,1,2,0:T(2,128)(2,1)S(1)}, u32[]{:S(2)}, u32[]{:S(2)}) async-start(bf16[16,2,1,1536]{3,1,2,0:T(2,128)(2,1)} %bitcast.29), calls=%async_computation.1 | async-start | bytes 196608 | tf_op jit(solution)/shard_map/all_to_all | solution.py:176
  106.6 11.3 %all-to-all-start.2 = ((bf16[16,2,1,1536]{3,1,2,0:T(2,128)(2,1)}), bf16[16,2,1,1536]{3,1,2,0:T(2,128)(2,1)S(1)}, u32[]{:S(2)}, u32[]{:S(2)}) async-start(bf16[16,2,1,1536]{3,1,2,0:T(2,128)(2,1)} %bitcast.34), calls=%async_computation.2 | async-start | bytes 196608 | tf_op jit(solution)/shard_map/all_to_all | solution.py:177

commit v3 on v2

--- a/solution.py
+++ b/solution.py
@@ -123,21 +123,41 @@
 ):
     req_index = lax.axis_index("req")
     kv_index = lax.axis_index("kv")
-    every_row = lax.all_gather(hidden, "req", axis=0, tiled=True)
-    my_perm = lax.dynamic_slice_in_dim(perm, req_index * REQ_DEV, REQ_DEV)
-    pick = (
-        my_perm[:, None] == jnp.arange(every_row.shape[0], dtype=jnp.int32)[None, :]
-    ).astype(every_row.dtype)
-    picked_rows = jnp.dot(pick, every_row, preferred_element_type=jnp.float32).astype(
-        every_row.dtype
-    )
-    tokens = lax.all_gather(picked_rows, "kv", axis=1, tiled=True)
+    n_req = lax.axis_size("req")
+    n_kv = lax.axis_size("kv")
+    local_rows, col_width = hidden.shape
+    deal = local_rows // n_req
+    source_block = (perm // local_rows).reshape(n_req, local_rows)
+    source_row = (perm % local_rows).reshape(n_req, local_rows)
+    mine = source_block == req_index
+    rank_sent = jnp.cumsum(mine.astype(jnp.int32), axis=1) - 1
+    send_key = jnp.where(mine, rank_sent * local_rows + source_row, -1)
+    send_ids = jnp.arange(deal * local_rows, dtype=jnp.int32)
+    send_pick = jnp.any(send_key[:, :, None] == send_ids[None, None, :], axis=1)
+    send_pick = send_pick.reshape(n_req * deal, local_rows).astype(hidden.dtype)
+    outgoing_rows = jnp.dot(send_pick, hidden, preferred_element_type=jnp.float32).astype(
+        hidden.dtype
+    )
+    arrived_rows = lax.all_to_all(
+        outgoing_rows.reshape(n_req, deal, col_width), "req", split_axis=0, concat_axis=0, tiled=True
+    ).reshape(n_req * deal, col_width)
+    my_source = lax.dynamic_slice_in_dim(perm, req_index * local_rows, local_rows) // local_rows
+    slot_ids = jnp.arange(local_rows, dtype=jnp.int32)
+    same_before = (my_source[None, :] == my_source[:, None]) & (slot_ids[None, :] < slot_ids[:, None])
+    rank_got = jnp.sum(same_before.astype(jnp.int32), axis=1)
+    take_key = my_source * deal + rank_got
+    take_pick = (take_key[:, None] == slot_ids[None, :]).astype(hidden.dtype)
+    picked_rows = jnp.dot(take_pick, arrived_rows, preferred_element_type=jnp.float32).astype(
+        hidden.dtype
+    )
+    spread = jnp.broadcast_to(picked_rows[None], (n_kv, local_rows, col_width))
+    gathered = lax.all_to_all(spread, "kv", split_axis=0, concat_axis=0, tiled=True)
+    tokens = gathered.transpose(1, 0, 2).reshape(local_rows, n_kv * col_width)
     normed = rms_norm(tokens, attn_gain)
     head_out = attend(normed, seq_lens, page_table, kv_cache, qkv_weight)
     sub_rows = routes.shape[0]
     width = tokens.shape[1]
     out_flat = out_weight.reshape(-1, out_weight.shape[2])
-    n_kv = lax.axis_size("kv")
     partial = jnp.dot(head_out, out_flat, preferred_element_type=jnp.float32).astype(jnp.bfloat16)
     partial_parts = lax.all_to_all(
         partial.reshape(n_kv, sub_rows, partial.shape[1]), "kv", split_axis=0, concat_axis=0, tiled=True
@@ -151,7 +171,6 @@
     sigmoid_vals = jax.nn.sigmoid(chosen)
     gates = sigmoid_vals / jnp.sum(sigmoid_vals, axis=1, keepdims=True)
     experts_all = router.shape[1]
-    n_req = lax.axis_size("req")
     local_experts = gate_up.shape[0]
     capacity = max(2, 2 * sub_rows // experts_all + 1)
     flat_routes = routes.reshape(-1)

time: 120 us -> 115 us (0.958)
  blocking collectives: 40.8 us -> 0 us
  starting transfers between devices: 12.1 us -> 27.2 us
  waiting for transfers between devices: 17.4 us -> 26.8 us
  local copies, waits for them, and re-layouts: 12.4 us -> 20 us
  other arithmetic: 11 us -> 14.1 us
    all_gather x2 -> x0, blocking collectives: 40.8 us -> none  [the longest x1 26.8 us: shards(): every_row = lax.all_gather(hidden, 'req', axis=0, tiled=True)]
    all_to_all x0 -> x2, starting transfers between devices: none -> 12.4 us  [the longest x1 7.12 us: shards(): lax.all_to_all(outgoing_rows.reshape(n_req, deal, col_width), 'req', spli...]
    all_to_all x0 -> x2, waiting for transfers between devices: none -> 7.39 us  [the longest x1 7.38 us: shards(): lax.all_to_all(spread, 'kv', split_axis=0, concat_axis=0, tiled=True)]
    all_to_all x1, starting transfers between devices: 4.48 us -> 7.22 us  [shards(): lax.all_to_all(outgoing, 'req', split_axis=0, concat_axis=0, tiled=True)]
    convert_element_type x0 -> x2, local copies, waits for them, and re-layouts: none -> 2.72 us  [rms_norm(): return (values * factor * gain_vec).astype(jnp.bfloat16)]
    all_to_all x1, waiting for transfers between devices: 2.12 us -> 4.13 us  [shards(): lax.all_to_all(partial.reshape(n_kv, sub_rows, partial.shape[1]), 'kv', s...]
    reshape x0 -> x5, local copies, waits for them, and re-layouts: none -> 1.99 us  [the longest x1 1.18 us: shards(): tokens = gathered.transpose(1, 0, 2).reshape(local_rows, n_kv * col_width)]
    select_n x0 -> x3, other arithmetic: none -> 1.62 us  [the longest x1 0.84 us: shards(): source_row = (perm % local_rows).reshape(n_req, local_rows)]
  transfers between devices with their start and end apart: 3 -> 5, of which waited for: 3 -> 4; matrix products, arithmetic and copies ran while one was open for 4% -> 10% of each run, Pallas kernels for 0% -> 0%
where the time goes in v3:
time: 115 us; the launch traced here: 114 us
  starting transfers between devices  27.2 us (24%)
  waiting for transfers between devices  26.8 us (23%)
  matrix products  25.4 us (22%)
  local copies, waits for them, and re-layouts  20 us (17%)
  other arithmetic  14.1 us (12%)
    all_to_all x1, waiting for transfers between devices, shards(): lax.all_to_all(outgoing, 'req', split_axis=0, concat_axis=0, tiled=True)  7.69 us
    all_to_all x1, waiting for transfers between devices, shards(): lax.all_to_all(expert_apply(arrived, gate_up, down), 'req', split_axis=0,...  7.62 us
    all_to_all x1, waiting for transfers between devices, shards(): lax.all_to_all(spread, 'kv', split_axis=0, concat_axis=0, tiled=True)  7.38 us
    all_to_all x1, starting transfers between devices, shards(): lax.all_to_all(outgoing, 'req', split_axis=0, concat_axis=0, tiled=True)  7.22 us
    all_to_all x1, starting transfers between devices, shards(): lax.all_to_all(outgoing_rows.reshape(n_req, deal, col_width), 'req', spli...  7.12 us
    dot_general x1, matrix products, attend(): jnp.einsum('pkgt,pkdt->pkgd', weights.astype(jnp.bfloat16), kv_cache[:, :...  6.53 us
    dot_general x1, matrix products, attend(): jnp.einsum('pkgd,pkdt->pkgt', page_queries, kv_cache[:, :, :head_dim, :],...  5.62 us
    all_to_all x1, starting transfers between devices, shards(): lax.all_to_all(spread, 'kv', split_axis=0, concat_axis=0, tiled=True)  5.31 us
  transfers between devices with their start and end apart: 5, of which 4 were waited for; matrix products, arithmetic and copies ran while one was open for 10% of the time, Pallas kernels for 0%

profile of v3, /device:TPU:0, one launch (start us, length us, event | category | flops | bytes accessed | tf_op | source)
XLA Modules:
  0.0 113.8 jit_solution(18385487759824137292)
XLA Ops:
  0.0 0.8 add_select_fusion.1
  2.4 0.9 convolution_convert_fusion.4
  3.9 7.1 %all-to-all-start = ((bf16[16,4,192]{2,1,0:T(4,128)(2,1)}), bf16[16,4,192]{2,1,0:T(4,128)(2,1)S(1)}, u32[]{:S(2)}, u32[]{:S(2)}) async-start(bf16[16,4,192]{2,1,0:T(4,128)(2,1)} %reshape.332), calls=%async_computation | async-start | bytes 65536 | tf_op jit(solution)/shard_map/all_to_all | solution.py:141
  12.6 0.9 fusion.7
  13.5 0.8 select_reduce_fusion
  20.7 5.3 %all-to-all-start.1 = ((bf16[8,64,192]{2,1,0:T(8,128)(2,1)}), bf16[8,64,192]{2,1,0:T(8,128)(2,1)S(1)}, u32[]{:S(2)}, u32[]{:S(2)}) async-start(bf16[8,64,192]{2,1,0:T(8,128)(2,1)} %broadcast_in_dim.84), calls=%async_computation.1 | async-start | bytes 524288 | tf_op jit(solution)/shard_map/all_to_all | solution.py:154
  26.2 7.4 %all-to-all-done.1 = bf16[8,64,192]{2,1,0:T(8,128)(2,1)S(1)} async-done(((bf16[8,64,192]{2,1,0:T(8,128)(2,1)}), bf16[8,64,192]{2,1,0:T(8,128)(2,1)S(1)}, u32[]{:S(2)}, u32[]{:S(2)}) %all-to-all-start.1) | async-done | bytes 196640 | tf_op jit(solution)/shard_map/all_to_all | solution.py:154
  33.9 0.8 copy.109
  34.7 1.9 %convert_element_type.108 = bf16[64,1536]{1,0:T(8,128)(2,1)} reshape(bf16[64,8,192]{2,1,0:T(8,128)(2,1)} %copy.109) | data formatting | bytes 393216 | tf_op jit(solution)/shard_map/convert_element_type | solution.py:16
  36.6 1.7 %convolution_bitcast_fusion = bf16[64,1,320]{2,0,1:T(8,128)(2,1)S(1)} fusion(bf16[64,1536]{1,0:T(8,128)(2,1)} %convert_element_type.108, bf16[1,1536,320]{1,2,0:T(8,128)(2,1)} %param.19), kind=kOutput, calls=%fused_computation.21 | convolution fusion | flops 62914560 | bytes 1220608 | tf_op jit(solution)/shard_map/sd,hdc->shc/dot_general | solution.py:25
  39.5 0.9 convolution_convert_fusion.2
  41.1 0.9 copy.135
  42.0 1.9 %copy.111 = bf16[320,3,64]{2,1,0:T(4,128)(2,1)} copy(bf16[320,3,64]{0,2,1:T(8,128)(2,1)} %bitcast.103) | data formatting | bytes 245760 | tf_op jit(solution)/shard_map/reshape.5
  43.8 5.6 %fusion.56 = (f32[320,3]{1,0:T(8,128)}, f32[320,3,128]{2,1,0:T(4,128)}) fusion(bf16[320,3,64]{2,1,0:T(4,128)(2,1)} %copy.111, bf16[320,1,128,128]{3,2,0,1:T(8,128)(2,1)} %bitcast.106, pred[320,128]{1,0:T(8,128)(4,1)S(1)} %add_compare_fusion), kind=kOutput, calls=%fused_computation.120 | convolution fusion | flops 16096320 | bytes 6106880 | tf_op jit(solution)/shard_map/pkgd,pkdt->pkgt/dot_general | solution.py:50
  49.4 1.0 copy.112
  51.5 0.8 copy.114
  52.3 1.9 %fusion.26 = f32[320,3]{1,0:T(8,128)S(1)} fusion(f32[320,3,128]{2,1,0:T(4,128)} %get-tuple-element.14, f32[320,3]{1,0:T(8,128)} %copy.114, pred[320,128]{1,0:T(8,128)(4,1)S(1)} %add_compare_fusion), kind=kLoop, calls=%fused_computation.40 | loop fusion | flops 367680 | bytes 540160 | tf_op jit(solution)/shard_map/reduce_sum | solution.py:74
  54.3 6.5 %fusion.2 = f32[320,3,64]{2,1,0:T(4,128)} fusion(bf16[320,1,128,128]{3,2,0,1:T(8,128)(2,1)} %bitcast.107, f32[320,3,128]{2,1,0:T(4,128)} %get-tuple-element.14, f32[320,3]{1,0:T(8,128)} %copy.114, pred[320,128]{1,0:T(8,128)(4,1)S(1)} %add_compare_fusion), kind=kOutput, calls=%fused_computation.4 | convolution fusion | flops 16097280 | bytes 6348800 | tf_op jit(solution)/shard_map/pkgt,pkdt->pkgd/dot_general | solution.py:75
  61.0 2.1 %copy.116 = f32[320,3,64]{0,2,1:T(8,128)} copy(f32[320,3,64]{2,1,0:T(4,128)} %fusion.2) | data formatting | bytes 491520 | tf_op jit(solution)/shard_map/pkgt,pkdt->pkgd/dot_general | solution.py:75
  63.1 1.3 %fusion.18 = bf16[64,3,64]{2,0,1:T(8,128)(2,1)S(1)} fusion(f32[320,3,64]{0,2,1:T(8,128)} %copy.116, pred[64,320]{1,0:T(8,128)(4,1)S(1)} %fusion.7, f32[64,3]{0,1:T(4,128)S(1)} %convolution_add_fusion.1, f32[64,64]{1,0:T(8,128)} %get-tuple-element.7, f32[64,3]{0,1:T(4,128)S(1)} %bitcast_convert_fusion), kind=kOutput, calls=%fused_computation.25 | convolution fusion | flops 47235072 | bytes 308736 | tf_op jit(solution)/shard_map/dot_general | solution.py:85
  64.5 2.0 %fusion.8 = bf16[8,8,1536]{2,1,0:T(8,128)(2,1)} fusion(bf16[64,192]{0,1:T(8,128)(2,1)S(1)} %bitcast.104, bf16[1,192,1536]{2,1,0:T(8,128)(2,1)} %param.20), kind=kOutput, calls=%fused_computation.14 | convolution fusion | flops 37847040 | bytes 811008 | tf_op jit(solution)/shard_map/dot_general | solution.py:161
  66.5 4.0 %all-to-all-start.2 = ((bf16[8,8,1536]{2,1,0:T(8,128)(2,1)}), bf16[8,8,1536]{2,1,0:T(8,128)(2,1)}, u32[]{:S(2)}, u32[]{:S(2)}) async-start(bf16[8,8,1536]{2,1,0:T(8,128)(2,1)} %fusion.8), calls=%async_computation.2 | async-start | bytes 393216 | tf_op jit(solution)/shard_map/all_to_all | solution.py:162
  71.2 0.8 copy.107
  72.1 1.2 %reshape.334 = bf16[64,1536]{1,0:T(8,128)(2,1)S(1)} reshape(bf16[64,8,192]{2,1,0:T(8,128)(2,1)} %copy.107) | data formatting | bytes 393216 | tf_op jit(solution)/shard_map/reshape | solution.py:155
  73.3 4.1 %all-to-all-done.2 = bf16[8,8,1536]{2,1,0:T(8,128)(2,1)} async-done(((bf16[8,8,1536]{2,1,0:T(8,128)(2,1)}), bf16[8,8,1536]{2,1,0:T(8,128)(2,1)}, u32[]{:S(2)}, u32[]{:S(2)}) %all-to-all-start.2) | async-done | bytes 196640 | tf_op jit(solution)/shard_map/all_to_all | solution.py:162
  77.4 1.0 convert_reduce_fusion
  78.6 0.9 fusion.58
  81.3 7.2 %all-to-all-start.3 = ((bf16[16,2,1,1536]{3,1,2,0:T(2,128)(2,1)}), bf16[16,2,1,1536]{3,1,2,0:T(2,128)(2,1)S(1)}, u32[]{:S(2)}, u32[]{:S(2)}) async-start(bf16[16,2,1,1536]{3,1,2,0:T(2,128)(2,1)} %bitcast.26), calls=%async_computation.3 | async-start | bytes 196608 | tf_op jit(solution)/shard_map/all_to_all | solution.py:195
  88.6 7.7 %all-to-all-done.3 = bf16[16,2,1,1536]{3,1,2,0:T(2,128)(2,1)S(1)} async-done(((bf16[16,2,1,1536]{3,1,2,0:T(2,128)(2,1)}), bf16[16,2,1,1536]{3,1,2,0:T(2,128)(2,1)S(1)}, u32[]{:S(2)}, u32[]{:S(2)}) %all-to-all-start.3) | async-done | bytes 98336 | tf_op jit(solution)/shard_map/all_to_all | solution.py:195
  96.4 4.0 %fusion.9 = f32[1,32,2048]{2,1,0:T(8,128)S(1)} fusion(bf16[32,1536]{1,0:T(8,128)(2,1)S(1)} %reshape.347, bf16[1,1536,2048]{2,1,0:T(8,128)(2,1)} %param.24), kind=kOutput, calls=%fused_computation.15 | convolution fusion | flops 201326592 | bytes 6651904 | tf_op jit(solution)/shard_map/erd,edf->erf/dot_general | solution.py:98
  101.6 3.5 %all-to-all-start.4 = ((bf16[16,2,1,1536]{3,1,2,0:T(2,128)(2,1)}), bf16[16,2,1,1536]{3,1,2,0:T(2,128)(2,1)S(1)}, u32[]{:S(2)}, u32[]{:S(2)}) async-start(bf16[16,2,1,1536]{3,1,2,0:T(2,128)(2,1)} %bitcast.31), calls=%async_computation.4 | async-start | bytes 196608 | tf_op jit(solution)/shard_map/all_to_all | solution.py:196
  105.3 7.6 %all-to-all-done.4 = bf16[16,2,1,1536]{3,1,2,0:T(2,128)(2,1)S(1)} async-done(((bf16[16,2,1,1536]{3,1,2,0:T(2,128)(2,1)}), bf16[16,2,1,1536]{3,1,2,0:T(2,128)(2,1)S(1)}, u32[]{:S(2)}, u32[]{:S(2)}) %all-to-all-start.4) | async-done | bytes 98336 | tf_op jit(solution)/shard_map/all_to_all | solution.py:196
  (75 shorter events, 18.9 us)
Async XLA Ops:
  0.0 100.3 %copy-start = (bf16[1,1024,1536]{2,1,0:T(8,128)(2,1)S(1)}, bf16[1,1024,1536]{2,1,0:T(8,128)(2,1)}, u32[]{:S(2)}) copy-start(bf16[1,1024,1536]{2,1,0:T(8,128)(2,1)} %param.25) | copy-start | bytes 9437188
  3.9 15.8 %all-to-all-start = ((bf16[16,4,192]{2,1,0:T(4,128)(2,1)}), bf16[16,4,192]{2,1,0:T(4,128)(2,1)S(1)}, u32[]{:S(2)}, u32[]{:S(2)}) async-start(bf16[16,4,192]{2,1,0:T(4,128)(2,1)} %reshape.332), calls=%async_computation | async-start | bytes 65536 | tf_op jit(solution)/shard_map/all_to_all | solution.py:141
  17.2 1.0 copy-start.2
  20.7 12.9 %all-to-all-start.1 = ((bf16[8,64,192]{2,1,0:T(8,128)(2,1)}), bf16[8,64,192]{2,1,0:T(8,128)(2,1)S(1)}, u32[]{:S(2)}, u32[]{:S(2)}) async-start(bf16[8,64,192]{2,1,0:T(8,128)(2,1)} %broadcast_in_dim.84), calls=%async_computation.1 | async-start | bytes 524288 | tf_op jit(solution)/shard_map/all_to_all | solution.py:154
  54.2 24.3 %copy-start.1 = (f32[1536]{0:T(1024)S(1)}, f32[1536]{0:T(1024)}, u32[]{:S(2)}) copy-start(f32[1536]{0:T(1024)} %param.21) | copy-start | bytes 18436
  66.5 10.9 %all-to-all-start.2 = ((bf16[8,8,1536]{2,1,0:T(8,128)(2,1)}), bf16[8,8,1536]{2,1,0:T(8,128)(2,1)}, u32[]{:S(2)}, u32[]{:S(2)}) async-start(bf16[8,8,1536]{2,1,0:T(8,128)(2,1)} %fusion.8), calls=%async_computation.2 | async-start | bytes 393216 | tf_op jit(solution)/shard_map/all_to_all | solution.py:162
  81.3 15.0 %all-to-all-start.3 = ((bf16[16,2,1,1536]{3,1,2,0:T(2,128)(2,1)}), bf16[16,2,1,1536]{3,1,2,0:T(2,128)(2,1)S(1)}, u32[]{:S(2)}, u32[]{:S(2)}) async-start(bf16[16,2,1,1536]{3,1,2,0:T(2,128)(2,1)} %bitcast.26), calls=%async_computation.3 | async-start | bytes 196608 | tf_op jit(solution)/shard_map/all_to_all | solution.py:195
  96.3 16.6 %copy-start.3 = (s32[8,2]{0,1:T(2,128)S(1)}, s32[8,2]{0,1:T(2,128)}, u32[]{:S(2)}) copy-start(s32[8,2]{0,1:T(2,128)} %copy.126) | copy-start | bytes 196
  101.6 11.3 %all-to-all-start.4 = ((bf16[16,2,1,1536]{3,1,2,0:T(2,128)(2,1)}), bf16[16,2,1,1536]{3,1,2,0:T(2,128)(2,1)S(1)}, u32[]{:S(2)}, u32[]{:S(2)}) async-start(bf16[16,2,1,1536]{3,1,2,0:T(2,128)(2,1)} %bitcast.31), calls=%async_computation.4 | async-start | bytes 196608 | tf_op jit(solution)/shard_map/all_to_all | solution.py:196

commit v4 on v3

--- a/solution.py
+++ b/solution.py
@@ -2,6 +2,8 @@
 import jax.numpy as jnp
 from jax import lax
 from jax.sharding import PartitionSpec as P
+from jax.experimental import pallas as pl
+import functools
 
 REQ_DEV = 64
 
@@ -14,6 +16,48 @@
     values = values.astype(jnp.float32)
     factor = lax.rsqrt(jnp.mean(values * values, axis=-1, keepdims=True) + EPS_NORM)
     return (values * factor * gain_vec).astype(jnp.bfloat16)
+
+
+def page_attention_kernel(scale, head_dim, q_ref, live_ref, kv_ref, acc_ref, peak_ref, sum_ref):
+    q = q_ref[...]
+    keys = kv_ref[:, 0, :head_dim, :]
+    values = kv_ref[:, 0, head_dim:, :]
+    live = live_ref[...] > 0.5
+    scores = jnp.einsum("pgd,pdt->pgt", q, keys, preferred_element_type=jnp.float32) * scale
+    scores = jnp.where(live, scores, NEG_FILL)
+    peak = jnp.max(scores, axis=2, keepdims=True)
+    weights = jnp.where(live, jnp.exp(scores - peak), 0.0)
+    peak_ref[...] = peak
+    sum_ref[...] = jnp.sum(weights, axis=2, keepdims=True)
+    acc_ref[...] = jnp.einsum(
+        "pgt,pdt->pgd", weights.astype(values.dtype), values, preferred_element_type=jnp.float32
+    )
+
+
+def page_attention(page_queries, live_f, kv_cache, block_pages=32):
+    pool_pages, rows, head_dim = page_queries.shape
+    page_len = kv_cache.shape[3]
+    grid = (pool_pages // block_pages,)
+    kernel = functools.partial(page_attention_kernel, head_dim ** (-0.5), head_dim)
+    return pl.pallas_call(
+        kernel,
+        grid=grid,
+        in_specs=[
+            pl.BlockSpec((block_pages, rows, head_dim), lambda i: (i, 0, 0)),
+            pl.BlockSpec((block_pages, 1, page_len), lambda i: (i, 0, 0)),
+            pl.BlockSpec((block_pages, 1, 2 * head_dim, page_len), lambda i: (i, 0, 0, 0)),
+        ],
+        out_specs=[
+            pl.BlockSpec((block_pages, rows, head_dim), lambda i: (i, 0, 0)),
+            pl.BlockSpec((block_pages, rows, 1), lambda i: (i, 0, 0)),
+            pl.BlockSpec((block_pages, rows, 1), lambda i: (i, 0, 0)),
+        ],
+        out_shape=[
+            jax.ShapeDtypeStruct((pool_pages, rows, head_dim), jnp.float32),
+            jax.ShapeDtypeStruct((pool_pages, rows, 1), jnp.float32),
+            jax.ShapeDtypeStruct((pool_pages, rows, 1), jnp.float32),
+        ],
+    )(page_queries, live_f, kv_cache)
 
 
 def attend(normed, seq_lens, page_table, kv_cache, qkv_weight):
@@ -41,54 +85,39 @@
     position = page_order[:, None] * page_len + jnp.arange(page_len, dtype=jnp.int32)[None, :]
     live = position < owner_len[:, None]
     scale_factor = head_dim ** (-0.5)
+    row_pad = 8
+    padded_queries = jnp.pad(
+        queries.reshape(slot_count, groups, head_dim), ((0, 0), (0, row_pad - groups), (0, 0))
+    )
     page_queries = jnp.dot(
         belongs.T.astype(jnp.bfloat16),
-        queries.reshape(slot_count, -1),
+        padded_queries.reshape(slot_count, -1),
         preferred_element_type=jnp.float32,
-    ).astype(jnp.bfloat16).reshape(pool_pages, local_heads, groups, head_dim)
-    scores = (
-        jnp.einsum(
-            "pkgd,pkdt->pkgt",
-            page_queries,
-            kv_cache[:, :, :head_dim, :],
-            preferred_element_type=jnp.float32,
-        )
-        * scale_factor
-    )
-    scores = jnp.where(live[:, None, None, :], scores, NEG_FILL)
+    ).astype(jnp.bfloat16).reshape(pool_pages, row_pad, head_dim)
+    live_f = live.astype(jnp.float32).reshape(pool_pages, 1, page_len)
+    page_value, page_peak, page_total = page_attention(page_queries, live_f, kv_cache)
+    page_value = page_value[:, :groups, :]
+    page_peak = page_peak[:, :groups, 0]
+    page_total = page_total[:, :groups, 0]
     score_new = (
         jnp.einsum("skgd,skd->skg", queries, key_new, preferred_element_type=jnp.float32)
         * scale_factor
-    )
-    page_peak = jnp.max(scores, axis=3)
-    slot_peak = jnp.max(jnp.where(belongs[:, :, None, None], page_peak[None], NEG_FILL), axis=1)
+    ).reshape(slot_count, groups)
+    slot_peak = jnp.max(jnp.where(belongs[:, :, None], page_peak[None], NEG_FILL), axis=1)
     slot_peak = jnp.maximum(slot_peak, score_new)
-    page_peak_of_owner = jnp.max(
-        jnp.where(belongs[:, :, None, None], slot_peak[:, None], NEG_FILL), axis=0
-    )
-    weights = jnp.where(
-        live[:, None, None, :],
-        jnp.exp(scores - page_peak_of_owner[..., None]),
-        0.0,
-    )
-    page_total = jnp.sum(weights, axis=3)
-    page_value = jnp.einsum(
-        "pkgt,pkdt->pkgd",
-        weights.astype(jnp.bfloat16),
-        kv_cache[:, :, head_dim:, :],
-        preferred_element_type=jnp.float32,
-    )
+    page_peak_of_owner = jnp.max(jnp.where(belongs[:, :, None], slot_peak[:, None], NEG_FILL), axis=0)
+    page_scale = jnp.exp(page_peak - page_peak_of_owner)
     belongs_f = belongs.astype(jnp.float32)
-    total_sum = jnp.dot(
-        belongs_f, page_total.reshape(pool_pages, -1), precision=lax.Precision.HIGHEST
-    ).reshape(slot_count, local_heads, groups)
+    total_sum = jnp.dot(belongs_f, page_total * page_scale, precision=lax.Precision.HIGHEST)
     value_sum = jnp.dot(
-        belongs_f, page_value.reshape(pool_pages, -1), precision=lax.Precision.HIGHEST
-    ).reshape(slot_count, local_heads, groups, head_dim)
+        belongs_f,
+        (page_value * page_scale[..., None]).reshape(pool_pages, -1),
+        precision=lax.Precision.HIGHEST,
+    ).reshape(slot_count, groups, head_dim)
     weight_new = jnp.exp(score_new - slot_peak)
     total_sum = total_sum + weight_new
     rounded_new = lax.optimization_barrier(weight_new.astype(jnp.bfloat16)).astype(jnp.float32)
-    value_sum = value_sum + rounded_new[..., None] * value_new.astype(jnp.float32)[:, :, None, :]
+    value_sum = value_sum + rounded_new[..., None] * value_new.astype(jnp.float32).reshape(slot_count, 1, head_dim)
     return (value_sum / total_sum[..., None]).astype(jnp.bfloat16).reshape(slot_count, -1)
 
 

time: 115 us -> 127 us (1.10)
  matrix products: 25.4 us -> 13.1 us
  Pallas kernels: 0 us -> 11.1 us
  local copies, waits for them, and re-layouts: 20 us -> 30.3 us
  other arithmetic: 14.1 us -> 17.4 us
    dot_general x5 -> x3, matrix products: 14.6 us -> 3.07 us  [the longest x1 1.94 us: attend(): jnp.dot(belongs_f, (page_value * page_scale[..., None]).reshape(pool_page...]
    pallas_call x0 -> x1, Pallas kernels: none -> 11.1 us  [page_attention(): pl.pallas_call(kernel, grid=grid, in_specs=[pl.BlockSpec((block_pages, ro...]
    slice x0 -> x4, local copies, waits for them, and re-layouts: none -> 7.18 us  [the longest x2 3.6 us: attend(): page_peak = page_peak[:, :groups, 0]]
    mul x0 -> x2, local copies, waits for them, and re-layouts: none -> 2.83 us  [attend(): page_value * page_scale[..., None]]
    mul x2, other arithmetic: 0.62 us -> 3.2 us  [the longest x1 2.59 us: attend(): page_value * page_scale[..., None]]
    exp x0 -> x1, other arithmetic: none -> 2.57 us  [attend(): page_scale = jnp.exp(page_peak - page_peak_of_owner)]
    reshape x0 -> x1, local copies, waits for them, and re-layouts: none -> 2.2 us  [attend(): page_queries = jnp.dot(belongs.T.astype(jnp.bfloat16), padded_queries.res...]
    dot_general x1 -> x0, local copies, waits for them, and re-layouts: 2.07 us -> none  [attend(): jnp.einsum('pkgt,pkdt->pkgd', weights.astype(jnp.bfloat16), kv_cache[:, :...]
where the time goes in v4:
time: 127 us; the launch traced here: 125 us
  local copies, waits for them, and re-layouts  30.3 us (24%)
  starting transfers between devices  27.2 us (21%)
  waiting for transfers between devices  25.9 us (20%)
  other arithmetic  17.4 us (14%)
  matrix products  13.1 us (10%)
  Pallas kernels  11.1 us (9%)
    pallas_call x1, Pallas kernels, page_attention(): pl.pallas_call(kernel, grid=grid, in_specs=[pl.BlockSpec((block_pages, ro...  11.1 us
    all_to_all x1, waiting for transfers between devices, shards(): lax.all_to_all(outgoing, 'req', split_axis=0, concat_axis=0, tiled=True)  7.69 us
    all_to_all x1, waiting for transfers between devices, shards(): lax.all_to_all(expert_apply(arrived, gate_up, down), 'req', split_axis=0,...  7.62 us
    all_to_all x1, starting transfers between devices, shards(): lax.all_to_all(outgoing, 'req', split_axis=0, concat_axis=0, tiled=True)  7.22 us
    all_to_all x1, starting transfers between devices, shards(): lax.all_to_all(outgoing_rows.reshape(n_req, deal, col_width), 'req', spli...  7.12 us
    all_to_all x1, waiting for transfers between devices, shards(): lax.all_to_all(spread, 'kv', split_axis=0, concat_axis=0, tiled=True)  5.78 us
    all_to_all x1, starting transfers between devices, shards(): lax.all_to_all(spread, 'kv', split_axis=0, concat_axis=0, tiled=True)  5.31 us
    all_to_all x1, waiting for transfers between devices, shards(): lax.all_to_all(partial.reshape(n_kv, sub_rows, partial.shape[1]), 'kv', s...  4.77 us
  transfers between devices with their start and end apart: 5, of which 4 were waited for; matrix products, arithmetic and copies ran while one was open for 10% of the time, Pallas kernels for 0%

profile of v4, /device:TPU:0, one launch (start us, length us, event | category | flops | bytes accessed | tf_op | source)
XLA Modules:
  0.0 125.2 jit_solution(11191017435355625817)
XLA Ops:
  2.4 0.9 convolution_convert_fusion.5
  3.9 7.1 %all-to-all-start = ((bf16[16,4,192]{2,1,0:T(4,128)(2,1)}), bf16[16,4,192]{2,1,0:T(4,128)(2,1)S(1)}, u32[]{:S(2)}, u32[]{:S(2)}) async-start(bf16[16,4,192]{2,1,0:T(4,128)(2,1)} %reshape.291), calls=%async_computation | async-start | bytes 65536 | tf_op jit(solution)/shard_map/all_to_all | solution.py:170
  13.4 0.9 fusion.5
  21.0 5.3 %all-to-all-start.1 = ((bf16[8,64,192]{2,1,0:T(8,128)(2,1)}), bf16[8,64,192]{2,1,0:T(8,128)(2,1)S(1)}, u32[]{:S(2)}, u32[]{:S(2)}) async-start(bf16[8,64,192]{2,1,0:T(8,128)(2,1)} %broadcast_in_dim.61), calls=%async_computation.1 | async-start | bytes 524288 | tf_op jit(solution)/shard_map/all_to_all | solution.py:183
  26.5 1.7 %compare_convert_fusion.live_ref = f32[320,1,128]{2,1,0:T(1,128)} fusion(s32[320,1,128]{2,1,0:T(1,128)S(1)} %bitcast.92, s32[320]{0:T(512)S(1)} %select_reduce_fusion.3), kind=kLoop, calls=%fused_computation.32 | loop fusion | flops 122880 | bytes 328960 | tf_op jit(solution)/shard_map/convert_element_type | solution.py:97
  28.1 5.8 %all-to-all-done.1 = bf16[8,64,192]{2,1,0:T(8,128)(2,1)S(1)} async-done(((bf16[8,64,192]{2,1,0:T(8,128)(2,1)}), bf16[8,64,192]{2,1,0:T(8,128)(2,1)S(1)}, u32[]{:S(2)}, u32[]{:S(2)}) %all-to-all-start.1) | async-done | bytes 196640 | tf_op jit(solution)/shard_map/all_to_all | solution.py:183
  35.1 1.9 %convert_element_type.109 = bf16[64,1536]{1,0:T(8,128)(2,1)} reshape(bf16[64,8,192]{2,1,0:T(8,128)(2,1)} %copy.143) | data formatting | bytes 393216 | tf_op jit(solution)/shard_map/convert_element_type | solution.py:18
  36.9 1.7 %fusion.16 = bf16[64,1,320]{2,0,1:T(8,128)(2,1)S(1)} fusion(bf16[64,1536]{1,0:T(8,128)(2,1)} %convert_element_type.109, bf16[1,1536,320]{1,2,0:T(8,128)(2,1)} %param.19), kind=kOutput, calls=%fused_computation.21 | convolution fusion | flops 62935040 | bytes 1220608 | tf_op jit(solution)/shard_map/sd,hdc->shc/dot_general | solution.py:69
  39.5 1.0 convolution_convert_fusion.2
  40.5 1.9 %copy.145 = bf16[320,512]{0,1:T(8,128)(2,1)} copy(bf16[320,512]{1,0:T(8,128)(2,1)} %convolution_convert_fusion.2) | data formatting | bytes 655360 | tf_op jit(solution)/shard_map/convert_element_type | solution.py:96
  42.4 2.2 %copy.147.q_ref = bf16[320,8,64]{2,1,0:T(8,128)(2,1)} copy(bf16[320,8,64]{0,2,1:T(8,128)(2,1)} %bitcast.91) | data formatting | bytes 655360 | tf_op jit(solution)/shard_map/reshape | solution.py:96
  44.6 11.1 %shard_map.127 = (f32[320,8,64]{2,1,0:T(8,128)}, f32[320,8,1]{2,1,0:T(8,128)}, f32[320,8,1]{2,1,0:T(8,128)}) custom-call(bf16[320,8,64]{2,1,0:T(8,128)(2,1)} %copy.147.q_ref, f32[320,1,128]{2,1,0:T(1,128)} %compare_convert_fusion.live_ref, bf16[320,1,128,128]{3,2,1,0:T(8,128)(2,1)} %kv_ref.1), custom_call_target="tpu_custom_call" | custom-call | tf_op jit(solution)/shard_map/pallas_call | solution.py:42
  55.7 2.2 %slice.32 = f32[320,3,1]{2,1,0:T(4,128)} slice(f32[320,8,1]{2,1,0:T(8,128)} %get-tuple-element.10), slice={[0:320], [0:3], [0:1]} | slice | bytes 7680 | tf_op jit(solution)/shard_map/slice | solution.py:101
  58.0 1.3 %copy.153 = f32[320,3,1]{0,1,2:T(4,128)S(1)} copy(f32[320,3,1]{2,1,0:T(4,128)} %slice.32) | data formatting | bytes 7680 | tf_op jit(solution)/shard_map/slice | solution.py:101
  59.3 2.3 %slice.29 = f32[320,3,1]{2,1,0:T(4,128)} slice(f32[320,8,1]{2,1,0:T(8,128)} %get-tuple-element.9), slice={[0:320], [0:3], [0:1]} | slice | bytes 7680 | tf_op jit(solution)/shard_map/slice | solution.py:100
  61.6 1.3 %copy.148 = f32[320,3,1]{0,1,2:T(4,128)S(1)} copy(f32[320,3,1]{2,1,0:T(4,128)} %slice.29) | data formatting | bytes 7680 | tf_op jit(solution)/shard_map/slice | solution.py:100
  63.3 1.2 copy.149
  64.5 2.6 %subtract_exponential_fusion = f32[320,3,1]{2,1,0:T(4,128)} fusion(f32[320,3,1]{2,1,0:T(4,128)} %copy.149, f32[320,8,1]{2,1,0:T(8,128)} %get-tuple-element.9), kind=kLoop, calls=%fused_computation.30 | loop fusion | flops 960 | bytes 11520 | tf_op jit(solution)/shard_map/exp | solution.py:109
  67.1 1.4 %copy.150 = f32[320,3,1]{0,1,2:T(4,128)S(1)} copy(f32[320,3,1]{2,1,0:T(4,128)} %subtract_exponential_fusion) | data formatting | bytes 7680 | tf_op jit(solution)/shard_map/exp | solution.py:109
  69.3 2.6 %slice_multiply_fusion = f32[320,3,64]{2,1,0:T(4,128)} fusion(f32[320,8,64]{2,1,0:T(8,128)} %get-tuple-element.8, f32[320,3]{1,0:T(8,128)} %copy.151), kind=kLoop, calls=%fused_computation.31 | loop fusion | flops 61440 | bytes 495360 | tf_op jit(solution)/shard_map/mul | solution.py:114
  71.8 2.0 %copy.152 = f32[320,3,64]{0,2,1:T(8,128)} copy(f32[320,3,64]{2,1,0:T(4,128)} %slice_multiply_fusion) | data formatting | bytes 491520 | tf_op jit(solution)/shard_map/mul | solution.py:114
  73.9 1.9 %fusion.15 = bf16[64,3,64]{2,0,1:T(8,128)(2,1)} fusion(f32[320,3,64]{0,2,1:T(8,128)} %copy.152, pred[64,320]{1,0:T(8,128)(4,1)S(1)} %fusion.5, f32[64,3]{0,1:T(4,128)S(1)} %convolution_add_fusion.1, f32[64,64]{1,0:T(8,128)} %get-tuple-element.13, f32[64,3]{0,1:T(4,128)S(1)} %convert_element_type.114), kind=kOutput, calls=%fused_computation.20 | convolution fusion | flops 47235072 | bytes 308736 | tf_op jit(solution)/shard_map/dot_general | solution.py:112
  76.7 2.0 %fusion.6 = bf16[8,8,1536]{2,1,0:T(8,128)(2,1)} fusion(bf16[64,192]{0,1:T(8,128)(2,1)S(1)} %bitcast.96, bf16[1,192,1536]{2,1,0:T(8,128)(2,1)} %param.20), kind=kOutput, calls=%fused_computation.10 | convolution fusion | flops 37847040 | bytes 811008 | tf_op jit(solution)/shard_map/dot_general | solution.py:190
  78.7 4.0 %all-to-all-start.2 = ((bf16[8,8,1536]{2,1,0:T(8,128)(2,1)}), bf16[8,8,1536]{2,1,0:T(8,128)(2,1)}, u32[]{:S(2)}, u32[]{:S(2)}) async-start(bf16[8,8,1536]{2,1,0:T(8,128)(2,1)} %fusion.6), calls=%async_computation.2 | async-start | bytes 393216 | tf_op jit(solution)/shard_map/all_to_all | solution.py:191
  83.6 1.2 reshape.293
  84.8 4.8 %all-to-all-done.2 = bf16[8,8,1536]{2,1,0:T(8,128)(2,1)} async-done(((bf16[8,8,1536]{2,1,0:T(8,128)(2,1)}), bf16[8,8,1536]{2,1,0:T(8,128)(2,1)}, u32[]{:S(2)}, u32[]{:S(2)}) %all-to-all-start.2) | async-done | bytes 196640 | tf_op jit(solution)/shard_map/all_to_all | solution.py:191
  89.5 1.0 convert_reduce_fusion
  92.6 7.2 %all-to-all-start.3 = ((bf16[16,2,1,1536]{3,1,2,0:T(2,128)(2,1)}), bf16[16,2,1,1536]{3,1,2,0:T(2,128)(2,1)S(1)}, u32[]{:S(2)}, u32[]{:S(2)}) async-start(bf16[16,2,1,1536]{3,1,2,0:T(2,128)(2,1)} %bitcast.25), calls=%async_computation.3 | async-start | bytes 196608 | tf_op jit(solution)/shard_map/all_to_all | solution.py:224
  100.0 7.7 %all-to-all-done.3 = bf16[16,2,1,1536]{3,1,2,0:T(2,128)(2,1)S(1)} async-done(((bf16[16,2,1,1536]{3,1,2,0:T(2,128)(2,1)}), bf16[16,2,1,1536]{3,1,2,0:T(2,128)(2,1)S(1)}, u32[]{:S(2)}, u32[]{:S(2)}) %all-to-all-start.3) | async-done | bytes 98336 | tf_op jit(solution)/shard_map/all_to_all | solution.py:224
  107.7 4.0 %fusion.7 = f32[1,32,2048]{2,1,0:T(8,128)S(1)} fusion(bf16[32,1536]{1,0:T(8,128)(2,1)S(1)} %reshape.305, bf16[1,1536,2048]{2,1,0:T(8,128)(2,1)} %param.24), kind=kOutput, calls=%fused_computation.11 | convolution fusion | flops 201326592 | bytes 6651904 | tf_op jit(solution)/shard_map/erd,edf->erf/dot_general | solution.py:127
  113.0 3.5 %all-to-all-start.4 = ((bf16[16,2,1,1536]{3,1,2,0:T(2,128)(2,1)}), bf16[16,2,1,1536]{3,1,2,0:T(2,128)(2,1)S(1)}, u32[]{:S(2)}, u32[]{:S(2)}) async-start(bf16[16,2,1,1536]{3,1,2,0:T(2,128)(2,1)} %bitcast.30), calls=%async_computation.4 | async-start | bytes 196608 | tf_op jit(solution)/shard_map/all_to_all | solution.py:225
  116.7 7.6 %all-to-all-done.4 = bf16[16,2,1,1536]{3,1,2,0:T(2,128)(2,1)S(1)} async-done(((bf16[16,2,1,1536]{3,1,2,0:T(2,128)(2,1)}), bf16[16,2,1,1536]{3,1,2,0:T(2,128)(2,1)S(1)}, u32[]{:S(2)}, u32[]{:S(2)}) %all-to-all-start.4) | async-done | bytes 98336 | tf_op jit(solution)/shard_map/all_to_all | solution.py:225
  (91 shorter events, 21.7 us)
Async XLA Ops:
  0.0 111.7 %copy-start = (bf16[1,1024,1536]{2,1,0:T(8,128)(2,1)S(1)}, bf16[1,1024,1536]{2,1,0:T(8,128)(2,1)}, u32[]{:S(2)}) copy-start(bf16[1,1024,1536]{2,1,0:T(8,128)(2,1)} %param.25) | copy-start | bytes 9437188
  3.9 16.2 %all-to-all-start = ((bf16[16,4,192]{2,1,0:T(4,128)(2,1)}), bf16[16,4,192]{2,1,0:T(4,128)(2,1)S(1)}, u32[]{:S(2)}, u32[]{:S(2)}) async-start(bf16[16,4,192]{2,1,0:T(4,128)(2,1)} %reshape.291), calls=%async_computation | async-start | bytes 65536 | tf_op jit(solution)/shard_map/all_to_all | solution.py:170
  16.9 21.8 %copy-start.3 = (s32[16]{0:T(128)}, s32[16]{0:T(128)S(1)}, u32[]{:S(2)}) copy-start(s32[16]{0:T(128)S(1)} %eq.135) | copy-start | bytes 196
  17.2 0.6 copy-start.5
  21.0 12.9 %all-to-all-start.1 = ((bf16[8,64,192]{2,1,0:T(8,128)(2,1)}), bf16[8,64,192]{2,1,0:T(8,128)(2,1)S(1)}, u32[]{:S(2)}, u32[]{:S(2)}) async-start(bf16[8,64,192]{2,1,0:T(8,128)(2,1)} %broadcast_in_dim.61), calls=%async_computation.1 | async-start | bytes 524288 | tf_op jit(solution)/shard_map/all_to_all | solution.py:183
  64.5 18.2 %copy-start.4 = (s32[16]{0:T(128)S(1)}, s32[16]{0:T(128)}, u32[]{:S(2)}) copy-start(s32[16]{0:T(128)} %copy-done.3) | copy-start | bytes 196
  64.5 18.2 %copy-start.6 = (s32[16]{0:T(128)S(1)}, s32[16]{0:T(128)}, u32[]{:S(2)}) copy-start(s32[16]{0:T(128)} %copy-done.5) | copy-start | bytes 196
  67.1 23.6 %copy-start.2 = (f32[1536]{0:T(1024)S(1)}, f32[1536]{0:T(1024)}, u32[]{:S(2)}) copy-start(f32[1536]{0:T(1024)} %param.21) | copy-start | bytes 18436
  67.1 23.7 %copy-start.1 = (bf16[1536,16]{0,1:T(8,128)(2,1)S(1)}, bf16[1536,16]{0,1:T(8,128)(2,1)}, u32[]{:S(2)}) copy-start(bf16[1536,16]{0,1:T(8,128)(2,1)} %param.22) | copy-start | bytes 147460
  78.7 10.9 %all-to-all-start.2 = ((bf16[8,8,1536]{2,1,0:T(8,128)(2,1)}), bf16[8,8,1536]{2,1,0:T(8,128)(2,1)}, u32[]{:S(2)}, u32[]{:S(2)}) async-start(bf16[8,8,1536]{2,1,0:T(8,128)(2,1)} %fusion.6), calls=%async_computation.2 | async-start | bytes 393216 | tf_op jit(solution)/shard_map/all_to_all | solution.py:191
  92.6 15.0 %all-to-all-start.3 = ((bf16[16,2,1,1536]{3,1,2,0:T(2,128)(2,1)}), bf16[16,2,1,1536]{3,1,2,0:T(2,128)(2,1)S(1)}, u32[]{:S(2)}, u32[]{:S(2)}) async-start(bf16[16,2,1,1536]{3,1,2,0:T(2,128)(2,1)} %bitcast.25), calls=%async_computation.3 | async-start | bytes 196608 | tf_op jit(solution)/shard_map/all_to_all | solution.py:224
  111.7 12.6 %copy-start.7 = (s32[8,2]{0,1:T(2,128)S(1)}, s32[8,2]{0,1:T(2,128)}, u32[]{:S(2)}) copy-start(s32[8,2]{0,1:T(2,128)} %copy.163) | copy-start | bytes 196
  113.0 11.3 %all-to-all-start.4 = ((bf16[16,2,1,1536]{3,1,2,0:T(2,128)(2,1)}), bf16[16,2,1,1536]{3,1,2,0:T(2,128)(2,1)S(1)}, u32[]{:S(2)}, u32[]{:S(2)}) async-start(bf16[16,2,1,1536]{3,1,2,0:T(2,128)(2,1)} %bitcast.30), calls=%async_computation.4 | async-start | bytes 196608 | tf_op jit(solution)/shard_map/all_to_all | solution.py:225

commit v5 on v3

--- a/solution.py
+++ b/solution.py
@@ -19,10 +19,13 @@
 def attend(normed, seq_lens, page_table, kv_cache, qkv_weight):
     pool_pages, local_heads, twice_hd, page_len = kv_cache.shape
     head_dim = twice_hd // 2
-    slot_count = normed.shape[0]
+    kv_parts, slot_count, part_width = normed.shape
     groups = qkv_weight.shape[2] // head_dim - 2
     max_pages = page_table.shape[1]
-    projected = jnp.einsum("sd,hdc->shc", normed, qkv_weight, preferred_element_type=jnp.float32)
+    weight_parts = qkv_weight.reshape(local_heads, kv_parts, part_width, qkv_weight.shape[2])
+    projected = jnp.einsum(
+        "ksd,hkdc->shc", normed, weight_parts, preferred_element_type=jnp.float32
+    )
     queries = (
         projected[:, :, : groups * head_dim]
         .reshape(slot_count, local_heads, groups, head_dim)
@@ -41,11 +44,9 @@
     position = page_order[:, None] * page_len + jnp.arange(page_len, dtype=jnp.int32)[None, :]
     live = position < owner_len[:, None]
     scale_factor = head_dim ** (-0.5)
-    page_queries = jnp.dot(
-        belongs.T.astype(jnp.bfloat16),
-        queries.reshape(slot_count, -1),
-        preferred_element_type=jnp.float32,
-    ).astype(jnp.bfloat16).reshape(pool_pages, local_heads, groups, head_dim)
+    page_queries = jnp.einsum(
+        "sp,skgd->pkgd", belongs.astype(jnp.bfloat16), queries, preferred_element_type=jnp.float32
+    ).astype(jnp.bfloat16)
     scores = (
         jnp.einsum(
             "pkgd,pkdt->pkgt",
@@ -79,12 +80,10 @@
         preferred_element_type=jnp.float32,
     )
     belongs_f = belongs.astype(jnp.float32)
-    total_sum = jnp.dot(
-        belongs_f, page_total.reshape(pool_pages, -1), precision=lax.Precision.HIGHEST
-    ).reshape(slot_count, local_heads, groups)
-    value_sum = jnp.dot(
-        belongs_f, page_value.reshape(pool_pages, -1), precision=lax.Precision.HIGHEST
-    ).reshape(slot_count, local_heads, groups, head_dim)
+    total_sum = jnp.einsum("sp,pkg->skg", belongs_f, page_total, precision=lax.Precision.HIGHEST)
+    value_sum = jnp.einsum(
+        "sp,pkgd->skgd", belongs_f, page_value, precision=lax.Precision.HIGHEST
+    )
     weight_new = jnp.exp(score_new - slot_peak)
     total_sum = total_sum + weight_new
     rounded_new = lax.optimization_barrier(weight_new.astype(jnp.bfloat16)).astype(jnp.float32)
@@ -152,18 +151,22 @@
     )
     spread = jnp.broadcast_to(picked_rows[None], (n_kv, local_rows, col_width))
     gathered = lax.all_to_all(spread, "kv", split_axis=0, concat_axis=0, tiled=True)
-    tokens = gathered.transpose(1, 0, 2).reshape(local_rows, n_kv * col_width)
-    normed = rms_norm(tokens, attn_gain)
+    gathered_f = gathered.astype(jnp.float32)
+    norm_factor = lax.rsqrt(
+        jnp.sum(gathered_f * gathered_f, axis=(0, 2), keepdims=True) / (n_kv * col_width) + EPS_NORM
+    )
+    normed = (gathered_f * norm_factor * attn_gain.reshape(n_kv, 1, col_width)).astype(jnp.bfloat16)
     head_out = attend(normed, seq_lens, page_table, kv_cache, qkv_weight)
     sub_rows = routes.shape[0]
-    width = tokens.shape[1]
+    width = n_kv * col_width
     out_flat = out_weight.reshape(-1, out_weight.shape[2])
     partial = jnp.dot(head_out, out_flat, preferred_element_type=jnp.float32).astype(jnp.bfloat16)
     partial_parts = lax.all_to_all(
         partial.reshape(n_kv, sub_rows, partial.shape[1]), "kv", split_axis=0, concat_axis=0, tiled=True
     )
     attn_rows = jnp.sum(partial_parts.astype(jnp.float32), axis=0)
-    own_tokens = lax.dynamic_slice_in_dim(tokens, kv_index * sub_rows, sub_rows, 0)
+    own_tokens = lax.dynamic_slice_in_dim(gathered, kv_index * sub_rows, sub_rows, 1)
+    own_tokens = own_tokens.transpose(1, 0, 2).reshape(sub_rows, width)
     residual = (own_tokens.astype(jnp.float32) + attn_rows).astype(jnp.bfloat16)
     normed_ffn = rms_norm(residual, ffn_gain)
     logits = jnp.dot(normed_ffn, router, preferred_element_type=jnp.float32)

time: 115 us -> 114 us (level)
  local copies, waits for them, and re-layouts: 20 us -> 16.7 us
  other arithmetic: 14.1 us -> 16.9 us
  matrix products: 25.4 us -> 23.6 us
  waiting for transfers between devices: 26.8 us -> 28.1 us
    unnamed x12 -> x36, local copies, waits for them, and re-layouts: 3.13 us -> 6.26 us
    dot_general x1 -> x0, local copies, waits for them, and re-layouts: 2.07 us -> none  [attend(): jnp.einsum('pkgt,pkdt->pkgd', weights.astype(jnp.bfloat16), kv_cache[:, :...]
    dot_general x4 -> x3, matrix products: 4.19 us -> 2.3 us  [the longest x1 1.71 us: attend(): jnp.einsum('ksd,hkdc->shc', normed, weight_parts, preferred_element_type=...]
    another operation x2 -> x1, local copies, waits for them, and re-layouts: 1.89 us -> 0.04 us
    all_to_all x1, waiting for transfers between devices: 4.13 us -> 5.8 us  [shards(): lax.all_to_all(partial.reshape(n_kv, sub_rows, partial.shape[1]), 'kv', s...]
    convert_element_type x0 -> x2, other arithmetic: none -> 1.67 us  [the longest x1 1.66 us: attend(): page_queries = jnp.einsum('sp,skgd->pkgd', belongs.astype(jnp.bfloat16),...]
    reshape x1 -> x0, local copies, waits for them, and re-layouts: 1.18 us -> none  [shards(): tokens = gathered.transpose(1, 0, 2).reshape(local_rows, n_kv * col_width)]
    convert_element_type x2 -> x3, local copies, waits for them, and re-layouts: 2.72 us -> 2.56 us  [the longest x1 1.84 us: attend(): page_queries = jnp.einsum('sp,skgd->pkgd', belongs.astype(jnp.bfloat16),...]
  transfers between devices with their start and end apart: 5 -> 5, of which waited for: 4 -> 4; matrix products, arithmetic and copies ran while one was open for 10% -> 11% of each run, Pallas kernels for 0% -> 0%
where the time goes in v5:
time: 114 us; the launch traced here: 113 us
  waiting for transfers between devices  28.1 us (25%)
  starting transfers between devices  27.3 us (24%)
  matrix products  23.6 us (21%)
  other arithmetic  16.9 us (15%)
  local copies, waits for them, and re-layouts  16.7 us (15%)
    all_to_all x1, waiting for transfers between devices, shards(): lax.all_to_all(outgoing, 'req', split_axis=0, concat_axis=0, tiled=True)  7.68 us
    all_to_all x1, waiting for transfers between devices, shards(): lax.all_to_all(expert_apply(arrived, gate_up, down), 'req', split_axis=0,...  7.62 us
    all_to_all x1, starting transfers between devices, shards(): lax.all_to_all(outgoing, 'req', split_axis=0, concat_axis=0, tiled=True)  7.22 us
    all_to_all x1, starting transfers between devices, shards(): lax.all_to_all(outgoing_rows.reshape(n_req, deal, col_width), 'req', spli...  7.12 us
    all_to_all x1, waiting for transfers between devices, shards(): lax.all_to_all(spread, 'kv', split_axis=0, concat_axis=0, tiled=True)  6.96 us
    unnamed x36, local copies, waits for them, and re-layouts  6.26 us
    all_to_all x1, waiting for transfers between devices, shards(): lax.all_to_all(partial.reshape(n_kv, sub_rows, partial.shape[1]), 'kv', s...  5.8 us
    dot_general x1, matrix products, attend(): jnp.einsum('pkgt,pkdt->pkgd', weights.astype(jnp.bfloat16), kv_cache[:, :...  5.66 us
  transfers between devices with their start and end apart: 5, of which 4 were waited for; matrix products, arithmetic and copies ran while one was open for 11% of the time, Pallas kernels for 0%

profile of v5, /device:TPU:0, one launch (start us, length us, event | category | flops | bytes accessed | tf_op | source)
XLA Modules:
  0.0 112.8 jit_solution(17873501488279285)
XLA Ops:
  0.0 0.8 add_select_fusion.1
  0.8 0.8 fusion.54
  2.4 0.9 convolution_convert_fusion.3
  3.9 7.1 %all-to-all-start = ((bf16[16,4,192]{2,1,0:T(4,128)(2,1)}), bf16[16,4,192]{2,1,0:T(4,128)(2,1)S(1)}, u32[]{:S(2)}, u32[]{:S(2)}) async-start(bf16[16,4,192]{2,1,0:T(4,128)(2,1)} %reshape.319), calls=%async_computation | async-start | bytes 65536 | tf_op jit(solution)/shard_map/all_to_all | solution.py:140
  11.0 0.8 copy.91
  12.6 0.9 fusion.7
  13.5 0.8 select_reduce_fusion
  19.1 0.8 multiply_add_fusion.2
  19.8 2.3 %copy.92 = bf16[1,1536,320]{2,1,0:T(8,128)(2,1)} copy(bf16[1,1536,320]{1,2,0:T(8,128)(2,1)} %param.19) | data formatting | bytes 1966080 | tf_op args[6]
  24.0 5.3 %all-to-all-start.1 = ((bf16[8,64,192]{2,1,0:T(8,128)(2,1)}), bf16[8,64,192]{2,1,0:T(8,128)(2,1)S(1)}, u32[]{:S(2)}, u32[]{:S(2)}) async-start(bf16[8,64,192]{2,1,0:T(8,128)(2,1)} %broadcast_in_dim.84), calls=%async_computation.1 | async-start | bytes 524288 | tf_op jit(solution)/shard_map/all_to_all | solution.py:153
  29.9 7.0 %all-to-all-done.1 = bf16[8,64,192]{2,1,0:T(8,128)(2,1)S(1)} async-done(((bf16[8,64,192]{2,1,0:T(8,128)(2,1)}), bf16[8,64,192]{2,1,0:T(8,128)(2,1)S(1)}, u32[]{:S(2)}, u32[]{:S(2)}) %all-to-all-start.1) | async-done | bytes 196640 | tf_op jit(solution)/shard_map/all_to_all | solution.py:153
  37.0 1.7 %fusion.20 = bf16[64,1,320]{2,0,1:T(8,128)(2,1)S(1)} fusion(bf16[8,192,320]{2,1,0:T(8,128)(2,1)} %bitcast.102, bf16[8,64,192]{2,1,0:T(8,128)(2,1)S(1)} %all-to-all-done.1, f32[8,192]{1,0:T(8,128)S(1)} %mul.149, f32[64]{0:T(128)S(1)} %add_rsqrt_fusion.1), kind=kOutput, calls=%fused_computation.26 | convolution fusion | flops 63328256 | bytes 1227008 | tf_op jit(solution)/shard_map/ksd,hkdc->shc/dot_general | solution.py:26
  39.3 0.9 fusion.45
  41.1 1.7 %convert_element_type.118 = bf16[320,3,64]{0,2,1:T(8,128)(2,1)} convert(f32[320,3,64]{0,2,1:T(8,128)} %bitcast.103) | non-fusion elementwise | flops 61440 | bytes 368640 | tf_op jit(solution)/shard_map/convert_element_type | solution.py:49
  42.7 1.8 %copy.95 = bf16[320,3,64]{2,1,0:T(4,128)(2,1)} copy(bf16[320,3,64]{0,2,1:T(8,128)(2,1)} %convert_element_type.118) | data formatting | bytes 245760 | tf_op jit(solution)/shard_map/convert_element_type | solution.py:49
  44.6 5.6 %fusion.62 = (f32[320,3]{1,0:T(8,128)}, f32[320,3,128]{2,1,0:T(4,128)}) fusion(bf16[320,3,64]{2,1,0:T(4,128)(2,1)} %copy.95, bf16[320,1,128,128]{3,2,0,1:T(8,128)(2,1)} %bitcast.106, pred[320,128]{1,0:T(8,128)(4,1)S(1)} %add_compare_fusion), kind=kOutput, calls=%fused_computation.125 | convolution fusion | flops 16096320 | bytes 6106880 | tf_op jit(solution)/shard_map/pkgd,pkdt->pkgt/dot_general | solution.py:51
  50.2 1.6 %copy.96 = f32[320,3]{0,1:T(4,128)} copy(f32[320,3]{1,0:T(8,128)} %get-tuple-element.13) | data formatting | bytes 7680 | tf_op jit(solution)/shard_map/reduce_max | solution.py:64
  51.8 0.8 select_reduce_fusion.2
  53.4 0.8 copy.97
  54.2 1.9 %fusion.28 = f32[320,3]{1,0:T(8,128)S(1)} fusion(f32[320,3,128]{2,1,0:T(4,128)} %get-tuple-element.14, f32[320,3]{1,0:T(8,128)} %copy.97, pred[320,128]{1,0:T(8,128)(4,1)S(1)} %add_compare_fusion), kind=kLoop, calls=%fused_computation.41 | loop fusion | flops 367680 | bytes 540160 | tf_op jit(solution)/shard_map/reduce_sum | solution.py:75
  56.2 5.7 %fusion.2 = f32[320,3,64]{2,1,0:T(4,128)S(1)} fusion(bf16[320,1,128,128]{3,2,0,1:T(8,128)(2,1)} %bitcast.107, f32[320,3,128]{2,1,0:T(4,128)} %get-tuple-element.14, f32[320,3]{1,0:T(8,128)} %copy.97, pred[320,128]{1,0:T(8,128)(4,1)S(1)} %add_compare_fusion), kind=kOutput, calls=%fused_computation.4 | convolution fusion | flops 16097280 | bytes 6348800 | tf_op jit(solution)/shard_map/pkgt,pkdt->pkgd/dot_general | solution.py:76
  62.6 2.0 %fusion.8 = bf16[8,8,1536]{2,1,0:T(8,128)(2,1)} fusion(bf16[64,192]{0,1:T(8,128)(2,1)S(1)} %bitcast.104, bf16[1,192,1536]{2,1,0:T(8,128)(2,1)} %param.20), kind=kOutput, calls=%fused_computation.14 | convolution fusion | flops 37847040 | bytes 811008 | tf_op jit(solution)/shard_map/dot_general | solution.py:163
  64.6 4.1 %all-to-all-start.2 = ((bf16[8,8,1536]{2,1,0:T(8,128)(2,1)}), bf16[8,8,1536]{2,1,0:T(8,128)(2,1)}, u32[]{:S(2)}, u32[]{:S(2)}) async-start(bf16[8,8,1536]{2,1,0:T(8,128)(2,1)} %fusion.8), calls=%async_computation.2 | async-start | bytes 393216 | tf_op jit(solution)/shard_map/all_to_all | solution.py:164
  69.8 5.8 %all-to-all-done.2 = bf16[8,8,1536]{2,1,0:T(8,128)(2,1)} async-done(((bf16[8,8,1536]{2,1,0:T(8,128)(2,1)}), bf16[8,8,1536]{2,1,0:T(8,128)(2,1)}, u32[]{:S(2)}, u32[]{:S(2)}) %all-to-all-start.2) | async-done | bytes 196640 | tf_op jit(solution)/shard_map/all_to_all | solution.py:164
  75.6 1.0 convert_reduce_fusion
  76.8 0.9 fusion.43
  77.7 0.9 fusion.63
  80.3 7.2 %all-to-all-start.3 = ((bf16[16,2,1,1536]{3,1,2,0:T(2,128)(2,1)}), bf16[16,2,1,1536]{3,1,2,0:T(2,128)(2,1)S(1)}, u32[]{:S(2)}, u32[]{:S(2)}) async-start(bf16[16,2,1,1536]{3,1,2,0:T(2,128)(2,1)} %bitcast.24), calls=%async_computation.3 | async-start | bytes 196608 | tf_op jit(solution)/shard_map/all_to_all | solution.py:198
  87.7 7.7 %all-to-all-done.3 = bf16[16,2,1,1536]{3,1,2,0:T(2,128)(2,1)S(1)} async-done(((bf16[16,2,1,1536]{3,1,2,0:T(2,128)(2,1)}), bf16[16,2,1,1536]{3,1,2,0:T(2,128)(2,1)S(1)}, u32[]{:S(2)}, u32[]{:S(2)}) %all-to-all-start.3) | async-done | bytes 98336 | tf_op jit(solution)/shard_map/all_to_all | solution.py:198
  95.4 4.0 %fusion.9 = f32[1,32,2048]{2,1,0:T(8,128)S(1)} fusion(bf16[32,1536]{1,0:T(8,128)(2,1)S(1)} %reshape.331, bf16[1,1536,2048]{2,1,0:T(8,128)(2,1)} %param.24), kind=kOutput, calls=%fused_computation.15 | convolution fusion | flops 201326592 | bytes 6651904 | tf_op jit(solution)/shard_map/erd,edf->erf/dot_general | solution.py:97
  100.7 3.5 %all-to-all-start.4 = ((bf16[16,2,1,1536]{3,1,2,0:T(2,128)(2,1)}), bf16[16,2,1,1536]{3,1,2,0:T(2,128)(2,1)S(1)}, u32[]{:S(2)}, u32[]{:S(2)}) async-start(bf16[16,2,1,1536]{3,1,2,0:T(2,128)(2,1)} %bitcast.29), calls=%async_computation.4 | async-start | bytes 196608 | tf_op jit(solution)/shard_map/all_to_all | solution.py:199
  104.4 7.6 %all-to-all-done.4 = bf16[16,2,1,1536]{3,1,2,0:T(2,128)(2,1)S(1)} async-done(((bf16[16,2,1,1536]{3,1,2,0:T(2,128)(2,1)}), bf16[16,2,1,1536]{3,1,2,0:T(2,128)(2,1)S(1)}, u32[]{:S(2)}, u32[]{:S(2)}) %all-to-all-start.4) | async-done | bytes 98336 | tf_op jit(solution)/shard_map/all_to_all | solution.py:199
  (99 shorter events, 17.7 us)
Async XLA Ops:
  0.0 99.4 %copy-start = (bf16[1,1024,1536]{2,1,0:T(8,128)(2,1)S(1)}, bf16[1,1024,1536]{2,1,0:T(8,128)(2,1)}, u32[]{:S(2)}) copy-start(bf16[1,1024,1536]{2,1,0:T(8,128)(2,1)} %param.25) | copy-start | bytes 9437188
  3.9 19.1 %all-to-all-start = ((bf16[16,4,192]{2,1,0:T(4,128)(2,1)}), bf16[16,4,192]{2,1,0:T(4,128)(2,1)S(1)}, u32[]{:S(2)}, u32[]{:S(2)}) async-start(bf16[16,4,192]{2,1,0:T(4,128)(2,1)} %reshape.319), calls=%async_computation | async-start | bytes 65536 | tf_op jit(solution)/shard_map/all_to_all | solution.py:140
  16.8 6.2 %copy-start.2 = (s32[8,2]{1,0:T(8,128)}, s32[8,2]{1,0:T(8,128)S(1)}, u32[]{:S(2)}) copy-start(s32[8,2]{1,0:T(8,128)S(1)} %copy.101) | copy-start | bytes 196
  16.9 0.6 copy-start.11
  17.7 0.6 copy-start.14
  24.0 12.9 %all-to-all-start.1 = ((bf16[8,64,192]{2,1,0:T(8,128)(2,1)}), bf16[8,64,192]{2,1,0:T(8,128)(2,1)S(1)}, u32[]{:S(2)}, u32[]{:S(2)}) async-start(bf16[8,64,192]{2,1,0:T(8,128)(2,1)} %broadcast_in_dim.84), calls=%async_computation.1 | async-start | bytes 524288 | tf_op jit(solution)/shard_map/all_to_all | solution.py:153
  44.6 8.1 %copy-start.1 = (f32[64,64]{0,1:T(8,128)S(1)}, f32[64,64]{0,1:T(8,128)}, u32[]{:S(2)}) copy-start(f32[64,64]{0,1:T(8,128)} %copy.120) | copy-start | bytes 49156
  52.6 0.6 copy-start.5
  52.7 0.6 copy-start.7
  56.1 5.7 %copy-start.6 = (f32[64,3]{0,1:T(4,128)S(1)}, f32[64,3]{0,1:T(4,128)}, u32[]{:S(2)}) copy-start(f32[64,3]{0,1:T(4,128)} %copy-done.5) | copy-start | bytes 2308
  56.1 5.7 %copy-start.8 = (f32[64,3]{0,1:T(4,128)S(1)}, f32[64,3]{0,1:T(4,128)}, u32[]{:S(2)}) copy-start(f32[64,3]{0,1:T(4,128)} %copy-done.7) | copy-start | bytes 2308
  56.1 6.0 %copy-start.4 = (f32[64,64]{1,0:T(8,128)S(1)}, f32[64,64]{1,0:T(8,128)}, u32[]{:S(2)}) copy-start(f32[64,64]{1,0:T(8,128)} %get-tuple-element.7) | copy-start | bytes 49156
  56.1 12.6 %copy-start.12 = (s32[16]{0:T(128)S(1)}, s32[16]{0:T(128)}, u32[]{:S(2)}) copy-start(s32[16]{0:T(128)} %copy-done.11) | copy-start | bytes 196
  56.1 12.6 %copy-start.15 = (s32[16]{0:T(128)S(1)}, s32[16]{0:T(128)}, u32[]{:S(2)}) copy-start(s32[16]{0:T(128)} %copy-done.14) | copy-start | bytes 196
  56.1 12.7 %copy-start.13 = (s32[8,2,1]{0,1,2:T(2,128)S(1)}, s32[8,2,1]{0,1,2:T(2,128)}, u32[]{:S(2)}) copy-start(s32[8,2,1]{0,1,2:T(2,128)} %bitcast_or_fusion) | copy-start | bytes 196
  56.1 12.8 %copy-start.9 = (s32[8,2]{1,0:T(8,128)S(1)}, s32[8,2]{1,0:T(8,128)}, u32[]{:S(2)}) copy-start(s32[8,2]{1,0:T(8,128)} %get-tuple-element.9) | copy-start | bytes 196
  56.2 20.6 %copy-start.10 = (f32[1536]{0:T(1024)S(1)}, f32[1536]{0:T(1024)}, u32[]{:S(2)}) copy-start(f32[1536]{0:T(1024)} %param.21) | copy-start | bytes 18436
  64.6 23.0 %copy-start.3 = (s32[8,2]{1,0:T(8,128)S(1)}, s32[8,2]{1,0:T(8,128)}, u32[]{:S(2)}) copy-start(s32[8,2]{1,0:T(8,128)} %copy-done.2) | copy-start | bytes 196
  64.6 11.0 %all-to-all-start.2 = ((bf16[8,8,1536]{2,1,0:T(8,128)(2,1)}), bf16[8,8,1536]{2,1,0:T(8,128)(2,1)}, u32[]{:S(2)}, u32[]{:S(2)}) async-start(bf16[8,8,1536]{2,1,0:T(8,128)(2,1)} %fusion.8), calls=%async_computation.2 | async-start | bytes 393216 | tf_op jit(solution)/shard_map/all_to_all | solution.py:164
  80.3 15.0 %all-to-all-start.3 = ((bf16[16,2,1,1536]{3,1,2,0:T(2,128)(2,1)}), bf16[16,2,1,1536]{3,1,2,0:T(2,128)(2,1)S(1)}, u32[]{:S(2)}, u32[]{:S(2)}) async-start(bf16[16,2,1,1536]{3,1,2,0:T(2,128)(2,1)} %bitcast.24), calls=%async_computation.3 | async-start | bytes 196608 | tf_op jit(solution)/shard_map/all_to_all | solution.py:198
  100.7 11.3 %all-to-all-start.4 = ((bf16[16,2,1,1536]{3,1,2,0:T(2,128)(2,1)}), bf16[16,2,1,1536]{3,1,2,0:T(2,128)(2,1)S(1)}, u32[]{:S(2)}, u32[]{:S(2)}) async-start(bf16[16,2,1,1536]{3,1,2,0:T(2,128)(2,1)} %bitcast.29), calls=%async_computation.4 | async-start | bytes 196608 | tf_op jit(solution)/shard_map/all_to_all | solution.py:199

commit v6 on v5

--- a/solution.py
+++ b/solution.py
@@ -19,13 +19,10 @@
 def attend(normed, seq_lens, page_table, kv_cache, qkv_weight):
     pool_pages, local_heads, twice_hd, page_len = kv_cache.shape
     head_dim = twice_hd // 2
-    kv_parts, slot_count, part_width = normed.shape
+    slot_count = normed.shape[0]
     groups = qkv_weight.shape[2] // head_dim - 2
     max_pages = page_table.shape[1]
-    weight_parts = qkv_weight.reshape(local_heads, kv_parts, part_width, qkv_weight.shape[2])
-    projected = jnp.einsum(
-        "ksd,hkdc->shc", normed, weight_parts, preferred_element_type=jnp.float32
-    )
+    projected = jnp.einsum("sd,hdc->shc", normed, qkv_weight, preferred_element_type=jnp.float32)
     queries = (
         projected[:, :, : groups * head_dim]
         .reshape(slot_count, local_heads, groups, head_dim)
@@ -37,10 +34,30 @@
     page_ids = jnp.arange(max_pages, dtype=jnp.int32)
     in_use = page_ids[None, :] < page_need[:, None]
     pool_ids = jnp.arange(pool_pages, dtype=jnp.int32)
-    match = (page_table[:, :, None] == pool_ids[None, None, :]) & in_use[:, :, None]
-    belongs = jnp.any(match, axis=1)
-    page_order = jnp.sum(jnp.where(match, page_ids[None, :, None], 0), axis=(0, 1))
-    owner_len = jnp.sum(jnp.where(belongs, seq_lens[:, None], 0), axis=0)
+    entry_slot = jnp.broadcast_to(
+        jnp.arange(slot_count, dtype=jnp.int32)[:, None], (slot_count, max_pages)
+    ).reshape(-1)
+    entry_page = jnp.where(in_use, page_table, -1).reshape(-1)
+    entry_order = jnp.broadcast_to(page_ids[None, :], (slot_count, max_pages)).reshape(-1)
+    entry_len = jnp.broadcast_to(seq_lens[:, None], (slot_count, max_pages)).reshape(-1)
+    len_unit = 64
+    facts = jnp.concatenate(
+        [
+            (entry_slot[None, :] == jnp.arange(slot_count, dtype=jnp.int32)[:, None]).astype(jnp.float32),
+            entry_order[None, :].astype(jnp.float32),
+            (entry_len // len_unit)[None, :].astype(jnp.float32),
+            (entry_len % len_unit)[None, :].astype(jnp.float32),
+        ],
+        axis=0,
+    ).astype(jnp.bfloat16)
+    entry_hit = (entry_page[:, None] == pool_ids[None, :]).astype(jnp.bfloat16)
+    page_facts = jnp.dot(facts, entry_hit, preferred_element_type=jnp.float32)
+    belongs = page_facts[:slot_count] > 0.5
+    page_order = page_facts[slot_count].astype(jnp.int32)
+    owner_len = (
+        page_facts[slot_count + 1].astype(jnp.int32) * len_unit
+        + page_facts[slot_count + 2].astype(jnp.int32)
+    )
     position = page_order[:, None] * page_len + jnp.arange(page_len, dtype=jnp.int32)[None, :]
     live = position < owner_len[:, None]
     scale_factor = head_dim ** (-0.5)
@@ -149,13 +166,11 @@
     picked_rows = jnp.dot(take_pick, arrived_rows, preferred_element_type=jnp.float32).astype(
         hidden.dtype
     )
-    spread = jnp.broadcast_to(picked_rows[None], (n_kv, local_rows, col_width))
-    gathered = lax.all_to_all(spread, "kv", split_axis=0, concat_axis=0, tiled=True)
-    gathered_f = gathered.astype(jnp.float32)
-    norm_factor = lax.rsqrt(
-        jnp.sum(gathered_f * gathered_f, axis=(0, 2), keepdims=True) / (n_kv * col_width) + EPS_NORM
-    )
-    normed = (gathered_f * norm_factor * attn_gain.reshape(n_kv, 1, col_width)).astype(jnp.bfloat16)
+    spread = jnp.broadcast_to(picked_rows[:, None], (local_rows, n_kv, col_width))
+    tokens = lax.all_to_all(spread, "kv", split_axis=1, concat_axis=1, tiled=True).reshape(
+        local_rows, n_kv * col_width
+    )
+    normed = rms_norm(tokens, attn_gain)
     head_out = attend(normed, seq_lens, page_table, kv_cache, qkv_weight)
     sub_rows = routes.shape[0]
     width = n_kv * col_width
@@ -165,8 +180,7 @@
         partial.reshape(n_kv, sub_rows, partial.shape[1]), "kv", split_axis=0, concat_axis=0, tiled=True
     )
     attn_rows = jnp.sum(partial_parts.astype(jnp.float32), axis=0)
-    own_tokens = lax.dynamic_slice_in_dim(gathered, kv_index * sub_rows, sub_rows, 1)
-    own_tokens = own_tokens.transpose(1, 0, 2).reshape(sub_rows, width)
+    own_tokens = lax.dynamic_slice_in_dim(tokens, kv_index * sub_rows, sub_rows, 0)
     residual = (own_tokens.astype(jnp.float32) + attn_rows).astype(jnp.bfloat16)
     normed_ffn = rms_norm(residual, ffn_gain)
     logits = jnp.dot(normed_ffn, router, preferred_element_type=jnp.float32)

time: 114 us -> 113 us (level)
  local copies, waits for them, and re-layouts: 16.7 us -> 19.8 us
  other arithmetic: 16.9 us -> 14.5 us
  waiting for transfers between devices: 28.1 us -> 26.2 us
    unnamed x36 -> x18, local copies, waits for them, and re-layouts: 6.26 us -> 2.16 us
    convert_element_type x2 -> x3, local copies, waits for them, and re-layouts: 0.72 us -> 2.8 us  [the longest x2 2.72 us: rms_norm(): return (values * factor * gain_vec).astype(jnp.bfloat16)]
    reduce_sum x3 -> x0, other arithmetic: 1.76 us -> none  [the longest x1 0.85 us: attend(): jnp.sum(jnp.where(match, page_ids[None, :, None], 0), axis=(0, 1))]
    all_to_all x1, waiting for transfers between devices: 5.8 us -> 4.13 us  [shards(): lax.all_to_all(partial.reshape(n_kv, sub_rows, partial.shape[1]), 'kv', s...]
    slice x2, local copies, waits for them, and re-layouts: 0.11 us -> 1.47 us  [attend(): projected[:, :, :groups * head_dim]]
    reshape x0 -> x2, local copies, waits for them, and re-layouts: none -> 1.27 us  [the longest x1 1.18 us: shards(): lax.all_to_all(spread, 'kv', split_axis=1, concat_axis=1, tiled=True)]
    dot_general x1 -> x2, matrix products: 1.71 us -> 2.57 us  [the longest x1 1.73 us: attend(): jnp.einsum('sd,hdc->shc', normed, qkv_weight, preferred_element_type=jnp....]
where the time goes in v6:
time: 113 us; the launch traced here: 112 us
  starting transfers between devices  27.2 us (24%)
  waiting for transfers between devices  26.2 us (23%)
  matrix products  23.6 us (21%)
  local copies, waits for them, and re-layouts  19.8 us (18%)
  other arithmetic  14.5 us (13%)
    all_to_all x1, waiting for transfers between devices, shards(): lax.all_to_all(outgoing, 'req', split_axis=0, concat_axis=0, tiled=True)  7.69 us
    all_to_all x1, waiting for transfers between devices, shards(): lax.all_to_all(expert_apply(arrived, gate_up, down), 'req', split_axis=0,...  7.62 us
    all_to_all x1, starting transfers between devices, shards(): lax.all_to_all(outgoing, 'req', split_axis=0, concat_axis=0, tiled=True)  7.22 us
    all_to_all x1, starting transfers between devices, shards(): lax.all_to_all(outgoing_rows.reshape(n_req, deal, col_width), 'req', spli...  7.12 us
    all_to_all x1, waiting for transfers between devices, shards(): lax.all_to_all(spread, 'kv', split_axis=1, concat_axis=1, tiled=True)  6.78 us
    dot_general x1, matrix products, attend(): jnp.einsum('pkgt,pkdt->pkgd', weights.astype(jnp.bfloat16), kv_cache[:, :...  5.67 us
    dot_general x1, matrix products, attend(): jnp.einsum('pkgd,pkdt->pkgt', page_queries, kv_cache[:, :, :head_dim, :],...  5.62 us
    all_to_all x1, starting transfers between devices, shards(): lax.all_to_all(spread, 'kv', split_axis=1, concat_axis=1, tiled=True)  5.31 us
  transfers between devices with their start and end apart: 5, of which 4 were waited for; matrix products, arithmetic and copies ran while one was open for 11% of the time, Pallas kernels for 0%

profile of v6, /device:TPU:0, one launch (start us, length us, event | category | flops | bytes accessed | tf_op | source)
XLA Modules:
  0.0 111.6 jit_solution(7799450541351599082)
XLA Ops:
  0.0 0.8 add_select_fusion.1
  0.8 0.8 fusion.61
  2.4 0.9 convolution_convert_fusion.4
  3.9 7.1 %all-to-all-start = ((bf16[16,4,192]{2,1,0:T(4,128)(2,1)}), bf16[16,4,192]{2,1,0:T(4,128)(2,1)S(1)}, u32[]{:S(2)}, u32[]{:S(2)}) async-start(bf16[16,4,192]{2,1,0:T(4,128)(2,1)} %reshape.457), calls=%async_computation | async-start | bytes 65536 | tf_op jit(solution)/shard_map/all_to_all | solution.py:157
  15.5 0.8 fusion.6
  18.3 0.8 fusion.70
  21.7 5.3 %all-to-all-start.1 = ((bf16[64,8,192]{2,0,1:T(8,128)(2,1)}), bf16[64,8,192]{2,0,1:T(8,128)(2,1)S(1)}, u32[]{:S(2)}, u32[]{:S(2)}) async-start(bf16[64,8,192]{2,0,1:T(8,128)(2,1)} %broadcast_in_dim.65), calls=%async_computation.1 | async-start | bytes 524288 | tf_op jit(solution)/shard_map/all_to_all | solution.py:170
  27.7 6.8 %all-to-all-done.1 = bf16[64,8,192]{2,0,1:T(8,128)(2,1)S(1)} async-done(((bf16[64,8,192]{2,0,1:T(8,128)(2,1)}), bf16[64,8,192]{2,0,1:T(8,128)(2,1)S(1)}, u32[]{:S(2)}, u32[]{:S(2)}) %all-to-all-start.1) | async-done | bytes 196640 | tf_op jit(solution)/shard_map/all_to_all | solution.py:170
  34.8 0.8 copy.102
  35.7 1.9 %convert_element_type.177 = bf16[64,1536]{1,0:T(8,128)(2,1)} reshape(bf16[64,8,192]{2,1,0:T(8,128)(2,1)} %copy.102) | data formatting | bytes 393216 | tf_op jit(solution)/shard_map/convert_element_type | solution.py:16
  37.5 1.7 %fusion.19 = bf16[64,1,320]{2,0,1:T(8,128)(2,1)S(1)} fusion(bf16[64,1536]{1,0:T(8,128)(2,1)} %convert_element_type.177, bf16[1,1536,320]{1,2,0:T(8,128)(2,1)} %param.19), kind=kOutput, calls=%fused_computation.24 | convolution fusion | flops 62935040 | bytes 1220608 | tf_op jit(solution)/shard_map/sd,hdc->shc/dot_general | solution.py:25
  41.2 0.9 copy.103
  43.0 1.8 %copy.105 = bf16[320,3,64]{2,1,0:T(4,128)(2,1)} copy(bf16[320,3,64]{0,2,1:T(8,128)(2,1)} %convert_element_type.179) | data formatting | bytes 245760 | tf_op jit(solution)/shard_map/convert_element_type | solution.py:66
  44.8 5.6 %fusion.75 = (f32[320,3]{1,0:T(8,128)}, f32[320,3,128]{2,1,0:T(4,128)}) fusion(bf16[320,3,64]{2,1,0:T(4,128)(2,1)} %copy.105, bf16[320,1,128,128]{3,2,0,1:T(8,128)(2,1)} %bitcast.97, pred[320,128]{1,0:T(8,128)(4,1)} %add_compare_fusion), kind=kOutput, calls=%fused_computation.147 | convolution fusion | flops 16096320 | bytes 6106880 | tf_op jit(solution)/shard_map/pkgd,pkdt->pkgt/dot_general | solution.py:68
  50.5 1.0 copy.106
  51.6 0.8 multiply_reduce_fusion
  52.5 0.8 copy.107
  53.3 1.9 %fusion.28 = f32[320,3]{1,0:T(8,128)S(1)} fusion(f32[320,3,128]{2,1,0:T(4,128)} %get-tuple-element.18, f32[320,3]{1,0:T(8,128)} %copy.107, pred[320,128]{1,0:T(8,128)(4,1)S(1)} %copy-done.1), kind=kLoop, calls=%fused_computation.42 | loop fusion | flops 367680 | bytes 540160 | tf_op jit(solution)/shard_map/reduce_sum | solution.py:92
  55.3 5.7 %fusion.2 = f32[320,3,64]{2,1,0:T(4,128)S(1)} fusion(bf16[320,1,128,128]{3,2,0,1:T(8,128)(2,1)} %bitcast.98, f32[320,3,128]{2,1,0:T(4,128)} %get-tuple-element.18, f32[320,3]{1,0:T(8,128)} %copy.107, pred[320,128]{1,0:T(8,128)(4,1)S(1)} %copy-done.1), kind=kOutput, calls=%fused_computation.4 | convolution fusion | flops 16097280 | bytes 6348800 | tf_op jit(solution)/shard_map/pkgt,pkdt->pkgd/dot_general | solution.py:93
  61.3 1.0 fusion.17
  62.2 0.9 copy.110
  63.1 2.0 %fusion.7 = bf16[8,8,1536]{2,1,0:T(8,128)(2,1)} fusion(bf16[64,192]{0,1:T(8,128)(2,1)S(1)} %bitcast.95, bf16[1,192,1536]{2,1,0:T(8,128)(2,1)} %param.20), kind=kOutput, calls=%fused_computation.12 | convolution fusion | flops 37847040 | bytes 811008 | tf_op jit(solution)/shard_map/dot_general | solution.py:178
  65.1 4.0 %all-to-all-start.2 = ((bf16[8,8,1536]{2,1,0:T(8,128)(2,1)}), bf16[8,8,1536]{2,1,0:T(8,128)(2,1)}, u32[]{:S(2)}, u32[]{:S(2)}) async-start(bf16[8,8,1536]{2,1,0:T(8,128)(2,1)} %fusion.7), calls=%async_computation.2 | async-start | bytes 393216 | tf_op jit(solution)/shard_map/all_to_all | solution.py:179
  69.8 0.8 copy.100
  70.6 1.2 %reshape.459 = bf16[64,1536]{1,0:T(8,128)(2,1)S(1)} reshape(bf16[64,8,192]{2,1,0:T(8,128)(2,1)} %copy.100) | data formatting | bytes 393216 | tf_op jit(solution)/shard_map/reshape | solution.py:170
  71.8 4.1 %all-to-all-done.2 = bf16[8,8,1536]{2,1,0:T(8,128)(2,1)} async-done(((bf16[8,8,1536]{2,1,0:T(8,128)(2,1)}), bf16[8,8,1536]{2,1,0:T(8,128)(2,1)}, u32[]{:S(2)}, u32[]{:S(2)}) %all-to-all-start.2) | async-done | bytes 196640 | tf_op jit(solution)/shard_map/all_to_all | solution.py:179
  76.0 1.0 convert_reduce_fusion
  79.0 7.2 %all-to-all-start.3 = ((bf16[16,2,1,1536]{3,1,2,0:T(2,128)(2,1)}), bf16[16,2,1,1536]{3,1,2,0:T(2,128)(2,1)S(1)}, u32[]{:S(2)}, u32[]{:S(2)}) async-start(bf16[16,2,1,1536]{3,1,2,0:T(2,128)(2,1)} %bitcast.22), calls=%async_computation.3 | async-start | bytes 196608 | tf_op jit(solution)/shard_map/all_to_all | solution.py:212
  86.4 7.7 %all-to-all-done.3 = bf16[16,2,1,1536]{3,1,2,0:T(2,128)(2,1)S(1)} async-done(((bf16[16,2,1,1536]{3,1,2,0:T(2,128)(2,1)}), bf16[16,2,1,1536]{3,1,2,0:T(2,128)(2,1)S(1)}, u32[]{:S(2)}, u32[]{:S(2)}) %all-to-all-start.3) | async-done | bytes 98336 | tf_op jit(solution)/shard_map/all_to_all | solution.py:212
  94.1 4.0 %fusion.8 = f32[1,32,2048]{2,1,0:T(8,128)S(1)} fusion(bf16[32,1536]{1,0:T(8,128)(2,1)S(1)} %reshape.471, bf16[1,1536,2048]{2,1,0:T(8,128)(2,1)} %param.24), kind=kOutput, calls=%fused_computation.13 | convolution fusion | flops 201326592 | bytes 6651904 | tf_op jit(solution)/shard_map/erd,edf->erf/dot_general | solution.py:114
  99.4 3.5 %all-to-all-start.4 = ((bf16[16,2,1,1536]{3,1,2,0:T(2,128)(2,1)}), bf16[16,2,1,1536]{3,1,2,0:T(2,128)(2,1)S(1)}, u32[]{:S(2)}, u32[]{:S(2)}) async-start(bf16[16,2,1,1536]{3,1,2,0:T(2,128)(2,1)} %bitcast.27), calls=%async_computation.4 | async-start | bytes 196608 | tf_op jit(solution)/shard_map/all_to_all | solution.py:213
  103.1 7.6 %all-to-all-done.4 = bf16[16,2,1,1536]{3,1,2,0:T(2,128)(2,1)S(1)} async-done(((bf16[16,2,1,1536]{3,1,2,0:T(2,128)(2,1)}), bf16[16,2,1,1536]{3,1,2,0:T(2,128)(2,1)S(1)}, u32[]{:S(2)}, u32[]{:S(2)}) %all-to-all-start.4) | async-done | bytes 98336 | tf_op jit(solution)/shard_map/all_to_all | solution.py:213
  (92 shorter events, 19.9 us)
Async XLA Ops:
  0.0 98.1 %copy-start = (bf16[1,1024,1536]{2,1,0:T(8,128)(2,1)S(1)}, bf16[1,1024,1536]{2,1,0:T(8,128)(2,1)}, u32[]{:S(2)}) copy-start(bf16[1,1024,1536]{2,1,0:T(8,128)(2,1)} %param.25) | copy-start | bytes 9437188
  3.9 16.8 %all-to-all-start = ((bf16[16,4,192]{2,1,0:T(4,128)(2,1)}), bf16[16,4,192]{2,1,0:T(4,128)(2,1)S(1)}, u32[]{:S(2)}, u32[]{:S(2)}) async-start(bf16[16,4,192]{2,1,0:T(4,128)(2,1)} %reshape.457), calls=%async_computation | async-start | bytes 65536 | tf_op jit(solution)/shard_map/all_to_all | solution.py:157
  16.3 0.6 copy-start.2
  18.1 22.4 %copy-start.6 = (s32[16]{0:T(128)}, s32[16]{0:T(128)S(1)}, u32[]{:S(2)}) copy-start(s32[16]{0:T(128)S(1)} %select_reduce_fusion.2) | copy-start | bytes 196
  21.7 12.9 %all-to-all-start.1 = ((bf16[64,8,192]{2,0,1:T(8,128)(2,1)}), bf16[64,8,192]{2,0,1:T(8,128)(2,1)S(1)}, u32[]{:S(2)}, u32[]{:S(2)}) async-start(bf16[64,8,192]{2,0,1:T(8,128)(2,1)} %broadcast_in_dim.65), calls=%async_computation.1 | async-start | bytes 524288 | tf_op jit(solution)/shard_map/all_to_all | solution.py:170
  42.3 11.0 %copy-start.1 = (pred[320,128]{1,0:T(8,128)(4,1)S(1)}, pred[320,128]{1,0:T(8,128)(4,1)}, u32[]{:S(2)}) copy-start(pred[320,128]{1,0:T(8,128)(4,1)} %add_compare_fusion) | copy-start | bytes 122884
  53.3 7.9 %copy-start.4 = (f32[64,64]{1,0:T(8,128)S(1)}, f32[64,64]{1,0:T(8,128)}, u32[]{:S(2)}) copy-start(f32[64,64]{1,0:T(8,128)} %get-tuple-element.11) | copy-start | bytes 49156
  55.2 21.8 %copy-start.5 = (f32[1536]{0:T(1024)S(1)}, f32[1536]{0:T(1024)}, u32[]{:S(2)}) copy-start(f32[1536]{0:T(1024)} %param.21) | copy-start | bytes 18436
  55.3 21.9 %copy-start.3 = (bf16[1536,16]{0,1:T(8,128)(2,1)S(1)}, bf16[1536,16]{0,1:T(8,128)(2,1)}, u32[]{:S(2)}) copy-start(bf16[1536,16]{0,1:T(8,128)(2,1)} %param.22) | copy-start | bytes 147460
  65.1 10.9 %all-to-all-start.2 = ((bf16[8,8,1536]{2,1,0:T(8,128)(2,1)}), bf16[8,8,1536]{2,1,0:T(8,128)(2,1)}, u32[]{:S(2)}, u32[]{:S(2)}) async-start(bf16[8,8,1536]{2,1,0:T(8,128)(2,1)} %fusion.7), calls=%async_computation.2 | async-start | bytes 393216 | tf_op jit(solution)/shard_map/all_to_all | solution.py:179
  79.0 15.0 %all-to-all-start.3 = ((bf16[16,2,1,1536]{3,1,2,0:T(2,128)(2,1)}), bf16[16,2,1,1536]{3,1,2,0:T(2,128)(2,1)S(1)}, u32[]{:S(2)}, u32[]{:S(2)}) async-start(bf16[16,2,1,1536]{3,1,2,0:T(2,128)(2,1)} %bitcast.22), calls=%async_computation.3 | async-start | bytes 196608 | tf_op jit(solution)/shard_map/all_to_all | solution.py:212
  94.1 16.6 %copy-start.7 = (s32[8,2]{0,1:T(2,128)S(1)}, s32[8,2]{0,1:T(2,128)}, u32[]{:S(2)}) copy-start(s32[8,2]{0,1:T(2,128)} %copy.119) | copy-start | bytes 196
  99.4 11.3 %all-to-all-start.4 = ((bf16[16,2,1,1536]{3,1,2,0:T(2,128)(2,1)}), bf16[16,2,1,1536]{3,1,2,0:T(2,128)(2,1)S(1)}, u32[]{:S(2)}, u32[]{:S(2)}) async-start(bf16[16,2,1,1536]{3,1,2,0:T(2,128)(2,1)} %bitcast.27), calls=%async_computation.4 | async-start | bytes 196608 | tf_op jit(solution)/shard_map/all_to_all | solution.py:213

commit v7 on v6

--- a/solution.py
+++ b/solution.py
@@ -2,6 +2,9 @@
 import jax.numpy as jnp
 from jax import lax
 from jax.sharding import PartitionSpec as P
+from jax.experimental import pallas as pl
+from jax.experimental.pallas import tpu as pltpu
+import functools
 
 REQ_DEV = 64
 
@@ -14,6 +17,101 @@
     values = values.astype(jnp.float32)
     factor = lax.rsqrt(jnp.mean(values * values, axis=-1, keepdims=True) + EPS_NORM)
     return (values * factor * gain_vec).astype(jnp.bfloat16)
+
+
+def paged_attention_kernel(
+    scale, head_dim, block_pages, owner_ref, q_ref, live_ref, kv_ref, knew_ref, vnew_ref,
+    out_ref, page_q, page_peak, page_sum, page_acc, slot_peak, slot_sum, slot_acc,
+):
+    step = pl.program_id(0)
+    base = step * block_pages
+
+    @pl.when(step == 0)
+    def _():
+        slot_peak[...] = jnp.full(slot_peak.shape, NEG_FILL, jnp.float32)
+        slot_sum[...] = jnp.zeros(slot_sum.shape, jnp.float32)
+        slot_acc[...] = jnp.zeros(slot_acc.shape, jnp.float32)
+
+    def gather_one(p, carry):
+        page_q[p] = q_ref[owner_ref[base + p]]
+        return carry
+
+    lax.fori_loop(0, block_pages, gather_one, 0)
+    keys = kv_ref[:, 0, :head_dim, :]
+    values = kv_ref[:, 0, head_dim:, :]
+    token_ids = lax.broadcasted_iota(jnp.int32, (1, 1, keys.shape[2]), 2)
+    live = token_ids < live_ref[...]
+    scores = jnp.einsum(
+        "pgd,pdt->pgt", page_q[...], keys, preferred_element_type=jnp.float32
+    ) * scale
+    scores = jnp.where(live, scores, NEG_FILL)
+    peak = jnp.max(scores, axis=2, keepdims=True)
+    weights = jnp.where(live, jnp.exp(scores - peak), 0.0)
+    page_peak[...] = peak
+    page_sum[...] = jnp.sum(weights, axis=2, keepdims=True)
+    page_acc[...] = jnp.einsum(
+        "pgt,pdt->pgd", weights.astype(values.dtype), values, preferred_element_type=jnp.float32
+    )
+
+    def fold_one(p, carry):
+        owner = owner_ref[base + p]
+        old_peak = slot_peak[owner]
+        this_peak = page_peak[p]
+        new_peak = jnp.maximum(old_peak, this_peak)
+        keep = jnp.exp(old_peak - new_peak)
+        add = jnp.exp(this_peak - new_peak)
+        slot_sum[owner] = keep * slot_sum[owner] + add * page_sum[p]
+        slot_acc[owner] = keep * slot_acc[owner] + add * page_acc[p]
+        slot_peak[owner] = new_peak
+        return carry
+
+    lax.fori_loop(0, block_pages, fold_one, 0)
+
+    @pl.when(step == pl.num_programs(0) - 1)
+    def _():
+        queries = q_ref[...].astype(jnp.float32)
+        score_new = jnp.sum(queries * knew_ref[...].astype(jnp.float32), axis=2, keepdims=True) * scale
+        peak_all = jnp.maximum(slot_peak[...], score_new)
+        keep = jnp.exp(slot_peak[...] - peak_all)
+        weight_new = jnp.exp(score_new - peak_all)
+        total = slot_sum[...] * keep + weight_new
+        rounded_new = weight_new.astype(jnp.bfloat16).astype(jnp.float32)
+        value = slot_acc[...] * keep + rounded_new * vnew_ref[...].astype(jnp.float32)
+        out_ref[...] = value / total
+
+
+def paged_attention(owner, queries, live_len, kv_cache, key_new, value_new, block_pages=32):
+    slot_count, rows, head_dim = queries.shape
+    pool_pages = kv_cache.shape[0]
+    page_len = kv_cache.shape[3]
+    kernel = functools.partial(paged_attention_kernel, head_dim ** (-0.5), head_dim, block_pages)
+    grid_spec = pltpu.PrefetchScalarGridSpec(
+        num_scalar_prefetch=1,
+        grid=(pool_pages // block_pages,),
+        in_specs=[
+            pl.BlockSpec((slot_count, rows, head_dim), lambda i, own: (0, 0, 0)),
+            pl.BlockSpec((block_pages, 1, 1), lambda i, own: (i, 0, 0)),
+            pl.BlockSpec((block_pages, 1, 2 * head_dim, page_len), lambda i, own: (i, 0, 0, 0)),
+            pl.BlockSpec((slot_count, 1, head_dim), lambda i, own: (0, 0, 0)),
+            pl.BlockSpec((slot_count, 1, head_dim), lambda i, own: (0, 0, 0)),
+        ],
+        out_specs=pl.BlockSpec((slot_count, rows, head_dim), lambda i, own: (0, 0, 0)),
+        scratch_shapes=[
+            pltpu.VMEM((block_pages, rows, head_dim), queries.dtype),
+            pltpu.VMEM((block_pages, rows, 1), jnp.float32),
+            pltpu.VMEM((block_pages, rows, 1), jnp.float32),
+            pltpu.VMEM((block_pages, rows, head_dim), jnp.float32),
+            pltpu.VMEM((slot_count, rows, 1), jnp.float32),
+            pltpu.VMEM((slot_count, rows, 1), jnp.float32),
+            pltpu.VMEM((slot_count, rows, head_dim), jnp.float32),
+        ],
+    )
+    return pl.pallas_call(
+        kernel,
+        grid_spec=grid_spec,
+        out_shape=jax.ShapeDtypeStruct((slot_count, rows, head_dim), jnp.float32),
+        compiler_params=pltpu.CompilerParams(dimension_semantics=("arbitrary",)),
+    )(owner, queries, live_len, kv_cache, key_new, value_new)
 
 
 def attend(normed, seq_lens, page_table, kv_cache, qkv_weight):
@@ -43,7 +141,7 @@
     len_unit = 64
     facts = jnp.concatenate(
         [
-            (entry_slot[None, :] == jnp.arange(slot_count, dtype=jnp.int32)[:, None]).astype(jnp.float32),
+            entry_slot[None, :].astype(jnp.float32),
             entry_order[None, :].astype(jnp.float32),
             (entry_len // len_unit)[None, :].astype(jnp.float32),
             (entry_len % len_unit)[None, :].astype(jnp.float32),
@@ -52,60 +150,16 @@
     ).astype(jnp.bfloat16)
     entry_hit = (entry_page[:, None] == pool_ids[None, :]).astype(jnp.bfloat16)
     page_facts = jnp.dot(facts, entry_hit, preferred_element_type=jnp.float32)
-    belongs = page_facts[:slot_count] > 0.5
-    page_order = page_facts[slot_count].astype(jnp.int32)
-    owner_len = (
-        page_facts[slot_count + 1].astype(jnp.int32) * len_unit
-        + page_facts[slot_count + 2].astype(jnp.int32)
-    )
-    position = page_order[:, None] * page_len + jnp.arange(page_len, dtype=jnp.int32)[None, :]
-    live = position < owner_len[:, None]
-    scale_factor = head_dim ** (-0.5)
-    page_queries = jnp.einsum(
-        "sp,skgd->pkgd", belongs.astype(jnp.bfloat16), queries, preferred_element_type=jnp.float32
-    ).astype(jnp.bfloat16)
-    scores = (
-        jnp.einsum(
-            "pkgd,pkdt->pkgt",
-            page_queries,
-            kv_cache[:, :, :head_dim, :],
-            preferred_element_type=jnp.float32,
-        )
-        * scale_factor
-    )
-    scores = jnp.where(live[:, None, None, :], scores, NEG_FILL)
-    score_new = (
-        jnp.einsum("skgd,skd->skg", queries, key_new, preferred_element_type=jnp.float32)
-        * scale_factor
-    )
-    page_peak = jnp.max(scores, axis=3)
-    slot_peak = jnp.max(jnp.where(belongs[:, :, None, None], page_peak[None], NEG_FILL), axis=1)
-    slot_peak = jnp.maximum(slot_peak, score_new)
-    page_peak_of_owner = jnp.max(
-        jnp.where(belongs[:, :, None, None], slot_peak[:, None], NEG_FILL), axis=0
-    )
-    weights = jnp.where(
-        live[:, None, None, :],
-        jnp.exp(scores - page_peak_of_owner[..., None]),
-        0.0,
-    )
-    page_total = jnp.sum(weights, axis=3)
-    page_value = jnp.einsum(
-        "pkgt,pkdt->pkgd",
-        weights.astype(jnp.bfloat16),
-        kv_cache[:, :, head_dim:, :],
-        preferred_element_type=jnp.float32,
-    )
-    belongs_f = belongs.astype(jnp.float32)
-    total_sum = jnp.einsum("sp,pkg->skg", belongs_f, page_total, precision=lax.Precision.HIGHEST)
-    value_sum = jnp.einsum(
-        "sp,pkgd->skgd", belongs_f, page_value, precision=lax.Precision.HIGHEST
-    )
-    weight_new = jnp.exp(score_new - slot_peak)
-    total_sum = total_sum + weight_new
-    rounded_new = lax.optimization_barrier(weight_new.astype(jnp.bfloat16)).astype(jnp.float32)
-    value_sum = value_sum + rounded_new[..., None] * value_new.astype(jnp.float32)[:, :, None, :]
-    return (value_sum / total_sum[..., None]).astype(jnp.bfloat16).reshape(slot_count, -1)
+    owner = page_facts[0].astype(jnp.int32)
+    page_order = page_facts[1].astype(jnp.int32)
+    owner_len = page_facts[2].astype(jnp.int32) * len_unit + page_facts[3].astype(jnp.int32)
+    live_len = jnp.clip(owner_len - page_order * page_len, 0, page_len).reshape(pool_pages, 1, 1)
+    row_pad = 8
+    padded_queries = jnp.pad(
+        queries.reshape(slot_count, groups, head_dim), ((0, 0), (0, row_pad - groups), (0, 0))
+    )
+    head_out = paged_attention(owner, padded_queries, live_len, kv_cache, key_new, value_new)
+    return head_out[:, :groups, :].astype(jnp.bfloat16).reshape(slot_count, -1)
 
 
 def expert_apply(piece, gate_up, down):

time: 113 us -> 132 us (1.17)
  Pallas kernels: 0 us -> 40.1 us
  matrix products: 23.6 us -> 11.5 us
  other arithmetic: 14.5 us -> 8.58 us
  local copies, waits for them, and re-layouts: 19.8 us -> 16 us
    pallas_call x0 -> x1, Pallas kernels: none -> 40.1 us  [paged_attention(): pl.pallas_call(kernel, grid_spec=grid_spec, out_shape=jax.ShapeDtypeStruc...]
    dot_general x4 -> x0, matrix products: 12.5 us -> none  [the longest x1 5.67 us: attend(): jnp.einsum('pkgt,pkdt->pkgd', weights.astype(jnp.bfloat16), kv_cache[:, :...]
    convert_element_type x2, local copies, waits for them, and re-layouts: 2.73 us -> 0.21 us  [the longest x1 0.12 us: attend(): queries = projected[:, :, :groups * head_dim].reshape(slot_count, local_h...]
    reduce_sum x1 -> x0, other arithmetic: 1.9 us -> none  [attend(): page_total = jnp.sum(weights, axis=3)]
    reduce_max x2 -> x0, local copies, waits for them, and re-layouts: 1.81 us -> none  [the longest x1 1 us: attend(): page_peak = jnp.max(scores, axis=3)]
    mul x3 -> x0, other arithmetic: 1.46 us -> none  [the longest x1 0.85 us: attend(): page_order[:, None] * page_len]
    slice x2, local copies, waits for them, and re-layouts: 1.47 us -> 0.11 us  [attend(): projected[:, :, :groups * head_dim]]
  transfers between devices with their start and end apart: 5 -> 5, of which waited for: 4 -> 4; matrix products, arithmetic and copies ran while one was open for 11% -> 9% of each run, Pallas kernels for 0% -> 0%
where the time goes in v7:
time: 132 us; the launch traced here: 131 us
  Pallas kernels  40.1 us (30%)
  waiting for transfers between devices  27.4 us (21%)
  starting transfers between devices  27.2 us (21%)
  local copies, waits for them, and re-layouts  16 us (12%)
  matrix products  11.5 us (9%)
  other arithmetic  8.58 us (6%)
    pallas_call x1, Pallas kernels, paged_attention(): pl.pallas_call(kernel, grid_spec=grid_spec, out_shape=jax.ShapeDtypeStruc...  40.1 us
    all_to_all x1, waiting for transfers between devices, shards(): lax.all_to_all(outgoing, 'req', split_axis=0, concat_axis=0, tiled=True)  7.69 us
    all_to_all x1, waiting for transfers between devices, shards(): lax.all_to_all(expert_apply(arrived, gate_up, down), 'req', split_axis=0,...  7.62 us
    all_to_all x1, waiting for transfers between devices, shards(): lax.all_to_all(spread, 'kv', split_axis=1, concat_axis=1, tiled=True)  7.28 us
    all_to_all x1, starting transfers between devices, shards(): lax.all_to_all(outgoing, 'req', split_axis=0, concat_axis=0, tiled=True)  7.21 us
    all_to_all x1, starting transfers between devices, shards(): lax.all_to_all(outgoing_rows.reshape(n_req, deal, col_width), 'req', spli...  7.12 us
    all_to_all x1, starting transfers between devices, shards(): lax.all_to_all(spread, 'kv', split_axis=1, concat_axis=1, tiled=True)  5.31 us
    all_to_all x1, waiting for transfers between devices, shards(): lax.all_to_all(partial.reshape(n_kv, sub_rows, partial.shape[1]), 'kv', s...  4.79 us
  transfers between devices with their start and end apart: 5, of which 4 were waited for; matrix products, arithmetic and copies ran while one was open for 9% of the time, Pallas kernels for 0%

profile of v7, /device:TPU:0, one launch (start us, length us, event | category | flops | bytes accessed | tf_op | source)
XLA Modules:
  0.0 130.9 jit_solution(5890588791615514914)
XLA Ops:
  0.0 0.8 add_select_fusion.1
  0.8 0.8 fusion.43
  2.4 0.9 convolution_convert_fusion.4
  3.9 7.1 %all-to-all-start = ((bf16[16,4,192]{2,1,0:T(4,128)(2,1)}), bf16[16,4,192]{2,1,0:T(4,128)(2,1)S(1)}, u32[]{:S(2)}, u32[]{:S(2)}) async-start(bf16[16,4,192]{2,1,0:T(4,128)(2,1)} %reshape.384), calls=%async_computation | async-start | bytes 65536 | tf_op jit(solution)/shard_map/all_to_all | solution.py:211
  11.1 0.8 and_select_fusion.3
  12.7 0.7 broadcast_in_dim.20
  13.6 0.7 fusion.37
  14.6 0.7 fusion.4
  16.0 0.8 copy.86
  17.2 0.8 multiply_add_fusion.2
  18.0 0.8 mul.128
  18.8 0.8 copy.84.live_ref
  19.9 0.7 broadcast_in_dim.17
  20.6 5.3 %all-to-all-start.1 = ((bf16[64,8,192]{2,0,1:T(8,128)(2,1)}), bf16[64,8,192]{2,0,1:T(8,128)(2,1)S(1)}, u32[]{:S(2)}, u32[]{:S(2)}) async-start(bf16[64,8,192]{2,0,1:T(8,128)(2,1)} %broadcast_in_dim.17), calls=%async_computation.1 | async-start | bytes 524288 | tf_op jit(solution)/shard_map/all_to_all | solution.py:224
  26.2 7.3 %all-to-all-done.1 = bf16[64,8,192]{2,0,1:T(8,128)(2,1)S(1)} async-done(((bf16[64,8,192]{2,0,1:T(8,128)(2,1)}), bf16[64,8,192]{2,0,1:T(8,128)(2,1)S(1)}, u32[]{:S(2)}, u32[]{:S(2)}) %all-to-all-start.1) | async-done | bytes 196640 | tf_op jit(solution)/shard_map/all_to_all | solution.py:224
  33.8 0.8 copy.79
  34.6 1.9 %convert_element_type.182 = bf16[64,1536]{1,0:T(8,128)(2,1)} reshape(bf16[64,8,192]{2,1,0:T(8,128)(2,1)} %copy.79) | data formatting | bytes 393216 | tf_op jit(solution)/shard_map/convert_element_type | solution.py:19
  36.5 1.7 %fusion.14 = bf16[64,1,320]{2,0,1:T(8,128)(2,1)S(1)} fusion(bf16[64,1536]{1,0:T(8,128)(2,1)} %convert_element_type.182, bf16[1,1536,320]{1,2,0:T(8,128)(2,1)} %param.19), kind=kOutput, calls=%fused_computation.16 | convolution fusion | flops 62935040 | bytes 1220608 | tf_op jit(solution)/shard_map/sd,hdc->shc/dot_general | solution.py:123
  40.5 40.1 %shard_map.127 = f32[64,8,64]{2,1,0:T(8,128)} custom-call(s32[320]{0:T(512)} %get-tuple-element.12.owner_ref, bf16[64,8,64]{2,1,0:T(8,128)(2,1)} %pad.4.q_ref, s32[320,1,1]{2,1,0:T(1,128)} %copy.84.live_ref, bf16[320,1,128,128]{3,2,1,0:T(8,128)(2,1)} %kv_ref.1, bf16[64,1,64]{2,1,0:T(2,128)(2,1)} %copy.97.knew_ref, bf16[64,1,64]{2,1,0:T(2,128)(2,1)} %copy.98.vnew_ref), custom_call_target="tpu_custom_call" | custom-call | tf_op jit(solution)/shard_map/pallas_call | solution.py:109
  80.6 1.0 slice.91
  81.7 2.0 %fusion.5 = bf16[8,8,1536]{2,1,0:T(8,128)(2,1)} fusion(bf16[64,192]{0,1:T(8,128)(2,1)S(1)} %bitcast.52, bf16[1,192,1536]{2,1,0:T(8,128)(2,1)} %param.20), kind=kOutput, calls=%fused_computation.8 | convolution fusion | flops 37847040 | bytes 811008 | tf_op jit(solution)/shard_map/dot_general | solution.py:232
  83.7 4.0 %all-to-all-start.2 = ((bf16[8,8,1536]{2,1,0:T(8,128)(2,1)}), bf16[8,8,1536]{2,1,0:T(8,128)(2,1)}, u32[]{:S(2)}, u32[]{:S(2)}) async-start(bf16[8,8,1536]{2,1,0:T(8,128)(2,1)} %fusion.5), calls=%async_computation.2 | async-start | bytes 393216 | tf_op jit(solution)/shard_map/all_to_all | solution.py:233
  87.8 0.8 copy.77
  88.6 1.2 reshape.386
  89.8 4.8 %all-to-all-done.2 = bf16[8,8,1536]{2,1,0:T(8,128)(2,1)} async-done(((bf16[8,8,1536]{2,1,0:T(8,128)(2,1)}), bf16[8,8,1536]{2,1,0:T(8,128)(2,1)}, u32[]{:S(2)}, u32[]{:S(2)}) %all-to-all-start.2) | async-done | bytes 196640 | tf_op jit(solution)/shard_map/all_to_all | solution.py:233
  94.6 1.0 convert_reduce_fusion
  95.8 0.9 fusion.56
  98.4 7.2 %all-to-all-start.3 = ((bf16[16,2,1,1536]{3,1,2,0:T(2,128)(2,1)}), bf16[16,2,1,1536]{3,1,2,0:T(2,128)(2,1)S(1)}, u32[]{:S(2)}, u32[]{:S(2)}) async-start(bf16[16,2,1,1536]{3,1,2,0:T(2,128)(2,1)} %bitcast.9), calls=%async_computation.3 | async-start | bytes 196608 | tf_op jit(solution)/shard_map/all_to_all | solution.py:266
  105.8 7.7 %all-to-all-done.3 = bf16[16,2,1,1536]{3,1,2,0:T(2,128)(2,1)S(1)} async-done(((bf16[16,2,1,1536]{3,1,2,0:T(2,128)(2,1)}), bf16[16,2,1,1536]{3,1,2,0:T(2,128)(2,1)S(1)}, u32[]{:S(2)}, u32[]{:S(2)}) %all-to-all-start.3) | async-done | bytes 98336 | tf_op jit(solution)/shard_map/all_to_all | solution.py:266
  113.5 4.0 %fusion.6 = f32[1,32,2048]{2,1,0:T(8,128)S(1)} fusion(bf16[32,1536]{1,0:T(8,128)(2,1)S(1)} %reshape.395, bf16[1,1536,2048]{2,1,0:T(8,128)(2,1)} %param.24), kind=kOutput, calls=%fused_computation.9 | convolution fusion | flops 201326592 | bytes 6651904 | tf_op jit(solution)/shard_map/erd,edf->erf/dot_general | solution.py:168
  118.8 3.5 %all-to-all-start.4 = ((bf16[16,2,1,1536]{3,1,2,0:T(2,128)(2,1)}), bf16[16,2,1,1536]{3,1,2,0:T(2,128)(2,1)S(1)}, u32[]{:S(2)}, u32[]{:S(2)}) async-start(bf16[16,2,1,1536]{3,1,2,0:T(2,128)(2,1)} %bitcast.14), calls=%async_computation.4 | async-start | bytes 196608 | tf_op jit(solution)/shard_map/all_to_all | solution.py:267
  122.5 7.6 %all-to-all-done.4 = bf16[16,2,1,1536]{3,1,2,0:T(2,128)(2,1)S(1)} async-done(((bf16[16,2,1,1536]{3,1,2,0:T(2,128)(2,1)}), bf16[16,2,1,1536]{3,1,2,0:T(2,128)(2,1)S(1)}, u32[]{:S(2)}, u32[]{:S(2)}) %all-to-all-start.4) | async-done | bytes 98336 | tf_op jit(solution)/shard_map/all_to_all | solution.py:267
  (68 shorter events, 11.5 us)
Async XLA Ops:
  0.0 117.5 %copy-start = (bf16[1,1024,1536]{2,1,0:T(8,128)(2,1)S(1)}, bf16[1,1024,1536]{2,1,0:T(8,128)(2,1)}, u32[]{:S(2)}) copy-start(bf16[1,1024,1536]{2,1,0:T(8,128)(2,1)} %param.25) | copy-start | bytes 9437188
  3.9 15.8 %all-to-all-start = ((bf16[16,4,192]{2,1,0:T(4,128)(2,1)}), bf16[16,4,192]{2,1,0:T(4,128)(2,1)S(1)}, u32[]{:S(2)}, u32[]{:S(2)}) async-start(bf16[16,4,192]{2,1,0:T(4,128)(2,1)} %reshape.384), calls=%async_computation | async-start | bytes 65536 | tf_op jit(solution)/shard_map/all_to_all | solution.py:211
  20.6 12.9 %all-to-all-start.1 = ((bf16[64,8,192]{2,0,1:T(8,128)(2,1)}), bf16[64,8,192]{2,0,1:T(8,128)(2,1)S(1)}, u32[]{:S(2)}, u32[]{:S(2)}) async-start(bf16[64,8,192]{2,0,1:T(8,128)(2,1)} %broadcast_in_dim.17), calls=%async_computation.1 | async-start | bytes 524288 | tf_op jit(solution)/shard_map/all_to_all | solution.py:224
  40.5 55.2 %copy-start.1 = (f32[1536]{0:T(1024)S(1)}, f32[1536]{0:T(1024)}, u32[]{:S(2)}) copy-start(f32[1536]{0:T(1024)} %param.21) | copy-start | bytes 18436
  83.7 10.9 %all-to-all-start.2 = ((bf16[8,8,1536]{2,1,0:T(8,128)(2,1)}), bf16[8,8,1536]{2,1,0:T(8,128)(2,1)}, u32[]{:S(2)}, u32[]{:S(2)}) async-start(bf16[8,8,1536]{2,1,0:T(8,128)(2,1)} %fusion.5), calls=%async_computation.2 | async-start | bytes 393216 | tf_op jit(solution)/shard_map/all_to_all | solution.py:233
  98.4 15.0 %all-to-all-start.3 = ((bf16[16,2,1,1536]{3,1,2,0:T(2,128)(2,1)}), bf16[16,2,1,1536]{3,1,2,0:T(2,128)(2,1)S(1)}, u32[]{:S(2)}, u32[]{:S(2)}) async-start(bf16[16,2,1,1536]{3,1,2,0:T(2,128)(2,1)} %bitcast.9), calls=%async_computation.3 | async-start | bytes 196608 | tf_op jit(solution)/shard_map/all_to_all | solution.py:266
  118.8 11.3 %all-to-all-start.4 = ((bf16[16,2,1,1536]{3,1,2,0:T(2,128)(2,1)}), bf16[16,2,1,1536]{3,1,2,0:T(2,128)(2,1)S(1)}, u32[]{:S(2)}, u32[]{:S(2)}) async-start(bf16[16,2,1,1536]{3,1,2,0:T(2,128)(2,1)} %bitcast.14), calls=%async_computation.4 | async-start | bytes 196608 | tf_op jit(solution)/shard_map/all_to_all | solution.py:267

commit v8 on v6

--- a/solution.py
+++ b/solution.py
@@ -142,6 +142,11 @@
     n_req = lax.axis_size("req")
     n_kv = lax.axis_size("kv")
     local_rows, col_width = hidden.shape
+    width = n_kv * col_width
+    spread = jnp.broadcast_to(hidden[:, None], (local_rows, n_kv, col_width))
+    block_rows = lax.all_to_all(spread, "kv", split_axis=1, concat_axis=1, tiled=True).reshape(
+        local_rows, width
+    )
     deal = local_rows // n_req
     source_block = (perm // local_rows).reshape(n_req, local_rows)
     source_row = (perm % local_rows).reshape(n_req, local_rows)
@@ -151,24 +156,20 @@
     send_ids = jnp.arange(deal * local_rows, dtype=jnp.int32)
     send_pick = jnp.any(send_key[:, :, None] == send_ids[None, None, :], axis=1)
     send_pick = send_pick.reshape(n_req * deal, local_rows).astype(hidden.dtype)
-    outgoing_rows = jnp.dot(send_pick, hidden, preferred_element_type=jnp.float32).astype(
+    outgoing_rows = jnp.dot(send_pick, block_rows, preferred_element_type=jnp.float32).astype(
         hidden.dtype
     )
     arrived_rows = lax.all_to_all(
-        outgoing_rows.reshape(n_req, deal, col_width), "req", split_axis=0, concat_axis=0, tiled=True
-    ).reshape(n_req * deal, col_width)
+        outgoing_rows.reshape(n_req, deal, width), "req", split_axis=0, concat_axis=0, tiled=True
+    ).reshape(n_req * deal, width)
     my_source = lax.dynamic_slice_in_dim(perm, req_index * local_rows, local_rows) // local_rows
     slot_ids = jnp.arange(local_rows, dtype=jnp.int32)
     same_before = (my_source[None, :] == my_source[:, None]) & (slot_ids[None, :] < slot_ids[:, None])
     rank_got = jnp.sum(same_before.astype(jnp.int32), axis=1)
     take_key = my_source * deal + rank_got
     take_pick = (take_key[:, None] == slot_ids[None, :]).astype(hidden.dtype)
-    picked_rows = jnp.dot(take_pick, arrived_rows, preferred_element_type=jnp.float32).astype(
+    tokens = jnp.dot(take_pick, arrived_rows, preferred_element_type=jnp.float32).astype(
         hidden.dtype
-    )
-    spread = jnp.broadcast_to(picked_rows[:, None], (local_rows, n_kv, col_width))
-    tokens = lax.all_to_all(spread, "kv", split_axis=1, concat_axis=1, tiled=True).reshape(
-        local_rows, n_kv * col_width
     )
     normed = rms_norm(tokens, attn_gain)
     head_out = attend(normed, seq_lens, page_table, kv_cache, qkv_weight)
@@ -208,11 +209,12 @@
     outgoing = jnp.einsum(
         "qe,qd->ed", placement_plan, paired_rows, preferred_element_type=jnp.float32
     )
-    outgoing = outgoing.astype(jnp.bfloat16).reshape(n_req, capacity, local_experts, width)
+    outgoing = outgoing.astype(jnp.bfloat16).reshape(n_req, capacity * local_experts, width)
     arrived = lax.all_to_all(outgoing, "req", split_axis=0, concat_axis=0, tiled=True)
-    returned = lax.all_to_all(
-        expert_apply(arrived, gate_up, down), "req", split_axis=0, concat_axis=0, tiled=True
-    )
+    expert_rows = expert_apply(
+        arrived.reshape(n_req, capacity, local_experts, width), gate_up, down
+    ).reshape(n_req, capacity * local_experts, width)
+    returned = lax.all_to_all(expert_rows, "req", split_axis=0, concat_axis=0, tiled=True)
     back_rows = returned.reshape(experts_all * capacity, width)
     paired_output = jnp.dot(placement_plan, back_rows, preferred_element_type=jnp.float32).reshape(
         sub_rows, 2, width

time: 113 us -> 107 us (0.947)
  local copies, waits for them, and re-layouts: 19.8 us -> 13.9 us
  starting transfers between devices: 27.2 us -> 23.9 us
  waiting for transfers between devices: 26.2 us -> 28.8 us
  matrix products: 23.6 us -> 25.3 us
  other arithmetic: 14.5 us -> 13.2 us
    all_to_all x2, waiting for transfers between devices: 7.63 us -> 15 us  [the longest x1 7.62 us: shards(): lax.all_to_all(expert_rows, 'req', split_axis=0, concat_axis=0, tiled=True)]
    all_to_all x1, waiting for transfers between devices: 6.78 us -> 0.01 us  [shards(): lax.all_to_all(spread, 'kv', split_axis=1, concat_axis=1, tiled=True)]
    all_to_all x1, starting transfers between devices: 7.22 us -> 3.51 us  [shards(): lax.all_to_all(outgoing, 'req', split_axis=0, concat_axis=0, tiled=True)]
    convert_element_type x2 -> x0, local copies, waits for them, and re-layouts: 2.72 us -> none  [rms_norm(): return (values * factor * gain_vec).astype(jnp.bfloat16)]
    all_to_all x1, waiting for transfers between devices: 4.13 us -> 6.16 us  [shards(): lax.all_to_all(partial.reshape(n_kv, sub_rows, partial.shape[1]), 'kv', s...]
  transfers between devices with their start and end apart: 5 -> 5, of which waited for: 4 -> 4; matrix products, arithmetic and copies ran while one was open for 11% -> 12% of each run, Pallas kernels for 0% -> 0%
where the time goes in v8:
time: 107 us; the launch traced here: 106 us
  waiting for transfers between devices  28.8 us (27%)
  matrix products  25.3 us (24%)
  starting transfers between devices  23.9 us (22%)
  local copies, waits for them, and re-layouts  13.9 us (13%)
  other arithmetic  13.2 us (12%)
    all_to_all x1, waiting for transfers between devices, shards(): lax.all_to_all(outgoing, 'req', split_axis=0, concat_axis=0, tiled=True)  7.65 us
    all_to_all x1, waiting for transfers between devices, shards(): lax.all_to_all(expert_rows, 'req', split_axis=0, concat_axis=0, tiled=True)  7.62 us
    all_to_all x1, waiting for transfers between devices, shards(): lax.all_to_all(outgoing_rows.reshape(n_req, deal, width), 'req', split_ax...  7.37 us
    all_to_all x1, starting transfers between devices, shards(): lax.all_to_all(outgoing_rows.reshape(n_req, deal, width), 'req', split_ax...  7.03 us
    all_to_all x1, waiting for transfers between devices, shards(): lax.all_to_all(partial.reshape(n_kv, sub_rows, partial.shape[1]), 'kv', s...  6.16 us
    dot_general x1, matrix products, attend(): jnp.einsum('pkgd,pkdt->pkgt', page_queries, kv_cache[:, :, :head_dim, :],...  5.64 us
    dot_general x1, matrix products, attend(): jnp.einsum('pkgt,pkdt->pkgd', weights.astype(jnp.bfloat16), kv_cache[:, :...  5.62 us
    all_to_all x1, starting transfers between devices, shards(): lax.all_to_all(spread, 'kv', split_axis=1, concat_axis=1, tiled=True)  5.4 us
  transfers between devices with their start and end apart: 5, of which 4 were waited for; matrix products, arithmetic and copies ran while one was open for 12% of the time, Pallas kernels for 0%

profile of v8, /device:TPU:0, one launch (start us, length us, event | category | flops | bytes accessed | tf_op | source)
XLA Modules:
  0.0 105.5 jit_solution(2824012023838022249)
XLA Ops:
  0.0 1.6 %broadcast_in_dim.65 = bf16[64,8,192]{2,0,1:T(8,128)(2,1)} broadcast(bf16[64,192]{1,0:T(8,128)(2,1)} %param.13), dimensions={0,2} | broadcast | bytes 221184 | tf_op jit(solution)/shard_map/broadcast_in_dim | solution.py:146
  1.6 5.4 %all-to-all-start = ((bf16[64,8,192]{2,0,1:T(8,128)(2,1)}), bf16[64,8,192]{2,0,1:T(8,128)(2,1)}, u32[]{:S(2)}, u32[]{:S(2)}) async-start(bf16[64,8,192]{2,0,1:T(8,128)(2,1)} %broadcast_in_dim.65), calls=%async_computation | async-start | bytes 524288 | tf_op jit(solution)/shard_map/all_to_all | solution.py:147
  7.7 0.7 broadcast_in_dim.68
  8.8 0.7 fusion.58
  9.7 0.8 fusion.6
  12.6 0.8 and_select_fusion.3
  14.3 0.8 copy.102
  16.9 0.8 add_compare_fusion
  17.6 1.1 %copy.92 = bf16[64,8,192]{2,1,0:T(8,128)(2,1)S(1)} copy(bf16[64,8,192]{2,0,1:T(8,128)(2,1)} %all-to-all-done) | data formatting | bytes 393216 | tf_op jit(solution)/shard_map/all_to_all | solution.py:147
  18.7 0.9 reshape.446
  19.6 1.1 %convolution_convert_fusion.2 = bf16[64,1536]{1,0:T(8,128)(2,1)S(1)} fusion(pred[64,64]{1,0:T(32,128)(4,1)S(1)} %reshape.445, bf16[64,1536]{1,0:T(8,128)(2,1)} %reshape.446), kind=kOutput, calls=%fused_computation.13 | convolution fusion | flops 12681216 | bytes 397312 | tf_op jit(solution)/shard_map/dot_general | solution.py:159
  21.5 7.0 %all-to-all-start.1 = ((bf16[16,4,1536]{2,1,0:T(4,128)(2,1)}), bf16[16,4,1536]{2,1,0:T(4,128)(2,1)S(1)}, u32[]{:S(2)}, u32[]{:S(2)}) async-start(bf16[16,4,1536]{2,1,0:T(4,128)(2,1)} %reshape.447), calls=%async_computation.1 | async-start | bytes 393216 | tf_op jit(solution)/shard_map/all_to_all | solution.py:162
  28.5 1.3 %multiply_add_fusion.2 = s32[64]{0:T(128)} fusion(s32[64]{0:T(128)S(1)} %convert_reduce_fusion.1, s32[1024]{0:T(1024)} %param.14, s32[]{:T(128)S(6)} %select_n.121), kind=kLoop, calls=%fused_computation.144 | loop fusion | flops 1088 | bytes 772 | tf_op jit(solution)/shard_map/add | solution.py:169
  29.8 7.4 %all-to-all-done.1 = bf16[16,4,1536]{2,1,0:T(4,128)(2,1)S(1)} async-done(((bf16[16,4,1536]{2,1,0:T(4,128)(2,1)}), bf16[16,4,1536]{2,1,0:T(4,128)(2,1)S(1)}, u32[]{:S(2)}, u32[]{:S(2)}) %all-to-all-start.1) | async-done | bytes 196640 | tf_op jit(solution)/shard_map/all_to_all | solution.py:162
  37.2 0.9 fusion.27
  38.2 1.6 %fusion.19 = bf16[64,1,320]{2,0,1:T(8,128)(2,1)S(1)} fusion(bf16[1,1536,320]{1,2,0:T(8,128)(2,1)} %param.19, bf16[64,1536]{1,0:T(8,128)(2,1)S(1)} %get-tuple-element.18, f32[1536]{0:T(1024)S(1)} %copy-done.5, f32[64]{0:T(128)S(1)} %add_rsqrt_fusion.1), kind=kOutput, calls=%fused_computation.26 | convolution fusion | flops 63328256 | bytes 1227008 | tf_op jit(solution)/shard_map/sd,hdc->shc/dot_general | solution.py:25
  41.9 1.0 fusion.52
  42.9 0.9 copy.96
  43.8 5.6 %fusion.78 = (f32[320,3]{1,0:T(8,128)}, f32[320,3,128]{2,1,0:T(4,128)}) fusion(bf16[320,3,64]{2,1,0:T(4,128)(2,1)} %copy.96, bf16[320,1,128,128]{3,2,0,1:T(8,128)(2,1)} %bitcast.90, pred[320,128]{1,0:T(8,128)(4,1)} %add_compare_fusion), kind=kOutput, calls=%fused_computation.149 | convolution fusion | flops 16096320 | bytes 6106880 | tf_op jit(solution)/shard_map/pkgd,pkdt->pkgt/dot_general | solution.py:68
  49.4 1.0 copy.97
  51.5 1.9 %fusion.25 = f32[320,3]{1,0:T(8,128)S(1)} fusion(f32[320,3,128]{2,1,0:T(4,128)} %get-tuple-element.20, f32[320,3]{1,0:T(8,128)S(1)} %copy.98, pred[320,128]{1,0:T(8,128)(4,1)} %add_compare_fusion), kind=kLoop, calls=%fused_computation.39 | loop fusion | flops 367680 | bytes 540160 | tf_op jit(solution)/shard_map/reduce_sum | solution.py:92
  53.4 5.6 %fusion.2 = f32[320,3,64]{2,1,0:T(4,128)S(1)} fusion(bf16[320,1,128,128]{3,2,0,1:T(8,128)(2,1)} %bitcast.91, f32[320,3,128]{2,1,0:T(4,128)} %get-tuple-element.20, f32[320,3]{1,0:T(8,128)S(1)} %copy.98, pred[320,128]{1,0:T(8,128)(4,1)} %add_compare_fusion), kind=kOutput, calls=%fused_computation.4 | convolution fusion | flops 16097280 | bytes 6188800 | tf_op jit(solution)/shard_map/pkgt,pkdt->pkgd/dot_general | solution.py:93
  59.8 2.0 %fusion.7 = bf16[8,8,1536]{2,1,0:T(8,128)(2,1)} fusion(bf16[64,192]{0,1:T(8,128)(2,1)S(1)} %bitcast.88, bf16[1,192,1536]{2,1,0:T(8,128)(2,1)} %param.20), kind=kOutput, calls=%fused_computation.14 | convolution fusion | flops 37847040 | bytes 811008 | tf_op jit(solution)/shard_map/dot_general | solution.py:179
  61.8 4.5 %all-to-all-start.2 = ((bf16[8,8,1536]{2,1,0:T(8,128)(2,1)}), bf16[8,8,1536]{2,1,0:T(8,128)(2,1)S(1)}, u32[]{:S(2)}, u32[]{:S(2)}) async-start(bf16[8,8,1536]{2,1,0:T(8,128)(2,1)} %fusion.7), calls=%async_computation.2 | async-start | bytes 393216 | tf_op jit(solution)/shard_map/all_to_all | solution.py:180
  66.9 6.2 %all-to-all-done.2 = bf16[8,8,1536]{2,1,0:T(8,128)(2,1)S(1)} async-done(((bf16[8,8,1536]{2,1,0:T(8,128)(2,1)}), bf16[8,8,1536]{2,1,0:T(8,128)(2,1)S(1)}, u32[]{:S(2)}, u32[]{:S(2)}) %all-to-all-start.2) | async-done | bytes 196640 | tf_op jit(solution)/shard_map/all_to_all | solution.py:180
  73.3 0.8 fusion.50
  74.1 0.9 fusion.79
  76.7 3.5 %all-to-all-start.3 = ((bf16[16,2,1536]{2,1,0:T(2,128)(2,1)}), bf16[16,2,1536]{2,1,0:T(2,128)(2,1)S(1)}, u32[]{:S(2)}, u32[]{:S(2)}) async-start(bf16[16,2,1536]{2,1,0:T(2,128)(2,1)} %reshape.459), calls=%async_computation.3 | async-start | bytes 196608 | tf_op jit(solution)/shard_map/all_to_all | solution.py:213
  80.4 7.7 %all-to-all-done.3 = bf16[16,2,1536]{2,1,0:T(2,128)(2,1)S(1)} async-done(((bf16[16,2,1536]{2,1,0:T(2,128)(2,1)}), bf16[16,2,1536]{2,1,0:T(2,128)(2,1)S(1)}, u32[]{:S(2)}, u32[]{:S(2)}) %all-to-all-start.3) | async-done | bytes 98336 | tf_op jit(solution)/shard_map/all_to_all | solution.py:213
  88.1 4.0 %fusion.8 = f32[1,32,2048]{2,1,0:T(8,128)S(1)} fusion(bf16[32,1536]{1,0:T(8,128)(2,1)S(1)} %reshape.460, bf16[1,1536,2048]{2,1,0:T(8,128)(2,1)} %param.24), kind=kOutput, calls=%fused_computation.15 | convolution fusion | flops 201326592 | bytes 6651904 | tf_op jit(solution)/shard_map/erd,edf->erf/dot_general | solution.py:114
  93.4 3.5 %all-to-all-start.4 = ((bf16[16,2,1536]{2,1,0:T(2,128)(2,1)}), bf16[16,2,1536]{2,1,0:T(2,128)(2,1)S(1)}, u32[]{:S(2)}, u32[]{:S(2)}) async-start(bf16[16,2,1536]{2,1,0:T(2,128)(2,1)} %reshape_transpose_reshape.4), calls=%async_computation.4 | async-start | bytes 196608 | tf_op jit(solution)/shard_map/all_to_all | solution.py:217
  97.0 7.6 %all-to-all-done.4 = bf16[16,2,1536]{2,1,0:T(2,128)(2,1)S(1)} async-done(((bf16[16,2,1536]{2,1,0:T(2,128)(2,1)}), bf16[16,2,1536]{2,1,0:T(2,128)(2,1)S(1)}, u32[]{:S(2)}, u32[]{:S(2)}) %all-to-all-start.4) | async-done | bytes 98336 | tf_op jit(solution)/shard_map/all_to_all | solution.py:217
  (91 shorter events, 15.6 us)
Async XLA Ops:
  0.0 92.0 %copy-start = (bf16[1,1024,1536]{2,1,0:T(8,128)(2,1)S(1)}, bf16[1,1024,1536]{2,1,0:T(8,128)(2,1)}, u32[]{:S(2)}) copy-start(bf16[1,1024,1536]{2,1,0:T(8,128)(2,1)} %param.25) | copy-start | bytes 9437188
  0.0 38.2 %copy-start.5 = (f32[1536]{0:T(1024)S(1)}, f32[1536]{0:T(1024)}, u32[]{:S(2)}) copy-start(f32[1536]{0:T(1024)} %param.18) | copy-start | bytes 18436
  1.6 16.0 %all-to-all-start = ((bf16[64,8,192]{2,0,1:T(8,128)(2,1)}), bf16[64,8,192]{2,0,1:T(8,128)(2,1)}, u32[]{:S(2)}, u32[]{:S(2)}) async-start(bf16[64,8,192]{2,0,1:T(8,128)(2,1)} %broadcast_in_dim.65), calls=%async_computation | async-start | bytes 524288 | tf_op jit(solution)/shard_map/all_to_all | solution.py:147
  15.2 14.6 %copy-start.6 = (s32[16]{0:T(128)}, s32[16]{0:T(128)S(1)}, u32[]{:S(2)}) copy-start(s32[16]{0:T(128)S(1)} %eq.159) | copy-start | bytes 196
  15.5 0.5 copy-start.8
  21.5 15.7 %all-to-all-start.1 = ((bf16[16,4,1536]{2,1,0:T(4,128)(2,1)}), bf16[16,4,1536]{2,1,0:T(4,128)(2,1)S(1)}, u32[]{:S(2)}, u32[]{:S(2)}) async-start(bf16[16,4,1536]{2,1,0:T(4,128)(2,1)} %reshape.447), calls=%async_computation.1 | async-start | bytes 393216 | tf_op jit(solution)/shard_map/all_to_all | solution.py:162
  38.2 12.3 %copy-start.1 = (pred[64,320]{1,0:T(8,128)(4,1)S(1)}, pred[64,320]{1,0:T(8,128)(4,1)}, u32[]{:S(2)}) copy-start(pred[64,320]{1,0:T(8,128)(4,1)} %slice_compare_fusion) | copy-start | bytes 61444
  43.8 6.8 %copy-start.2 = (bf16[64,1,192]{0,2,1:T(8,128)(2,1)S(1)}, bf16[64,1,192]{0,2,1:T(8,128)(2,1)}, u32[]{:S(2)}) copy-start(bf16[64,1,192]{0,2,1:T(8,128)(2,1)} %copy.94) | copy-start | bytes 73732
  43.8 6.8 %copy-start.3 = (f32[64,64]{0,1:T(8,128)S(1)}, f32[64,64]{0,1:T(8,128)}, u32[]{:S(2)}) copy-start(f32[64,64]{0,1:T(8,128)} %copy.118) | copy-start | bytes 49156
  51.5 7.8 %copy-start.7 = (bf16[64,1,3]{0,2,1:T(4,128)(2,1)S(1)}, bf16[64,1,3]{0,2,1:T(4,128)(2,1)}, u32[]{:S(2)}) copy-start(bf16[64,1,3]{0,2,1:T(4,128)(2,1)} %get-tuple-element.15) | copy-start | bytes 1156
  51.5 7.8 %copy-start.4 = (f32[64,64]{1,0:T(8,128)S(1)}, f32[64,64]{1,0:T(8,128)}, u32[]{:S(2)}) copy-start(f32[64,64]{1,0:T(8,128)} %get-tuple-element.11) | copy-start | bytes 49156
  61.8 11.3 %all-to-all-start.2 = ((bf16[8,8,1536]{2,1,0:T(8,128)(2,1)}), bf16[8,8,1536]{2,1,0:T(8,128)(2,1)S(1)}, u32[]{:S(2)}, u32[]{:S(2)}) async-start(bf16[8,8,1536]{2,1,0:T(8,128)(2,1)} %fusion.7), calls=%async_computation.2 | async-start | bytes 393216 | tf_op jit(solution)/shard_map/all_to_all | solution.py:180
  76.7 11.3 %all-to-all-start.3 = ((bf16[16,2,1536]{2,1,0:T(2,128)(2,1)}), bf16[16,2,1536]{2,1,0:T(2,128)(2,1)S(1)}, u32[]{:S(2)}, u32[]{:S(2)}) async-start(bf16[16,2,1536]{2,1,0:T(2,128)(2,1)} %reshape.459), calls=%async_computation.3 | async-start | bytes 196608 | tf_op jit(solution)/shard_map/all_to_all | solution.py:213
  88.1 16.6 %copy-start.9 = (s32[8,2]{0,1:T(2,128)S(1)}, s32[8,2]{0,1:T(2,128)}, u32[]{:S(2)}) copy-start(s32[8,2]{0,1:T(2,128)} %copy.110) | copy-start | bytes 196
  93.4 11.3 %all-to-all-start.4 = ((bf16[16,2,1536]{2,1,0:T(2,128)(2,1)}), bf16[16,2,1536]{2,1,0:T(2,128)(2,1)S(1)}, u32[]{:S(2)}, u32[]{:S(2)}) async-start(bf16[16,2,1536]{2,1,0:T(2,128)(2,1)} %reshape_transpose_reshape.4), calls=%async_computation.4 | async-start | bytes 196608 | tf_op jit(solution)/shard_map/all_to_all | solution.py:217

commit v9 on v8

--- a/solution.py
+++ b/solution.py
@@ -155,22 +155,21 @@
     send_key = jnp.where(mine, rank_sent * local_rows + source_row, -1)
     send_ids = jnp.arange(deal * local_rows, dtype=jnp.int32)
     send_pick = jnp.any(send_key[:, :, None] == send_ids[None, None, :], axis=1)
-    send_pick = send_pick.reshape(n_req * deal, local_rows).astype(hidden.dtype)
-    outgoing_rows = jnp.dot(send_pick, block_rows, preferred_element_type=jnp.float32).astype(
-        hidden.dtype
-    )
-    arrived_rows = lax.all_to_all(
-        outgoing_rows.reshape(n_req, deal, width), "req", split_axis=0, concat_axis=0, tiled=True
-    ).reshape(n_req * deal, width)
+    send_pick = send_pick.reshape(n_req, deal, local_rows).astype(hidden.dtype)
+    outgoing_rows = jnp.einsum(
+        "dir,rc->dic", send_pick, block_rows, preferred_element_type=jnp.float32
+    ).astype(hidden.dtype)
+    arrived_rows = lax.all_to_all(outgoing_rows, "req", split_axis=0, concat_axis=0, tiled=True)
     my_source = lax.dynamic_slice_in_dim(perm, req_index * local_rows, local_rows) // local_rows
     slot_ids = jnp.arange(local_rows, dtype=jnp.int32)
     same_before = (my_source[None, :] == my_source[:, None]) & (slot_ids[None, :] < slot_ids[:, None])
     rank_got = jnp.sum(same_before.astype(jnp.int32), axis=1)
     take_key = my_source * deal + rank_got
     take_pick = (take_key[:, None] == slot_ids[None, :]).astype(hidden.dtype)
-    tokens = jnp.dot(take_pick, arrived_rows, preferred_element_type=jnp.float32).astype(
-        hidden.dtype
-    )
+    tokens = jnp.einsum(
+        "sri,ric->sc", take_pick.reshape(local_rows, n_req, deal), arrived_rows,
+        preferred_element_type=jnp.float32,
+    ).astype(hidden.dtype)
     normed = rms_norm(tokens, attn_gain)
     head_out = attend(normed, seq_lens, page_table, kv_cache, qkv_weight)
     sub_rows = routes.shape[0]
@@ -185,7 +184,10 @@
     residual = (own_tokens.astype(jnp.float32) + attn_rows).astype(jnp.bfloat16)
     normed_ffn = rms_norm(residual, ffn_gain)
     logits = jnp.dot(normed_ffn, router, preferred_element_type=jnp.float32)
-    chosen = jnp.take_along_axis(logits, routes, axis=1)
+    expert_ids = jnp.arange(logits.shape[1], dtype=jnp.int32)
+    chosen = jnp.sum(
+        jnp.where(routes[:, :, None] == expert_ids[None, None, :], logits[:, None, :], 0.0), axis=2
+    )
     sigmoid_vals = jax.nn.sigmoid(chosen)
     gates = sigmoid_vals / jnp.sum(sigmoid_vals, axis=1, keepdims=True)
     experts_all = router.shape[1]
@@ -202,22 +204,24 @@
         + rank_in * local_experts
         + flat_routes % local_experts
     )
+    slots_per_dest = capacity * local_experts
+    dest_slot = (
+        jnp.arange(n_req, dtype=jnp.int32)[:, None] * slots_per_dest
+        + jnp.arange(slots_per_dest, dtype=jnp.int32)[None, :]
+    )
     placement_plan = (
-        place_at[:, None] == jnp.arange(experts_all * capacity, dtype=jnp.int32)[None, :]
-    ).astype(jnp.bfloat16)
-    paired_rows = jnp.repeat(normed_ffn, 2, axis=0)
+        place_at.reshape(sub_rows, 2)[:, :, None, None] == dest_slot[None, None, :, :]
+    ).astype(jnp.bfloat16)
     outgoing = jnp.einsum(
-        "qe,qd->ed", placement_plan, paired_rows, preferred_element_type=jnp.float32
-    )
-    outgoing = outgoing.astype(jnp.bfloat16).reshape(n_req, capacity * local_experts, width)
+        "rjnc,rd->ncd", placement_plan, normed_ffn, preferred_element_type=jnp.float32
+    ).astype(jnp.bfloat16)
     arrived = lax.all_to_all(outgoing, "req", split_axis=0, concat_axis=0, tiled=True)
     expert_rows = expert_apply(
         arrived.reshape(n_req, capacity, local_experts, width), gate_up, down
-    ).reshape(n_req, capacity * local_experts, width)
+    ).reshape(n_req, slots_per_dest, width)
     returned = lax.all_to_all(expert_rows, "req", split_axis=0, concat_axis=0, tiled=True)
-    back_rows = returned.reshape(experts_all * capacity, width)
-    paired_output = jnp.dot(placement_plan, back_rows, preferred_element_type=jnp.float32).reshape(
-        sub_rows, 2, width
+    paired_output = jnp.einsum(
+        "rjnc,ncd->rjd", placement_plan, returned, preferred_element_type=jnp.float32
     )
     mixed = residual.astype(jnp.float32) + jnp.sum(gates[:, :, None] * paired_output, axis=1)
     return mixed.astype(jnp.bfloat16)

time: 107 us -> 108 us (level)
  local copies, waits for them, and re-layouts: 13.9 us -> 11.9 us
  other arithmetic: 13.2 us -> 15.1 us
    convert_element_type x0 -> x2, local copies, waits for them, and re-layouts: none -> 1.56 us  [the longest x1 0.82 us: shards(): outgoing_rows = jnp.einsum('dir,rc->dic', send_pick, block_rows, preferre...]
    reshape x6 -> x1, local copies, waits for them, and re-layouts: 1.6 us -> 0.09 us  [shards(): send_pick = send_pick.reshape(n_req, deal, local_rows).astype(hidden.dtype)]
where the time goes in v9:
time: 108 us; the launch traced here: 106 us
  waiting for transfers between devices  28.9 us (27%)
  matrix products  26.2 us (24%)
  starting transfers between devices  23.9 us (22%)
  other arithmetic  15.1 us (14%)
  local copies, waits for them, and re-layouts  11.9 us (11%)
    all_to_all x1, waiting for transfers between devices, shards(): lax.all_to_all(expert_rows, 'req', split_axis=0, concat_axis=0, tiled=True)  7.76 us
    all_to_all x1, waiting for transfers between devices, shards(): lax.all_to_all(outgoing, 'req', split_axis=0, concat_axis=0, tiled=True)  7.75 us
    all_to_all x1, waiting for transfers between devices, shards(): lax.all_to_all(outgoing_rows, 'req', split_axis=0, concat_axis=0, tiled=T...  7.36 us
    all_to_all x1, starting transfers between devices, shards(): lax.all_to_all(outgoing_rows, 'req', split_axis=0, concat_axis=0, tiled=T...  7.04 us
    all_to_all x1, waiting for transfers between devices, shards(): lax.all_to_all(partial.reshape(n_kv, sub_rows, partial.shape[1]), 'kv', s...  6.04 us
    dot_general x1, matrix products, attend(): jnp.einsum('pkgd,pkdt->pkgt', page_queries, kv_cache[:, :, :head_dim, :],...  5.64 us
    dot_general x1, matrix products, attend(): jnp.einsum('pkgt,pkdt->pkgd', weights.astype(jnp.bfloat16), kv_cache[:, :...  5.62 us
    all_to_all x1, starting transfers between devices, shards(): lax.all_to_all(spread, 'kv', split_axis=1, concat_axis=1, tiled=True)  5.4 us
  transfers between devices with their start and end apart: 5, of which 4 were waited for; matrix products, arithmetic and copies ran while one was open for 12% of the time, Pallas kernels for 0%

profile of v9, /device:TPU:0, one launch (start us, length us, event | category | flops | bytes accessed | tf_op | source)
XLA Modules:
  0.0 106.3 jit_solution(14042320680332954751)
XLA Ops:
  0.0 1.6 %broadcast_in_dim.71 = bf16[64,8,192]{2,0,1:T(8,128)(2,1)} broadcast(bf16[64,192]{1,0:T(8,128)(2,1)} %param.13), dimensions={0,2} | broadcast | bytes 221184 | tf_op jit(solution)/shard_map/broadcast_in_dim | solution.py:146
  1.6 5.4 %all-to-all-start = ((bf16[64,8,192]{2,0,1:T(8,128)(2,1)}), bf16[64,8,192]{2,0,1:T(8,128)(2,1)}, u32[]{:S(2)}, u32[]{:S(2)}) async-start(bf16[64,8,192]{2,0,1:T(8,128)(2,1)} %broadcast_in_dim.71), calls=%async_computation | async-start | bytes 524288 | tf_op jit(solution)/shard_map/all_to_all | solution.py:147
  9.7 0.8 fusion.6
  16.6 0.8 add_compare_fusion
  17.4 1.1 %copy.84 = bf16[64,8,192]{2,1,0:T(8,128)(2,1)S(1)} copy(bf16[64,8,192]{2,0,1:T(8,128)(2,1)} %all-to-all-done) | data formatting | bytes 393216 | tf_op jit(solution)/shard_map/all_to_all | solution.py:147
  18.5 0.9 reshape.459
  19.4 1.1 %convolution_convert_fusion.1 = bf16[16,4,1536]{2,0,1:T(8,128)(2,1)S(1)} fusion(bf16[64,1536,1]{1,0,2:T(8,128)(2,1)} %reshape.459, pred[16,4,64]{2,1,0:T(4,128)(4,1)S(1)} %reshape.442), kind=kOutput, calls=%fused_computation.13 | convolution fusion | flops 12681216 | bytes 397312 | tf_op jit(solution)/shard_map/dir,rc->dic/dot_general | solution.py:159
  20.5 0.8 copy.86
  21.3 7.0 %all-to-all-start.1 = ((bf16[16,4,1536]{2,1,0:T(4,128)(2,1)}), bf16[16,4,1536]{2,1,0:T(4,128)(2,1)S(1)}, u32[]{:S(2)}, u32[]{:S(2)}) async-start(bf16[16,4,1536]{2,1,0:T(4,128)(2,1)} %copy.86), calls=%async_computation.1 | async-start | bytes 393216 | tf_op jit(solution)/shard_map/all_to_all | solution.py:162
  28.4 1.3 %multiply_add_fusion.2 = s32[64]{0:T(128)} fusion(s32[64]{0:T(128)} %convert_reduce_fusion.1, s32[1024]{0:T(1024)} %param.14, s32[]{:T(128)S(6)} %select_n.111), kind=kLoop, calls=%fused_computation.153 | loop fusion | flops 1088 | bytes 772 | tf_op jit(solution)/shard_map/add | solution.py:167
  29.6 7.4 %all-to-all-done.1 = bf16[16,4,1536]{2,1,0:T(4,128)(2,1)S(1)} async-done(((bf16[16,4,1536]{2,1,0:T(4,128)(2,1)}), bf16[16,4,1536]{2,1,0:T(4,128)(2,1)S(1)}, u32[]{:S(2)}, u32[]{:S(2)}) %all-to-all-start.1) | async-done | bytes 196640 | tf_op jit(solution)/shard_map/all_to_all | solution.py:162
  37.0 1.0 fusion.29
  38.0 1.6 %fusion.21 = bf16[64,1,320]{2,0,1:T(8,128)(2,1)S(1)} fusion(bf16[1,1536,320]{1,2,0:T(8,128)(2,1)} %param.19, bf16[64,1536]{1,0:T(8,128)(2,1)S(1)} %get-tuple-element.16, f32[1536]{0:T(1024)S(1)} %copy-done.5, f32[64]{0:T(128)S(1)} %add_rsqrt_fusion.1), kind=kOutput, calls=%fused_computation.27 | convolution fusion | flops 63328256 | bytes 1227008 | tf_op jit(solution)/shard_map/sd,hdc->shc/dot_general | solution.py:25
  41.7 1.0 fusion.57
  42.7 0.9 copy.91
  43.6 5.6 %fusion.89 = (f32[320,3]{1,0:T(8,128)}, f32[320,3,128]{2,1,0:T(4,128)}) fusion(bf16[320,3,64]{2,1,0:T(4,128)(2,1)} %copy.91, bf16[320,1,128,128]{3,2,0,1:T(8,128)(2,1)} %bitcast.96, pred[320,128]{1,0:T(8,128)(4,1)} %add_compare_fusion), kind=kOutput, calls=%fused_computation.158 | convolution fusion | flops 16096320 | bytes 6106880 | tf_op jit(solution)/shard_map/pkgd,pkdt->pkgt/dot_general | solution.py:68
  49.3 1.0 copy.92
  50.3 0.9 select_reduce_fusion.1
  51.2 0.8 select_reduce_fusion
  52.2 1.9 %fusion.27 = f32[320,3]{1,0:T(8,128)S(1)} fusion(f32[320,3,128]{2,1,0:T(4,128)} %get-tuple-element.18, f32[320,3]{1,0:T(8,128)S(1)} %copy.93, pred[320,128]{1,0:T(8,128)(4,1)} %add_compare_fusion), kind=kLoop, calls=%fused_computation.40 | loop fusion | flops 367680 | bytes 540160 | tf_op jit(solution)/shard_map/reduce_sum | solution.py:92
  54.1 5.6 %fusion.2 = f32[320,3,64]{2,1,0:T(4,128)S(1)} fusion(bf16[320,1,128,128]{3,2,0,1:T(8,128)(2,1)} %bitcast.97, f32[320,3,128]{2,1,0:T(4,128)} %get-tuple-element.18, f32[320,3]{1,0:T(8,128)S(1)} %copy.93, pred[320,128]{1,0:T(8,128)(4,1)} %add_compare_fusion), kind=kOutput, calls=%fused_computation.3 | convolution fusion | flops 16097280 | bytes 6188800 | tf_op jit(solution)/shard_map/pkgt,pkdt->pkgd/dot_general | solution.py:93
  60.5 2.0 %fusion.8 = bf16[8,8,1536]{2,1,0:T(8,128)(2,1)} fusion(bf16[64,192]{0,1:T(8,128)(2,1)S(1)} %bitcast.94, bf16[1,192,1536]{2,1,0:T(8,128)(2,1)} %param.20), kind=kOutput, calls=%fused_computation.14 | convolution fusion | flops 37847040 | bytes 811008 | tf_op jit(solution)/shard_map/dot_general | solution.py:178
  62.5 4.5 %all-to-all-start.2 = ((bf16[8,8,1536]{2,1,0:T(8,128)(2,1)}), bf16[8,8,1536]{2,1,0:T(8,128)(2,1)S(1)}, u32[]{:S(2)}, u32[]{:S(2)}) async-start(bf16[8,8,1536]{2,1,0:T(8,128)(2,1)} %fusion.8), calls=%async_computation.2 | async-start | bytes 393216 | tf_op jit(solution)/shard_map/all_to_all | solution.py:179
  67.8 6.0 %all-to-all-done.2 = bf16[8,8,1536]{2,1,0:T(8,128)(2,1)S(1)} async-done(((bf16[8,8,1536]{2,1,0:T(8,128)(2,1)}), bf16[8,8,1536]{2,1,0:T(8,128)(2,1)S(1)}, u32[]{:S(2)}, u32[]{:S(2)}) %all-to-all-start.2) | async-done | bytes 196640 | tf_op jit(solution)/shard_map/all_to_all | solution.py:179
  74.0 1.0 fusion.77
  75.0 0.8 select_reduce_fusion.3
  75.9 0.9 convolution_convert_fusion.2
  77.5 3.5 %all-to-all-start.3 = ((bf16[16,2,1536]{2,1,0:T(2,128)(2,1)}), bf16[16,2,1536]{2,1,0:T(2,128)(2,1)S(1)}, u32[]{:S(2)}, u32[]{:S(2)}) async-start(bf16[16,2,1536]{2,1,0:T(2,128)(2,1)} %copy.100), calls=%async_computation.3 | async-start | bytes 196608 | tf_op jit(solution)/shard_map/all_to_all | solution.py:218
  81.1 7.8 %all-to-all-done.3 = bf16[16,2,1536]{2,1,0:T(2,128)(2,1)S(1)} async-done(((bf16[16,2,1536]{2,1,0:T(2,128)(2,1)}), bf16[16,2,1536]{2,1,0:T(2,128)(2,1)S(1)}, u32[]{:S(2)}, u32[]{:S(2)}) %all-to-all-start.3) | async-done | bytes 98336 | tf_op jit(solution)/shard_map/all_to_all | solution.py:218
  88.9 4.0 %fusion.9 = f32[1,32,2048]{2,1,0:T(8,128)S(1)} fusion(bf16[32,1536]{1,0:T(8,128)(2,1)S(1)} %reshape.452, bf16[1,1536,2048]{2,1,0:T(8,128)(2,1)} %param.24), kind=kOutput, calls=%fused_computation.15 | convolution fusion | flops 201326592 | bytes 6651904 | tf_op jit(solution)/shard_map/erd,edf->erf/dot_general | solution.py:114
  94.1 3.5 %all-to-all-start.4 = ((bf16[16,2,1536]{2,1,0:T(2,128)(2,1)}), bf16[16,2,1536]{2,1,0:T(2,128)(2,1)S(1)}, u32[]{:S(2)}, u32[]{:S(2)}) async-start(bf16[16,2,1536]{2,1,0:T(2,128)(2,1)} %reshape_transpose_reshape.4), calls=%async_computation.4 | async-start | bytes 196608 | tf_op jit(solution)/shard_map/all_to_all | solution.py:222
  97.7 7.8 %all-to-all-done.4 = bf16[16,2,1536]{2,1,0:T(2,128)(2,1)S(1)} async-done(((bf16[16,2,1536]{2,1,0:T(2,128)(2,1)}), bf16[16,2,1536]{2,1,0:T(2,128)(2,1)S(1)}, u32[]{:S(2)}, u32[]{:S(2)}) %all-to-all-start.4) | async-done | bytes 98336 | tf_op jit(solution)/shard_map/all_to_all | solution.py:222
  (75 shorter events, 15.6 us)
Async XLA Ops:
  0.0 92.8 %copy-start = (bf16[1,1024,1536]{2,1,0:T(8,128)(2,1)S(1)}, bf16[1,1024,1536]{2,1,0:T(8,128)(2,1)}, u32[]{:S(2)}) copy-start(bf16[1,1024,1536]{2,1,0:T(8,128)(2,1)} %param.25) | copy-start | bytes 9437188
  0.0 38.0 %copy-start.5 = (f32[1536]{0:T(1024)S(1)}, f32[1536]{0:T(1024)}, u32[]{:S(2)}) copy-start(f32[1536]{0:T(1024)} %param.18) | copy-start | bytes 18436
  1.6 15.7 %all-to-all-start = ((bf16[64,8,192]{2,0,1:T(8,128)(2,1)}), bf16[64,8,192]{2,0,1:T(8,128)(2,1)}, u32[]{:S(2)}, u32[]{:S(2)}) async-start(bf16[64,8,192]{2,0,1:T(8,128)(2,1)} %broadcast_in_dim.71), calls=%async_computation | async-start | bytes 524288 | tf_op jit(solution)/shard_map/all_to_all | solution.py:147
  21.3 15.7 %all-to-all-start.1 = ((bf16[16,4,1536]{2,1,0:T(4,128)(2,1)}), bf16[16,4,1536]{2,1,0:T(4,128)(2,1)S(1)}, u32[]{:S(2)}, u32[]{:S(2)}) async-start(bf16[16,4,1536]{2,1,0:T(4,128)(2,1)} %copy.86), calls=%async_computation.1 | async-start | bytes 393216 | tf_op jit(solution)/shard_map/all_to_all | solution.py:162
  43.6 7.5 %copy-start.2 = (bf16[64,1,192]{0,2,1:T(8,128)(2,1)S(1)}, bf16[64,1,192]{0,2,1:T(8,128)(2,1)}, u32[]{:S(2)}) copy-start(bf16[64,1,192]{0,2,1:T(8,128)(2,1)} %copy.89) | copy-start | bytes 73732
  43.6 7.5 %copy-start.3 = (f32[64,64]{0,1:T(8,128)S(1)}, f32[64,64]{0,1:T(8,128)}, u32[]{:S(2)}) copy-start(f32[64,64]{0,1:T(8,128)} %copy.110) | copy-start | bytes 49156
  49.3 10.5 %copy-start.1 = (pred[64,320]{1,0:T(8,128)(4,1)S(1)}, pred[64,320]{1,0:T(8,128)(4,1)}, u32[]{:S(2)}) copy-start(pred[64,320]{1,0:T(8,128)(4,1)} %slice_compare_fusion) | copy-start | bytes 61444
  52.2 7.8 %copy-start.4 = (f32[64,64]{1,0:T(8,128)S(1)}, f32[64,64]{1,0:T(8,128)}, u32[]{:S(2)}) copy-start(f32[64,64]{1,0:T(8,128)} %get-tuple-element.11) | copy-start | bytes 49156
  62.5 11.3 %all-to-all-start.2 = ((bf16[8,8,1536]{2,1,0:T(8,128)(2,1)}), bf16[8,8,1536]{2,1,0:T(8,128)(2,1)S(1)}, u32[]{:S(2)}, u32[]{:S(2)}) async-start(bf16[8,8,1536]{2,1,0:T(8,128)(2,1)} %fusion.8), calls=%async_computation.2 | async-start | bytes 393216 | tf_op jit(solution)/shard_map/all_to_all | solution.py:179
  77.5 11.3 %all-to-all-start.3 = ((bf16[16,2,1536]{2,1,0:T(2,128)(2,1)}), bf16[16,2,1536]{2,1,0:T(2,128)(2,1)S(1)}, u32[]{:S(2)}, u32[]{:S(2)}) async-start(bf16[16,2,1536]{2,1,0:T(2,128)(2,1)} %copy.100), calls=%async_computation.3 | async-start | bytes 196608 | tf_op jit(solution)/shard_map/all_to_all | solution.py:218
  94.1 11.3 %all-to-all-start.4 = ((bf16[16,2,1536]{2,1,0:T(2,128)(2,1)}), bf16[16,2,1536]{2,1,0:T(2,128)(2,1)S(1)}, u32[]{:S(2)}, u32[]{:S(2)}) async-start(bf16[16,2,1536]{2,1,0:T(2,128)(2,1)} %reshape_transpose_reshape.4), calls=%async_computation.4 | async-start | bytes 196608 | tf_op jit(solution)/shard_map/all_to_all | solution.py:222

commit v10 on v8

--- a/solution.py
+++ b/solution.py
@@ -143,10 +143,8 @@
     n_kv = lax.axis_size("kv")
     local_rows, col_width = hidden.shape
     width = n_kv * col_width
-    spread = jnp.broadcast_to(hidden[:, None], (local_rows, n_kv, col_width))
-    block_rows = lax.all_to_all(spread, "kv", split_axis=1, concat_axis=1, tiled=True).reshape(
-        local_rows, width
-    )
+    spread = jnp.broadcast_to(hidden[None], (n_kv, local_rows, col_width))
+    block_parts = lax.all_to_all(spread, "kv", split_axis=0, concat_axis=0, tiled=True)
     deal = local_rows // n_req
     source_block = (perm // local_rows).reshape(n_req, local_rows)
     source_row = (perm % local_rows).reshape(n_req, local_rows)
@@ -155,10 +153,10 @@
     send_key = jnp.where(mine, rank_sent * local_rows + source_row, -1)
     send_ids = jnp.arange(deal * local_rows, dtype=jnp.int32)
     send_pick = jnp.any(send_key[:, :, None] == send_ids[None, None, :], axis=1)
-    send_pick = send_pick.reshape(n_req * deal, local_rows).astype(hidden.dtype)
-    outgoing_rows = jnp.dot(send_pick, block_rows, preferred_element_type=jnp.float32).astype(
-        hidden.dtype
-    )
+    send_pick = send_pick.reshape(n_req, deal, local_rows).astype(hidden.dtype)
+    outgoing_rows = jnp.einsum(
+        "dir,jrc->dijc", send_pick, block_parts, preferred_element_type=jnp.float32
+    ).astype(hidden.dtype)
     arrived_rows = lax.all_to_all(
         outgoing_rows.reshape(n_req, deal, width), "req", split_axis=0, concat_axis=0, tiled=True
     ).reshape(n_req * deal, width)

time: 107 us -> 106 us (level)
  local copies, waits for them, and re-layouts: 13.9 us -> 12.2 us
    all_to_all x1 -> x0, local copies, waits for them, and re-layouts: 1.1 us -> none  [shards(): lax.all_to_all(spread, 'kv', split_axis=1, concat_axis=1, tiled=True)]
  transfers between devices with their start and end apart: 5 -> 5, of which waited for: 4 -> 4; matrix products, arithmetic and copies ran while one was open for 12% -> 13% of each run, Pallas kernels for 0% -> 0%
where the time goes in v10:
time: 106 us; the launch traced here: 105 us
  waiting for transfers between devices  28.8 us (27%)
  matrix products  25.4 us (24%)
  starting transfers between devices  23.9 us (23%)
  other arithmetic  13.9 us (13%)
  local copies, waits for them, and re-layouts  12.2 us (12%)
    all_to_all x1, waiting for transfers between devices, shards(): lax.all_to_all(outgoing, 'req', split_axis=0, concat_axis=0, tiled=True)  7.65 us
    all_to_all x1, waiting for transfers between devices, shards(): lax.all_to_all(expert_rows, 'req', split_axis=0, concat_axis=0, tiled=True)  7.62 us
    all_to_all x1, waiting for transfers between devices, shards(): lax.all_to_all(outgoing_rows.reshape(n_req, deal, width), 'req', split_ax...  7.37 us
    all_to_all x1, starting transfers between devices, shards(): lax.all_to_all(outgoing_rows.reshape(n_req, deal, width), 'req', split_ax...  7.03 us
    all_to_all x1, waiting for transfers between devices, shards(): lax.all_to_all(partial.reshape(n_kv, sub_rows, partial.shape[1]), 'kv', s...  6.16 us
    dot_general x1, matrix products, attend(): jnp.einsum('pkgd,pkdt->pkgt', page_queries, kv_cache[:, :, :head_dim, :],...  5.64 us
    dot_general x1, matrix products, attend(): jnp.einsum('pkgt,pkdt->pkgd', weights.astype(jnp.bfloat16), kv_cache[:, :...  5.62 us
    all_to_all x1, starting transfers between devices, shards(): lax.all_to_all(spread, 'kv', split_axis=0, concat_axis=0, tiled=True)  5.4 us
  transfers between devices with their start and end apart: 5, of which 4 were waited for; matrix products, arithmetic and copies ran while one was open for 13% of the time, Pallas kernels for 0%

profile of v10, /device:TPU:0, one launch (start us, length us, event | category | flops | bytes accessed | tf_op | source)
XLA Modules:
  0.0 104.5 jit_solution(3667673102605956411)
XLA Ops:
  0.0 1.6 %broadcast_in_dim.65 = bf16[8,64,192]{2,1,0:T(8,128)(2,1)} broadcast(bf16[64,192]{1,0:T(8,128)(2,1)} %param.13), dimensions={1,2} | broadcast | bytes 221184 | tf_op jit(solution)/shard_map/broadcast_in_dim | solution.py:146
  1.6 5.4 %all-to-all-start = ((bf16[8,64,192]{2,1,0:T(8,128)(2,1)}), bf16[8,64,192]{2,1,0:T(8,128)(2,1)S(1)}, u32[]{:S(2)}, u32[]{:S(2)}) async-start(bf16[8,64,192]{2,1,0:T(8,128)(2,1)} %broadcast_in_dim.65), calls=%async_computation | async-start | bytes 524288 | tf_op jit(solution)/shard_map/all_to_all | solution.py:147
  7.7 0.7 broadcast_in_dim.68
  8.7 0.8 convert_convert_fusion
  9.4 0.7 fusion.60
  10.4 1.8 %fusion.6 = f32[67,320]{1,0:T(8,128)S(1)} fusion(s32[2048]{0:T(1024)S(1)} %eq.155, bf16[1,2048]{1,0:T(2,128)(2,1)S(1)} %fusion.62, bf16[1,2048]{1,0:T(2,128)(2,1)S(1)} %get-tuple-element.9, bf16[1,2048]{1,0:T(2,128)(2,1)S(1)} %convert_element_type.164, bf16[64,2048]{1,0:T(8,128)(2,1)} %convert_convert_fusion), kind=kOutput, calls=%fused_computation.10 | convolution fusion | flops 89571328 | bytes 368384 | tf_op jit(solution)/shard_map/dot_general | solution.py:54
  14.3 0.8 and_select_fusion.3
  15.9 0.8 copy.113
  18.5 0.8 add_compare_fusion
  19.6 0.9 reshape.483
  20.5 7.0 %all-to-all-start.1 = ((bf16[16,4,1536]{2,1,0:T(4,128)(2,1)}), bf16[16,4,1536]{2,1,0:T(4,128)(2,1)S(1)}, u32[]{:S(2)}, u32[]{:S(2)}) async-start(bf16[16,4,1536]{2,1,0:T(4,128)(2,1)} %reshape.483), calls=%async_computation.1 | async-start | bytes 393216 | tf_op jit(solution)/shard_map/all_to_all | solution.py:160
  27.5 1.3 %multiply_add_fusion.2 = s32[64]{0:T(128)} fusion(s32[64]{0:T(128)S(1)} %convert_reduce_fusion.1, s32[1024]{0:T(1024)} %param.14, s32[]{:T(128)S(6)} %select_n.121), kind=kLoop, calls=%fused_computation.146 | loop fusion | flops 1088 | bytes 772 | tf_op jit(solution)/shard_map/add | solution.py:167
  28.8 7.4 %all-to-all-done.1 = bf16[16,4,1536]{2,1,0:T(4,128)(2,1)S(1)} async-done(((bf16[16,4,1536]{2,1,0:T(4,128)(2,1)}), bf16[16,4,1536]{2,1,0:T(4,128)(2,1)S(1)}, u32[]{:S(2)}, u32[]{:S(2)}) %all-to-all-start.1) | async-done | bytes 196640 | tf_op jit(solution)/shard_map/all_to_all | solution.py:160
  36.2 0.9 fusion.27
  37.2 1.6 %fusion.19 = bf16[64,1,320]{2,0,1:T(8,128)(2,1)S(1)} fusion(bf16[1,1536,320]{1,2,0:T(8,128)(2,1)} %param.19, bf16[64,1536]{1,0:T(8,128)(2,1)S(1)} %get-tuple-element.18, f32[1536]{0:T(1024)S(1)} %copy-done.5, f32[64]{0:T(128)S(1)} %add_rsqrt_fusion.1), kind=kOutput, calls=%fused_computation.26 | convolution fusion | flops 63328256 | bytes 1227008 | tf_op jit(solution)/shard_map/sd,hdc->shc/dot_general | solution.py:25
  40.2 0.7 copy.105
  40.9 1.0 fusion.53
  41.9 0.9 copy.107
  42.8 5.6 %fusion.80 = (f32[320,3]{1,0:T(8,128)}, f32[320,3,128]{2,1,0:T(4,128)}) fusion(bf16[320,3,64]{2,1,0:T(4,128)(2,1)} %copy.107, bf16[320,1,128,128]{3,2,0,1:T(8,128)(2,1)} %bitcast.95, pred[320,128]{1,0:T(8,128)(4,1)} %add_compare_fusion), kind=kOutput, calls=%fused_computation.151 | convolution fusion | flops 16096320 | bytes 6106880 | tf_op jit(solution)/shard_map/pkgd,pkdt->pkgt/dot_general | solution.py:68
  48.5 1.0 copy.108
  50.5 1.9 %fusion.25 = f32[320,3]{1,0:T(8,128)S(1)} fusion(f32[320,3,128]{2,1,0:T(4,128)} %get-tuple-element.20, f32[320,3]{1,0:T(8,128)S(1)} %copy.109, pred[320,128]{1,0:T(8,128)(4,1)} %add_compare_fusion), kind=kLoop, calls=%fused_computation.39 | loop fusion | flops 367680 | bytes 540160 | tf_op jit(solution)/shard_map/reduce_sum | solution.py:92
  52.4 5.6 %fusion.2 = f32[320,3,64]{2,1,0:T(4,128)S(1)} fusion(bf16[320,1,128,128]{3,2,0,1:T(8,128)(2,1)} %bitcast.96, f32[320,3,128]{2,1,0:T(4,128)} %get-tuple-element.20, f32[320,3]{1,0:T(8,128)S(1)} %copy.109, pred[320,128]{1,0:T(8,128)(4,1)} %add_compare_fusion), kind=kOutput, calls=%fused_computation.4 | convolution fusion | flops 16097280 | bytes 6188800 | tf_op jit(solution)/shard_map/pkgt,pkdt->pkgd/dot_general | solution.py:93
  58.8 2.0 %fusion.7 = bf16[8,8,1536]{2,1,0:T(8,128)(2,1)} fusion(bf16[64,192]{0,1:T(8,128)(2,1)S(1)} %bitcast.92, bf16[1,192,1536]{2,1,0:T(8,128)(2,1)} %param.20), kind=kOutput, calls=%fused_computation.13 | convolution fusion | flops 37847040 | bytes 811008 | tf_op jit(solution)/shard_map/dot_general | solution.py:177
  60.8 4.5 %all-to-all-start.2 = ((bf16[8,8,1536]{2,1,0:T(8,128)(2,1)}), bf16[8,8,1536]{2,1,0:T(8,128)(2,1)S(1)}, u32[]{:S(2)}, u32[]{:S(2)}) async-start(bf16[8,8,1536]{2,1,0:T(8,128)(2,1)} %fusion.7), calls=%async_computation.2 | async-start | bytes 393216 | tf_op jit(solution)/shard_map/all_to_all | solution.py:178
  66.0 6.2 %all-to-all-done.2 = bf16[8,8,1536]{2,1,0:T(8,128)(2,1)S(1)} async-done(((bf16[8,8,1536]{2,1,0:T(8,128)(2,1)}), bf16[8,8,1536]{2,1,0:T(8,128)(2,1)S(1)}, u32[]{:S(2)}, u32[]{:S(2)}) %all-to-all-start.2) | async-done | bytes 196640 | tf_op jit(solution)/shard_map/all_to_all | solution.py:178
  72.3 0.8 fusion.51
  73.1 0.9 fusion.81
  75.8 3.5 %all-to-all-start.3 = ((bf16[16,2,1536]{2,1,0:T(2,128)(2,1)}), bf16[16,2,1536]{2,1,0:T(2,128)(2,1)S(1)}, u32[]{:S(2)}, u32[]{:S(2)}) async-start(bf16[16,2,1536]{2,1,0:T(2,128)(2,1)} %reshape.455), calls=%async_computation.3 | async-start | bytes 196608 | tf_op jit(solution)/shard_map/all_to_all | solution.py:211
  79.4 7.7 %all-to-all-done.3 = bf16[16,2,1536]{2,1,0:T(2,128)(2,1)S(1)} async-done(((bf16[16,2,1536]{2,1,0:T(2,128)(2,1)}), bf16[16,2,1536]{2,1,0:T(2,128)(2,1)S(1)}, u32[]{:S(2)}, u32[]{:S(2)}) %all-to-all-start.3) | async-done | bytes 98336 | tf_op jit(solution)/shard_map/all_to_all | solution.py:211
  87.1 4.0 %fusion.8 = f32[1,32,2048]{2,1,0:T(8,128)S(1)} fusion(bf16[32,1536]{1,0:T(8,128)(2,1)S(1)} %reshape.456, bf16[1,1536,2048]{2,1,0:T(8,128)(2,1)} %param.24), kind=kOutput, calls=%fused_computation.14 | convolution fusion | flops 201326592 | bytes 6651904 | tf_op jit(solution)/shard_map/erd,edf->erf/dot_general | solution.py:114
  92.4 3.5 %all-to-all-start.4 = ((bf16[16,2,1536]{2,1,0:T(2,128)(2,1)}), bf16[16,2,1536]{2,1,0:T(2,128)(2,1)S(1)}, u32[]{:S(2)}, u32[]{:S(2)}) async-start(bf16[16,2,1536]{2,1,0:T(2,128)(2,1)} %reshape_transpose_reshape.4), calls=%async_computation.4 | async-start | bytes 196608 | tf_op jit(solution)/shard_map/all_to_all | solution.py:215
  96.0 7.6 %all-to-all-done.4 = bf16[16,2,1536]{2,1,0:T(2,128)(2,1)S(1)} async-done(((bf16[16,2,1536]{2,1,0:T(2,128)(2,1)}), bf16[16,2,1536]{2,1,0:T(2,128)(2,1)S(1)}, u32[]{:S(2)}, u32[]{:S(2)}) %all-to-all-start.4) | async-done | bytes 98336 | tf_op jit(solution)/shard_map/all_to_all | solution.py:215
  (90 shorter events, 14.4 us)
Async XLA Ops:
  0.0 91.1 %copy-start = (bf16[1,1024,1536]{2,1,0:T(8,128)(2,1)S(1)}, bf16[1,1024,1536]{2,1,0:T(8,128)(2,1)}, u32[]{:S(2)}) copy-start(bf16[1,1024,1536]{2,1,0:T(8,128)(2,1)} %param.25) | copy-start | bytes 9437188
  0.0 37.2 %copy-start.5 = (f32[1536]{0:T(1024)S(1)}, f32[1536]{0:T(1024)}, u32[]{:S(2)}) copy-start(f32[1536]{0:T(1024)} %param.18) | copy-start | bytes 18436
  1.6 17.6 %all-to-all-start = ((bf16[8,64,192]{2,1,0:T(8,128)(2,1)}), bf16[8,64,192]{2,1,0:T(8,128)(2,1)S(1)}, u32[]{:S(2)}, u32[]{:S(2)}) async-start(bf16[8,64,192]{2,1,0:T(8,128)(2,1)} %broadcast_in_dim.65), calls=%async_computation | async-start | bytes 524288 | tf_op jit(solution)/shard_map/all_to_all | solution.py:147
  16.8 12.0 %copy-start.6 = (s32[16]{0:T(128)}, s32[16]{0:T(128)S(1)}, u32[]{:S(2)}) copy-start(s32[16]{0:T(128)S(1)} %eq.159) | copy-start | bytes 196
  17.1 0.5 copy-start.8
  20.5 15.7 %all-to-all-start.1 = ((bf16[16,4,1536]{2,1,0:T(4,128)(2,1)}), bf16[16,4,1536]{2,1,0:T(4,128)(2,1)S(1)}, u32[]{:S(2)}, u32[]{:S(2)}) async-start(bf16[16,4,1536]{2,1,0:T(4,128)(2,1)} %reshape.483), calls=%async_computation.1 | async-start | bytes 393216 | tf_op jit(solution)/shard_map/all_to_all | solution.py:160
  37.2 12.3 %copy-start.1 = (pred[64,320]{1,0:T(8,128)(4,1)S(1)}, pred[64,320]{1,0:T(8,128)(4,1)}, u32[]{:S(2)}) copy-start(pred[64,320]{1,0:T(8,128)(4,1)} %slice_compare_fusion) | copy-start | bytes 61444
  42.8 6.8 %copy-start.2 = (bf16[64,1,192]{0,2,1:T(8,128)(2,1)S(1)}, bf16[64,1,192]{0,2,1:T(8,128)(2,1)}, u32[]{:S(2)}) copy-start(bf16[64,1,192]{0,2,1:T(8,128)(2,1)} %copy.105) | copy-start | bytes 73732
  42.8 6.8 %copy-start.3 = (f32[64,64]{0,1:T(8,128)S(1)}, f32[64,64]{0,1:T(8,128)}, u32[]{:S(2)}) copy-start(f32[64,64]{0,1:T(8,128)} %copy.134) | copy-start | bytes 49156
  50.5 7.8 %copy-start.7 = (bf16[64,1,3]{0,2,1:T(4,128)(2,1)S(1)}, bf16[64,1,3]{0,2,1:T(4,128)(2,1)}, u32[]{:S(2)}) copy-start(bf16[64,1,3]{0,2,1:T(4,128)(2,1)} %get-tuple-element.15) | copy-start | bytes 1156
  50.5 7.8 %copy-start.4 = (f32[64,64]{1,0:T(8,128)S(1)}, f32[64,64]{1,0:T(8,128)}, u32[]{:S(2)}) copy-start(f32[64,64]{1,0:T(8,128)} %get-tuple-element.11) | copy-start | bytes 49156
  60.8 11.3 %all-to-all-start.2 = ((bf16[8,8,1536]{2,1,0:T(8,128)(2,1)}), bf16[8,8,1536]{2,1,0:T(8,128)(2,1)S(1)}, u32[]{:S(2)}, u32[]{:S(2)}) async-start(bf16[8,8,1536]{2,1,0:T(8,128)(2,1)} %fusion.7), calls=%async_computation.2 | async-start | bytes 393216 | tf_op jit(solution)/shard_map/all_to_all | solution.py:178
  75.8 11.3 %all-to-all-start.3 = ((bf16[16,2,1536]{2,1,0:T(2,128)(2,1)}), bf16[16,2,1536]{2,1,0:T(2,128)(2,1)S(1)}, u32[]{:S(2)}, u32[]{:S(2)}) async-start(bf16[16,2,1536]{2,1,0:T(2,128)(2,1)} %reshape.455), calls=%async_computation.3 | async-start | bytes 196608 | tf_op jit(solution)/shard_map/all_to_all | solution.py:211
  87.1 16.6 %copy-start.9 = (s32[8,2]{0,1:T(2,128)S(1)}, s32[8,2]{0,1:T(2,128)}, u32[]{:S(2)}) copy-start(s32[8,2]{0,1:T(2,128)} %copy.121) | copy-start | bytes 196
  92.4 11.3 %all-to-all-start.4 = ((bf16[16,2,1536]{2,1,0:T(2,128)(2,1)}), bf16[16,2,1536]{2,1,0:T(2,128)(2,1)S(1)}, u32[]{:S(2)}, u32[]{:S(2)}) async-start(bf16[16,2,1536]{2,1,0:T(2,128)(2,1)} %reshape_transpose_reshape.4), calls=%async_computation.4 | async-start | bytes 196608 | tf_op jit(solution)/shard_map/all_to_all | solution.py:215

commit v11 on v10

--- a/solution.py
+++ b/solution.py
@@ -90,9 +90,10 @@
         0.0,
     )
     page_total = jnp.sum(weights, axis=3)
+    rounded_weights = lax.optimization_barrier(weights.astype(jnp.bfloat16))
     page_value = jnp.einsum(
         "pkgt,pkdt->pkgd",
-        weights.astype(jnp.bfloat16),
+        rounded_weights,
         kv_cache[:, :, head_dim:, :],
         preferred_element_type=jnp.float32,
     )

time: 106 us -> 105 us (level)
  no operation moved by 1% of the time
where the time goes in v11:
time: 105 us; the launch traced here: 104 us
  waiting for transfers between devices  28.8 us (27%)
  matrix products  25.1 us (24%)
  starting transfers between devices  23.9 us (23%)
  other arithmetic  13.9 us (13%)
  local copies, waits for them, and re-layouts  12.2 us (12%)
    all_to_all x1, waiting for transfers between devices, shards(): lax.all_to_all(outgoing, 'req', split_axis=0, concat_axis=0, tiled=True)  7.65 us
    all_to_all x1, waiting for transfers between devices, shards(): lax.all_to_all(expert_rows, 'req', split_axis=0, concat_axis=0, tiled=True)  7.62 us
    all_to_all x1, waiting for transfers between devices, shards(): lax.all_to_all(outgoing_rows.reshape(n_req, deal, width), 'req', split_ax...  7.37 us
    all_to_all x1, starting transfers between devices, shards(): lax.all_to_all(outgoing_rows.reshape(n_req, deal, width), 'req', split_ax...  7.03 us
    all_to_all x1, waiting for transfers between devices, shards(): lax.all_to_all(partial.reshape(n_kv, sub_rows, partial.shape[1]), 'kv', s...  6.16 us
    dot_general x1, matrix products, attend(): jnp.einsum('pkgd,pkdt->pkgt', page_queries, kv_cache[:, :, :head_dim, :],...  5.64 us
    all_to_all x1, starting transfers between devices, shards(): lax.all_to_all(spread, 'kv', split_axis=0, concat_axis=0, tiled=True)  5.4 us
    dot_general x1, matrix products, attend(): jnp.einsum('pkgt,pkdt->pkgd', rounded_weights, kv_cache[:, :, head_dim:,...  5.36 us
  transfers between devices with their start and end apart: 5, of which 4 were waited for; matrix products, arithmetic and copies ran while one was open for 13% of the time, Pallas kernels for 0%

profile of v11, /device:TPU:0, one launch (start us, length us, event | category | flops | bytes accessed | tf_op | source)
XLA Modules:
  0.0 104.3 jit_solution(4447939729904486734)
XLA Ops:
  0.0 1.6 %broadcast_in_dim.65 = bf16[8,64,192]{2,1,0:T(8,128)(2,1)} broadcast(bf16[64,192]{1,0:T(8,128)(2,1)} %param.13), dimensions={1,2} | broadcast | bytes 221184 | tf_op jit(solution)/shard_map/broadcast_in_dim | solution.py:147
  1.6 5.4 %all-to-all-start = ((bf16[8,64,192]{2,1,0:T(8,128)(2,1)}), bf16[8,64,192]{2,1,0:T(8,128)(2,1)S(1)}, u32[]{:S(2)}, u32[]{:S(2)}) async-start(bf16[8,64,192]{2,1,0:T(8,128)(2,1)} %broadcast_in_dim.65), calls=%async_computation | async-start | bytes 524288 | tf_op jit(solution)/shard_map/all_to_all | solution.py:148
  7.7 0.7 broadcast_in_dim.68
  8.7 0.8 convert_convert_fusion
  9.4 0.7 fusion.58
  10.4 1.8 %fusion.6 = f32[67,320]{1,0:T(8,128)S(1)} fusion(s32[2048]{0:T(1024)S(1)} %eq.155, bf16[1,2048]{1,0:T(2,128)(2,1)S(1)} %fusion.60, bf16[1,2048]{1,0:T(2,128)(2,1)S(1)} %get-tuple-element.9, bf16[1,2048]{1,0:T(2,128)(2,1)S(1)} %convert_element_type.166, bf16[64,2048]{1,0:T(8,128)(2,1)} %convert_convert_fusion), kind=kOutput, calls=%fused_computation.10 | convolution fusion | flops 89571328 | bytes 368384 | tf_op jit(solution)/shard_map/dot_general | solution.py:54
  14.3 0.8 and_select_fusion.3
  15.9 0.8 copy.113
  18.5 0.8 add_compare_fusion
  19.6 0.9 reshape.485
  20.5 7.0 %all-to-all-start.1 = ((bf16[16,4,1536]{2,1,0:T(4,128)(2,1)}), bf16[16,4,1536]{2,1,0:T(4,128)(2,1)S(1)}, u32[]{:S(2)}, u32[]{:S(2)}) async-start(bf16[16,4,1536]{2,1,0:T(4,128)(2,1)} %reshape.485), calls=%async_computation.1 | async-start | bytes 393216 | tf_op jit(solution)/shard_map/all_to_all | solution.py:161
  27.5 1.3 %multiply_add_fusion.2 = s32[64]{0:T(128)} fusion(s32[64]{0:T(128)S(1)} %convert_reduce_fusion.1, s32[1024]{0:T(1024)} %param.14, s32[]{:T(128)S(6)} %select_n.121), kind=kLoop, calls=%fused_computation.145 | loop fusion | flops 1088 | bytes 772 | tf_op jit(solution)/shard_map/add | solution.py:168
  28.8 7.4 %all-to-all-done.1 = bf16[16,4,1536]{2,1,0:T(4,128)(2,1)S(1)} async-done(((bf16[16,4,1536]{2,1,0:T(4,128)(2,1)}), bf16[16,4,1536]{2,1,0:T(4,128)(2,1)S(1)}, u32[]{:S(2)}, u32[]{:S(2)}) %all-to-all-start.1) | async-done | bytes 196640 | tf_op jit(solution)/shard_map/all_to_all | solution.py:161
  36.2 0.9 fusion.27
  37.2 1.6 %fusion.19 = bf16[64,1,320]{2,0,1:T(8,128)(2,1)S(1)} fusion(bf16[1,1536,320]{1,2,0:T(8,128)(2,1)} %param.19, bf16[64,1536]{1,0:T(8,128)(2,1)S(1)} %get-tuple-element.20, f32[1536]{0:T(1024)S(1)} %copy-done.5, f32[64]{0:T(128)S(1)} %add_rsqrt_fusion.1), kind=kOutput, calls=%fused_computation.26 | convolution fusion | flops 63328256 | bytes 1227008 | tf_op jit(solution)/shard_map/sd,hdc->shc/dot_general | solution.py:25
  40.2 0.7 copy.105
  40.9 1.0 fusion.51
  41.9 0.9 copy.107
  42.8 5.6 %fusion.77 = (f32[320,3]{1,0:T(8,128)}, f32[320,3,128]{2,1,0:T(4,128)}) fusion(bf16[320,3,64]{2,1,0:T(4,128)(2,1)} %copy.107, bf16[320,1,128,128]{3,2,0,1:T(8,128)(2,1)} %bitcast.96, pred[320,128]{1,0:T(8,128)(4,1)} %add_compare_fusion), kind=kOutput, calls=%fused_computation.149 | convolution fusion | flops 16096320 | bytes 6106880 | tf_op jit(solution)/shard_map/pkgd,pkdt->pkgt/dot_general | solution.py:68
  48.5 1.0 copy.108
  50.5 1.9 %fusion.25 = (f32[320,3]{1,0:T(8,128)S(1)}, bf16[320,1,3,128]{3,2,0,1:T(4,128)(2,1)S(1)}) fusion(f32[320,3,128]{2,1,0:T(4,128)} %get-tuple-element.22, f32[320,3]{1,0:T(8,128)S(1)} %copy.109, pred[320,128]{1,0:T(8,128)(4,1)} %add_compare_fusion), kind=kLoop, calls=%fused_computation.39 | loop fusion | flops 490560 | bytes 785920 | tf_op jit(solution)/shard_map/reduce_sum | solution.py:92
  52.7 5.4 %fusion.2 = f32[320,3,64]{2,1,0:T(4,128)S(1)} fusion(bf16[320,1,128,128]{3,2,0,1:T(8,128)(2,1)} %bitcast.97, bf16[320,1,3,128]{3,2,0,1:T(4,128)(2,1)S(1)} %get-tuple-element.12), kind=kOutput, calls=%fused_computation.4 | convolution fusion | flops 15728640 | bytes 5734400 | tf_op jit(solution)/shard_map/pkgt,pkdt->pkgd/dot_general | solution.py:94
  58.5 2.0 %fusion.7 = bf16[8,8,1536]{2,1,0:T(8,128)(2,1)} fusion(bf16[64,192]{0,1:T(8,128)(2,1)S(1)} %bitcast.99, bf16[1,192,1536]{2,1,0:T(8,128)(2,1)} %param.20), kind=kOutput, calls=%fused_computation.13 | convolution fusion | flops 37847040 | bytes 811008 | tf_op jit(solution)/shard_map/dot_general | solution.py:178
  60.5 4.5 %all-to-all-start.2 = ((bf16[8,8,1536]{2,1,0:T(8,128)(2,1)}), bf16[8,8,1536]{2,1,0:T(8,128)(2,1)S(1)}, u32[]{:S(2)}, u32[]{:S(2)}) async-start(bf16[8,8,1536]{2,1,0:T(8,128)(2,1)} %fusion.7), calls=%async_computation.2 | async-start | bytes 393216 | tf_op jit(solution)/shard_map/all_to_all | solution.py:179
  65.7 6.2 %all-to-all-done.2 = bf16[8,8,1536]{2,1,0:T(8,128)(2,1)S(1)} async-done(((bf16[8,8,1536]{2,1,0:T(8,128)(2,1)}), bf16[8,8,1536]{2,1,0:T(8,128)(2,1)S(1)}, u32[]{:S(2)}, u32[]{:S(2)}) %all-to-all-start.2) | async-done | bytes 196640 | tf_op jit(solution)/shard_map/all_to_all | solution.py:179
  72.1 0.8 fusion.49
  72.8 0.9 fusion.78
  75.5 3.5 %all-to-all-start.3 = ((bf16[16,2,1536]{2,1,0:T(2,128)(2,1)}), bf16[16,2,1536]{2,1,0:T(2,128)(2,1)S(1)}, u32[]{:S(2)}, u32[]{:S(2)}) async-start(bf16[16,2,1536]{2,1,0:T(2,128)(2,1)} %reshape.457), calls=%async_computation.3 | async-start | bytes 196608 | tf_op jit(solution)/shard_map/all_to_all | solution.py:212
  79.1 7.7 %all-to-all-done.3 = bf16[16,2,1536]{2,1,0:T(2,128)(2,1)S(1)} async-done(((bf16[16,2,1536]{2,1,0:T(2,128)(2,1)}), bf16[16,2,1536]{2,1,0:T(2,128)(2,1)S(1)}, u32[]{:S(2)}, u32[]{:S(2)}) %all-to-all-start.3) | async-done | bytes 98336 | tf_op jit(solution)/shard_map/all_to_all | solution.py:212
  86.8 4.0 %fusion.8 = f32[1,32,2048]{2,1,0:T(8,128)S(1)} fusion(bf16[32,1536]{1,0:T(8,128)(2,1)S(1)} %reshape.458, bf16[1,1536,2048]{2,1,0:T(8,128)(2,1)} %param.24), kind=kOutput, calls=%fused_computation.14 | convolution fusion | flops 201326592 | bytes 6651904 | tf_op jit(solution)/shard_map/erd,edf->erf/dot_general | solution.py:115
  92.1 3.5 %all-to-all-start.4 = ((bf16[16,2,1536]{2,1,0:T(2,128)(2,1)}), bf16[16,2,1536]{2,1,0:T(2,128)(2,1)S(1)}, u32[]{:S(2)}, u32[]{:S(2)}) async-start(bf16[16,2,1536]{2,1,0:T(2,128)(2,1)} %reshape_transpose_reshape.4), calls=%async_computation.4 | async-start | bytes 196608 | tf_op jit(solution)/shard_map/all_to_all | solution.py:216
  95.8 7.6 %all-to-all-done.4 = bf16[16,2,1536]{2,1,0:T(2,128)(2,1)S(1)} async-done(((bf16[16,2,1536]{2,1,0:T(2,128)(2,1)}), bf16[16,2,1536]{2,1,0:T(2,128)(2,1)S(1)}, u32[]{:S(2)}, u32[]{:S(2)}) %all-to-all-start.4) | async-done | bytes 98336 | tf_op jit(solution)/shard_map/all_to_all | solution.py:216
  (90 shorter events, 14.3 us)
Async XLA Ops:
  0.0 90.8 %copy-start = (bf16[1,1024,1536]{2,1,0:T(8,128)(2,1)S(1)}, bf16[1,1024,1536]{2,1,0:T(8,128)(2,1)}, u32[]{:S(2)}) copy-start(bf16[1,1024,1536]{2,1,0:T(8,128)(2,1)} %param.25) | copy-start | bytes 9437188
  0.0 37.2 %copy-start.5 = (f32[1536]{0:T(1024)S(1)}, f32[1536]{0:T(1024)}, u32[]{:S(2)}) copy-start(f32[1536]{0:T(1024)} %param.18) | copy-start | bytes 18436
  1.6 17.6 %all-to-all-start = ((bf16[8,64,192]{2,1,0:T(8,128)(2,1)}), bf16[8,64,192]{2,1,0:T(8,128)(2,1)S(1)}, u32[]{:S(2)}, u32[]{:S(2)}) async-start(bf16[8,64,192]{2,1,0:T(8,128)(2,1)} %broadcast_in_dim.65), calls=%async_computation | async-start | bytes 524288 | tf_op jit(solution)/shard_map/all_to_all | solution.py:148
  16.8 12.0 %copy-start.6 = (s32[16]{0:T(128)}, s32[16]{0:T(128)S(1)}, u32[]{:S(2)}) copy-start(s32[16]{0:T(128)S(1)} %eq.159) | copy-start | bytes 196
  17.1 0.5 copy-start.8
  20.5 15.7 %all-to-all-start.1 = ((bf16[16,4,1536]{2,1,0:T(4,128)(2,1)}), bf16[16,4,1536]{2,1,0:T(4,128)(2,1)S(1)}, u32[]{:S(2)}, u32[]{:S(2)}) async-start(bf16[16,4,1536]{2,1,0:T(4,128)(2,1)} %reshape.485), calls=%async_computation.1 | async-start | bytes 393216 | tf_op jit(solution)/shard_map/all_to_all | solution.py:161
  37.2 12.3 %copy-start.1 = (pred[64,320]{1,0:T(8,128)(4,1)S(1)}, pred[64,320]{1,0:T(8,128)(4,1)}, u32[]{:S(2)}) copy-start(pred[64,320]{1,0:T(8,128)(4,1)} %slice_compare_fusion) | copy-start | bytes 61444
  42.8 6.8 %copy-start.2 = (bf16[64,1,192]{0,2,1:T(8,128)(2,1)S(1)}, bf16[64,1,192]{0,2,1:T(8,128)(2,1)}, u32[]{:S(2)}) copy-start(bf16[64,1,192]{0,2,1:T(8,128)(2,1)} %copy.105) | copy-start | bytes 73732
  42.8 6.8 %copy-start.3 = (f32[64,64]{0,1:T(8,128)S(1)}, f32[64,64]{0,1:T(8,128)}, u32[]{:S(2)}) copy-start(f32[64,64]{0,1:T(8,128)} %copy.134) | copy-start | bytes 49156
  50.5 7.6 %copy-start.7 = (bf16[64,1,3]{0,2,1:T(4,128)(2,1)S(1)}, bf16[64,1,3]{0,2,1:T(4,128)(2,1)}, u32[]{:S(2)}) copy-start(bf16[64,1,3]{0,2,1:T(4,128)(2,1)} %get-tuple-element.17) | copy-start | bytes 1156
  50.5 7.6 %copy-start.4 = (f32[64,64]{1,0:T(8,128)S(1)}, f32[64,64]{1,0:T(8,128)}, u32[]{:S(2)}) copy-start(f32[64,64]{1,0:T(8,128)} %get-tuple-element.13) | copy-start | bytes 49156
  60.5 11.3 %all-to-all-start.2 = ((bf16[8,8,1536]{2,1,0:T(8,128)(2,1)}), bf16[8,8,1536]{2,1,0:T(8,128)(2,1)S(1)}, u32[]{:S(2)}, u32[]{:S(2)}) async-start(bf16[8,8,1536]{2,1,0:T(8,128)(2,1)} %fusion.7), calls=%async_computation.2 | async-start | bytes 393216 | tf_op jit(solution)/shard_map/all_to_all | solution.py:179
  75.5 11.3 %all-to-all-start.3 = ((bf16[16,2,1536]{2,1,0:T(2,128)(2,1)}), bf16[16,2,1536]{2,1,0:T(2,128)(2,1)S(1)}, u32[]{:S(2)}, u32[]{:S(2)}) async-start(bf16[16,2,1536]{2,1,0:T(2,128)(2,1)} %reshape.457), calls=%async_computation.3 | async-start | bytes 196608 | tf_op jit(solution)/shard_map/all_to_all | solution.py:212
  86.8 16.6 %copy-start.9 = (s32[8,2]{0,1:T(2,128)S(1)}, s32[8,2]{0,1:T(2,128)}, u32[]{:S(2)}) copy-start(s32[8,2]{0,1:T(2,128)} %copy.121) | copy-start | bytes 196
  92.1 11.3 %all-to-all-start.4 = ((bf16[16,2,1536]{2,1,0:T(2,128)(2,1)}), bf16[16,2,1536]{2,1,0:T(2,128)(2,1)S(1)}, u32[]{:S(2)}, u32[]{:S(2)}) async-start(bf16[16,2,1536]{2,1,0:T(2,128)(2,1)} %reshape_transpose_reshape.4), calls=%async_computation.4 | async-start | bytes 196608 | tf_op jit(solution)/shard_map/all_to_all | solution.py:216

commit v12 on v11

--- a/solution.py
+++ b/solution.py
@@ -147,8 +147,9 @@
     spread = jnp.broadcast_to(hidden[None], (n_kv, local_rows, col_width))
     block_parts = lax.all_to_all(spread, "kv", split_axis=0, concat_axis=0, tiled=True)
     deal = local_rows // n_req
-    source_block = (perm // local_rows).reshape(n_req, local_rows)
-    source_row = (perm % local_rows).reshape(n_req, local_rows)
+    perm_blocks = perm.reshape(n_req, local_rows)
+    source_block = perm_blocks // local_rows
+    source_row = perm_blocks - source_block * local_rows
     mine = source_block == req_index
     rank_sent = jnp.cumsum(mine.astype(jnp.int32), axis=1) - 1
     send_key = jnp.where(mine, rank_sent * local_rows + source_row, -1)
@@ -161,7 +162,7 @@
     arrived_rows = lax.all_to_all(
         outgoing_rows.reshape(n_req, deal, width), "req", split_axis=0, concat_axis=0, tiled=True
     ).reshape(n_req * deal, width)
-    my_source = lax.dynamic_slice_in_dim(perm, req_index * local_rows, local_rows) // local_rows
+    my_source = lax.dynamic_slice_in_dim(source_block, req_index, 1, 0).reshape(local_rows)
     slot_ids = jnp.arange(local_rows, dtype=jnp.int32)
     same_before = (my_source[None, :] == my_source[:, None]) & (slot_ids[None, :] < slot_ids[:, None])
     rank_got = jnp.sum(same_before.astype(jnp.int32), axis=1)

time: 105 us -> 103 us (0.981)
  other arithmetic: 13.9 us -> 11.1 us
    select_n x3 -> x1, other arithmetic: 1.47 us -> 0.02 us  [shards(): source_block = perm_blocks // local_rows]
  transfers between devices with their start and end apart: 5 -> 5, of which waited for: 4 -> 4; matrix products, arithmetic and copies ran while one was open for 13% -> 11% of each run, Pallas kernels for 0% -> 0%
where the time goes in v12:
time: 103 us; the launch traced here: 102 us
  waiting for transfers between devices  29.6 us (29%)
  matrix products  25.1 us (24%)
  starting transfers between devices  23.9 us (23%)
  local copies, waits for them, and re-layouts  11.6 us (11%)
  other arithmetic  11.1 us (11%)
    all_to_all x1, waiting for transfers between devices, shards(): lax.all_to_all(outgoing_rows.reshape(n_req, deal, width), 'req', split_ax...  8.13 us
    all_to_all x1, waiting for transfers between devices, shards(): lax.all_to_all(outgoing, 'req', split_axis=0, concat_axis=0, tiled=True)  7.65 us
    all_to_all x1, waiting for transfers between devices, shards(): lax.all_to_all(expert_rows, 'req', split_axis=0, concat_axis=0, tiled=True)  7.62 us
    all_to_all x1, starting transfers between devices, shards(): lax.all_to_all(outgoing_rows.reshape(n_req, deal, width), 'req', split_ax...  7.03 us
    all_to_all x1, waiting for transfers between devices, shards(): lax.all_to_all(partial.reshape(n_kv, sub_rows, partial.shape[1]), 'kv', s...  6.16 us
    dot_general x1, matrix products, attend(): jnp.einsum('pkgd,pkdt->pkgt', page_queries, kv_cache[:, :, :head_dim, :],...  5.62 us
    all_to_all x1, starting transfers between devices, shards(): lax.all_to_all(spread, 'kv', split_axis=0, concat_axis=0, tiled=True)  5.4 us
    dot_general x1, matrix products, attend(): jnp.einsum('pkgt,pkdt->pkgd', rounded_weights, kv_cache[:, :, head_dim:,...  5.36 us
  transfers between devices with their start and end apart: 5, of which 4 were waited for; matrix products, arithmetic and copies ran while one was open for 11% of the time, Pallas kernels for 0%

profile of v12, /device:TPU:0, one launch (start us, length us, event | category | flops | bytes accessed | tf_op | source)
XLA Modules:
  0.0 101.6 jit_solution(2703293100978177524)
XLA Ops:
  0.0 1.6 %broadcast_in_dim.65 = bf16[8,64,192]{2,1,0:T(8,128)(2,1)} broadcast(bf16[64,192]{1,0:T(8,128)(2,1)} %param.13), dimensions={1,2} | broadcast | bytes 221184 | tf_op jit(solution)/shard_map/broadcast_in_dim | solution.py:147
  1.6 5.4 %all-to-all-start = ((bf16[8,64,192]{2,1,0:T(8,128)(2,1)}), bf16[8,64,192]{2,1,0:T(8,128)(2,1)S(1)}, u32[]{:S(2)}, u32[]{:S(2)}) async-start(bf16[8,64,192]{2,1,0:T(8,128)(2,1)} %broadcast_in_dim.65), calls=%async_computation | async-start | bytes 524288 | tf_op jit(solution)/shard_map/all_to_all | solution.py:148
  7.7 0.7 broadcast_in_dim.68
  8.7 0.8 convert_convert_fusion
  9.4 0.7 fusion.58
  10.4 1.8 %fusion.6 = f32[67,320]{1,0:T(8,128)S(1)} fusion(s32[2048]{0:T(1024)S(1)} %eq.149, bf16[1,2048]{1,0:T(2,128)(2,1)S(1)} %fusion.61, bf16[1,2048]{1,0:T(2,128)(2,1)S(1)} %get-tuple-element.9, bf16[1,2048]{1,0:T(2,128)(2,1)S(1)} %convert_element_type.166, bf16[64,2048]{1,0:T(8,128)(2,1)} %convert_convert_fusion), kind=kOutput, calls=%fused_computation.10 | convolution fusion | flops 89571328 | bytes 368384 | tf_op jit(solution)/shard_map/dot_general | solution.py:54
  12.9 0.8 reshape.497
  14.4 0.8 copy.113
  17.0 0.8 add_compare_fusion
  18.0 0.9 reshape.541
  19.0 7.0 %all-to-all-start.1 = ((bf16[16,4,1536]{2,1,0:T(4,128)(2,1)}), bf16[16,4,1536]{2,1,0:T(4,128)(2,1)S(1)}, u32[]{:S(2)}, u32[]{:S(2)}) async-start(bf16[16,4,1536]{2,1,0:T(4,128)(2,1)} %reshape.541), calls=%async_computation.1 | async-start | bytes 393216 | tf_op jit(solution)/shard_map/all_to_all | solution.py:162
  26.5 8.1 %all-to-all-done.1 = bf16[16,4,1536]{2,1,0:T(4,128)(2,1)S(1)} async-done(((bf16[16,4,1536]{2,1,0:T(4,128)(2,1)}), bf16[16,4,1536]{2,1,0:T(4,128)(2,1)S(1)}, u32[]{:S(2)}, u32[]{:S(2)}) %all-to-all-start.1) | async-done | bytes 196640 | tf_op jit(solution)/shard_map/all_to_all | solution.py:162
  34.7 0.9 fusion.27
  35.7 1.6 %fusion.19 = bf16[64,1,320]{2,0,1:T(8,128)(2,1)S(1)} fusion(bf16[1,1536,320]{1,2,0:T(8,128)(2,1)} %param.19, bf16[64,1536]{1,0:T(8,128)(2,1)S(1)} %get-tuple-element.22, f32[1536]{0:T(1024)S(1)} %copy-done.5, f32[64]{0:T(128)S(1)} %add_rsqrt_fusion.1), kind=kOutput, calls=%fused_computation.26 | convolution fusion | flops 63328256 | bytes 1227008 | tf_op jit(solution)/shard_map/sd,hdc->shc/dot_general | solution.py:25
  37.3 0.7 fusion.55
  38.0 1.0 fusion.51
  39.0 0.9 copy.107
  40.0 5.6 %fusion.77 = (f32[320,3]{1,0:T(8,128)}, f32[320,3,128]{2,1,0:T(4,128)}) fusion(bf16[320,3,64]{2,1,0:T(4,128)(2,1)} %copy.107, bf16[320,1,128,128]{3,2,0,1:T(8,128)(2,1)} %bitcast.100, pred[320,128]{1,0:T(8,128)(4,1)} %add_compare_fusion), kind=kOutput, calls=%fused_computation.146 | convolution fusion | flops 16096320 | bytes 6106880 | tf_op jit(solution)/shard_map/pkgd,pkdt->pkgt/dot_general | solution.py:68
  45.6 1.0 copy.108
  47.9 1.9 %fusion.25 = (f32[320,3]{1,0:T(8,128)S(1)}, bf16[320,1,3,128]{3,2,0,1:T(4,128)(2,1)S(1)}) fusion(f32[320,3,128]{2,1,0:T(4,128)} %get-tuple-element.24, f32[320,3]{1,0:T(8,128)S(1)} %copy.109, pred[320,128]{1,0:T(8,128)(4,1)} %add_compare_fusion), kind=kLoop, calls=%fused_computation.39 | loop fusion | flops 490560 | bytes 785920 | tf_op jit(solution)/shard_map/reduce_sum | solution.py:92
  50.0 5.4 %fusion.2 = f32[320,3,64]{2,1,0:T(4,128)S(1)} fusion(bf16[320,1,128,128]{3,2,0,1:T(8,128)(2,1)} %bitcast.101, bf16[320,1,3,128]{3,2,0,1:T(4,128)(2,1)S(1)} %get-tuple-element.12), kind=kOutput, calls=%fused_computation.4 | convolution fusion | flops 15728640 | bytes 5734400 | tf_op jit(solution)/shard_map/pkgt,pkdt->pkgd/dot_general | solution.py:94
  55.9 2.0 %fusion.7 = bf16[8,8,1536]{2,1,0:T(8,128)(2,1)} fusion(bf16[64,192]{0,1:T(8,128)(2,1)S(1)} %bitcast.103, bf16[1,192,1536]{2,1,0:T(8,128)(2,1)} %param.20), kind=kOutput, calls=%fused_computation.13 | convolution fusion | flops 37847040 | bytes 811008 | tf_op jit(solution)/shard_map/dot_general | solution.py:179
  57.9 4.5 %all-to-all-start.2 = ((bf16[8,8,1536]{2,1,0:T(8,128)(2,1)}), bf16[8,8,1536]{2,1,0:T(8,128)(2,1)S(1)}, u32[]{:S(2)}, u32[]{:S(2)}) async-start(bf16[8,8,1536]{2,1,0:T(8,128)(2,1)} %fusion.7), calls=%async_computation.2 | async-start | bytes 393216 | tf_op jit(solution)/shard_map/all_to_all | solution.py:180
  63.0 6.2 %all-to-all-done.2 = bf16[8,8,1536]{2,1,0:T(8,128)(2,1)S(1)} async-done(((bf16[8,8,1536]{2,1,0:T(8,128)(2,1)}), bf16[8,8,1536]{2,1,0:T(8,128)(2,1)S(1)}, u32[]{:S(2)}, u32[]{:S(2)}) %all-to-all-start.2) | async-done | bytes 196640 | tf_op jit(solution)/shard_map/all_to_all | solution.py:180
  69.4 0.8 fusion.49
  70.2 0.9 fusion.78
  72.8 3.5 %all-to-all-start.3 = ((bf16[16,2,1536]{2,1,0:T(2,128)(2,1)}), bf16[16,2,1536]{2,1,0:T(2,128)(2,1)S(1)}, u32[]{:S(2)}, u32[]{:S(2)}) async-start(bf16[16,2,1536]{2,1,0:T(2,128)(2,1)} %reshape.513), calls=%async_computation.3 | async-start | bytes 196608 | tf_op jit(solution)/shard_map/all_to_all | solution.py:213
  76.5 7.7 %all-to-all-done.3 = bf16[16,2,1536]{2,1,0:T(2,128)(2,1)S(1)} async-done(((bf16[16,2,1536]{2,1,0:T(2,128)(2,1)}), bf16[16,2,1536]{2,1,0:T(2,128)(2,1)S(1)}, u32[]{:S(2)}, u32[]{:S(2)}) %all-to-all-start.3) | async-done | bytes 98336 | tf_op jit(solution)/shard_map/all_to_all | solution.py:213
  84.2 4.0 %fusion.8 = f32[1,32,2048]{2,1,0:T(8,128)S(1)} fusion(bf16[32,1536]{1,0:T(8,128)(2,1)S(1)} %reshape.514, bf16[1,1536,2048]{2,1,0:T(8,128)(2,1)} %param.24), kind=kOutput, calls=%fused_computation.14 | convolution fusion | flops 201326592 | bytes 6651904 | tf_op jit(solution)/shard_map/erd,edf->erf/dot_general | solution.py:115
  88.8 0.7 reshape_transpose_reshape.4
  89.5 3.5 %all-to-all-start.4 = ((bf16[16,2,1536]{2,1,0:T(2,128)(2,1)}), bf16[16,2,1536]{2,1,0:T(2,128)(2,1)S(1)}, u32[]{:S(2)}, u32[]{:S(2)}) async-start(bf16[16,2,1536]{2,1,0:T(2,128)(2,1)} %reshape_transpose_reshape.4), calls=%async_computation.4 | async-start | bytes 196608 | tf_op jit(solution)/shard_map/all_to_all | solution.py:217
  93.1 7.6 %all-to-all-done.4 = bf16[16,2,1536]{2,1,0:T(2,128)(2,1)S(1)} async-done(((bf16[16,2,1536]{2,1,0:T(2,128)(2,1)}), bf16[16,2,1536]{2,1,0:T(2,128)(2,1)S(1)}, u32[]{:S(2)}, u32[]{:S(2)}) %all-to-all-start.4) | async-done | bytes 98336 | tf_op jit(solution)/shard_map/all_to_all | solution.py:217
  (88 shorter events, 11.5 us)
Async XLA Ops:
  0.0 88.1 %copy-start = (bf16[1,1024,1536]{2,1,0:T(8,128)(2,1)S(1)}, bf16[1,1024,1536]{2,1,0:T(8,128)(2,1)}, u32[]{:S(2)}) copy-start(bf16[1,1024,1536]{2,1,0:T(8,128)(2,1)} %param.25) | copy-start | bytes 9437188
  0.0 35.7 %copy-start.5 = (f32[1536]{0:T(1024)S(1)}, f32[1536]{0:T(1024)}, u32[]{:S(2)}) copy-start(f32[1536]{0:T(1024)} %param.18) | copy-start | bytes 18436
  1.6 16.1 %all-to-all-start = ((bf16[8,64,192]{2,1,0:T(8,128)(2,1)}), bf16[8,64,192]{2,1,0:T(8,128)(2,1)S(1)}, u32[]{:S(2)}, u32[]{:S(2)}) async-start(bf16[8,64,192]{2,1,0:T(8,128)(2,1)} %broadcast_in_dim.65), calls=%async_computation | async-start | bytes 524288 | tf_op jit(solution)/shard_map/all_to_all | solution.py:148
  15.3 11.3 %copy-start.6 = (s32[16]{0:T(128)}, s32[16]{0:T(128)S(1)}, u32[]{:S(2)}) copy-start(s32[16]{0:T(128)S(1)} %eq.153) | copy-start | bytes 196
  15.6 0.5 copy-start.8
  19.0 15.7 %all-to-all-start.1 = ((bf16[16,4,1536]{2,1,0:T(4,128)(2,1)}), bf16[16,4,1536]{2,1,0:T(4,128)(2,1)S(1)}, u32[]{:S(2)}, u32[]{:S(2)}) async-start(bf16[16,4,1536]{2,1,0:T(4,128)(2,1)} %reshape.541), calls=%async_computation.1 | async-start | bytes 393216 | tf_op jit(solution)/shard_map/all_to_all | solution.py:162
  35.7 10.9 %copy-start.1 = (pred[64,320]{1,0:T(8,128)(4,1)S(1)}, pred[64,320]{1,0:T(8,128)(4,1)}, u32[]{:S(2)}) copy-start(pred[64,320]{1,0:T(8,128)(4,1)} %slice_compare_fusion) | copy-start | bytes 61444
  37.3 1.7 %copy-start.2 = (bf16[64,1,320]{2,0,1:T(8,128)(2,1)}, bf16[64,1,320]{2,0,1:T(8,128)(2,1)S(1)}, u32[]{:S(2)}) copy-start(bf16[64,1,320]{2,0,1:T(8,128)(2,1)S(1)} %fusion.19) | copy-start | bytes 122884
  40.0 6.8 %copy-start.3 = (f32[64,64]{1,0:T(8,128)S(1)}, f32[64,64]{1,0:T(8,128)}, u32[]{:S(2)}) copy-start(f32[64,64]{1,0:T(8,128)} %get-tuple-element.14) | copy-start | bytes 49156
  40.0 6.9 %slice-start = ((bf16[64,1,320]{2,0,1:T(8,128)(2,1)}), bf16[64,1,192]{2,0,1:T(8,128)(2,1)S(1)}, s32[]{:S(2)}) async-start(bf16[64,1,320]{2,0,1:T(8,128)(2,1)} %copy-done.2), calls=%async_computation.5 | async-start | bytes 65536 | tf_op jit(solution)/shard_map/slice | solution.py:27
  47.8 7.6 %copy-start.7 = (bf16[64,1,3]{0,2,1:T(4,128)(2,1)S(1)}, bf16[64,1,3]{0,2,1:T(4,128)(2,1)}, u32[]{:S(2)}) copy-start(bf16[64,1,3]{0,2,1:T(4,128)(2,1)} %get-tuple-element.19) | copy-start | bytes 1156
  47.8 7.6 %copy-start.4 = (f32[64,64]{1,0:T(8,128)S(1)}, f32[64,64]{1,0:T(8,128)}, u32[]{:S(2)}) copy-start(f32[64,64]{1,0:T(8,128)} %get-tuple-element.13) | copy-start | bytes 49156
  57.9 11.3 %all-to-all-start.2 = ((bf16[8,8,1536]{2,1,0:T(8,128)(2,1)}), bf16[8,8,1536]{2,1,0:T(8,128)(2,1)S(1)}, u32[]{:S(2)}, u32[]{:S(2)}) async-start(bf16[8,8,1536]{2,1,0:T(8,128)(2,1)} %fusion.7), calls=%async_computation.2 | async-start | bytes 393216 | tf_op jit(solution)/shard_map/all_to_all | solution.py:180
  72.8 11.3 %all-to-all-start.3 = ((bf16[16,2,1536]{2,1,0:T(2,128)(2,1)}), bf16[16,2,1536]{2,1,0:T(2,128)(2,1)S(1)}, u32[]{:S(2)}, u32[]{:S(2)}) async-start(bf16[16,2,1536]{2,1,0:T(2,128)(2,1)} %reshape.513), calls=%async_computation.3 | async-start | bytes 196608 | tf_op jit(solution)/shard_map/all_to_all | solution.py:213
  84.2 16.6 %copy-start.9 = (s32[8,2]{0,1:T(2,128)S(1)}, s32[8,2]{0,1:T(2,128)}, u32[]{:S(2)}) copy-start(s32[8,2]{0,1:T(2,128)} %copy.121) | copy-start | bytes 196
  89.5 11.3 %all-to-all-start.4 = ((bf16[16,2,1536]{2,1,0:T(2,128)(2,1)}), bf16[16,2,1536]{2,1,0:T(2,128)(2,1)S(1)}, u32[]{:S(2)}, u32[]{:S(2)}) async-start(bf16[16,2,1536]{2,1,0:T(2,128)(2,1)} %reshape_transpose_reshape.4), calls=%async_computation.4 | async-start | bytes 196608 | tf_op jit(solution)/shard_map/all_to_all | solution.py:217

commit v13 on v12

--- a/solution.py
+++ b/solution.py
@@ -30,7 +30,7 @@
     )
     key_new = projected[:, :, groups * head_dim : (groups + 1) * head_dim].astype(jnp.bfloat16)
     value_new = projected[:, :, (groups + 1) * head_dim :].astype(jnp.bfloat16)
-    page_need = (seq_lens + page_len - 1) // page_len
+    page_need = lax.div(seq_lens + page_len - 1, page_len)
     page_ids = jnp.arange(max_pages, dtype=jnp.int32)
     in_use = page_ids[None, :] < page_need[:, None]
     pool_ids = jnp.arange(pool_pages, dtype=jnp.int32)
@@ -45,8 +45,8 @@
         [
             (entry_slot[None, :] == jnp.arange(slot_count, dtype=jnp.int32)[:, None]).astype(jnp.float32),
             entry_order[None, :].astype(jnp.float32),
-            (entry_len // len_unit)[None, :].astype(jnp.float32),
-            (entry_len % len_unit)[None, :].astype(jnp.float32),
+            lax.div(entry_len, len_unit)[None, :].astype(jnp.float32),
+            lax.rem(entry_len, len_unit)[None, :].astype(jnp.float32),
         ],
         axis=0,
     ).astype(jnp.bfloat16)
@@ -148,7 +148,7 @@
     block_parts = lax.all_to_all(spread, "kv", split_axis=0, concat_axis=0, tiled=True)
     deal = local_rows // n_req
     perm_blocks = perm.reshape(n_req, local_rows)
-    source_block = perm_blocks // local_rows
+    source_block = lax.div(perm_blocks, local_rows)
     source_row = perm_blocks - source_block * local_rows
     mine = source_block == req_index
     rank_sent = jnp.cumsum(mine.astype(jnp.int32), axis=1) - 1

time: 103 us -> 103 us (level)
  no operation moved by 1% of the time
where the time goes in v13:
time: 103 us; the launch traced here: 102 us
  waiting for transfers between devices  29.6 us (29%)
  matrix products  25.1 us (24%)
  starting transfers between devices  23.9 us (23%)
  local copies, waits for them, and re-layouts  11.6 us (11%)
  other arithmetic  11 us (11%)
    all_to_all x1, waiting for transfers between devices, shards(): lax.all_to_all(outgoing_rows.reshape(n_req, deal, width), 'req', split_ax...  8.13 us
    all_to_all x1, waiting for transfers between devices, shards(): lax.all_to_all(outgoing, 'req', split_axis=0, concat_axis=0, tiled=True)  7.65 us
    all_to_all x1, waiting for transfers between devices, shards(): lax.all_to_all(expert_rows, 'req', split_axis=0, concat_axis=0, tiled=True)  7.62 us
    all_to_all x1, starting transfers between devices, shards(): lax.all_to_all(outgoing_rows.reshape(n_req, deal, width), 'req', split_ax...  7.04 us
    all_to_all x1, waiting for transfers between devices, shards(): lax.all_to_all(partial.reshape(n_kv, sub_rows, partial.shape[1]), 'kv', s...  6.16 us
    dot_general x1, matrix products, attend(): jnp.einsum('pkgd,pkdt->pkgt', page_queries, kv_cache[:, :, :head_dim, :],...  5.62 us
    all_to_all x1, starting transfers between devices, shards(): lax.all_to_all(spread, 'kv', split_axis=0, concat_axis=0, tiled=True)  5.4 us
    dot_general x1, matrix products, attend(): jnp.einsum('pkgt,pkdt->pkgd', rounded_weights, kv_cache[:, :, head_dim:,...  5.36 us
  transfers between devices with their start and end apart: 5, of which 4 were waited for; matrix products, arithmetic and copies ran while one was open for 11% of the time, Pallas kernels for 0%

profile of v13, /device:TPU:0, one launch (start us, length us, event | category | flops | bytes accessed | tf_op | source)
XLA Modules:
  0.0 101.6 jit_solution(4445611412396005602)
XLA Ops:
  0.0 1.6 %broadcast_in_dim.65 = bf16[8,64,192]{2,1,0:T(8,128)(2,1)} broadcast(bf16[64,192]{1,0:T(8,128)(2,1)} %param.13), dimensions={1,2} | broadcast | bytes 221184 | tf_op jit(solution)/shard_map/broadcast_in_dim | solution.py:147
  1.6 5.4 %all-to-all-start = ((bf16[8,64,192]{2,1,0:T(8,128)(2,1)}), bf16[8,64,192]{2,1,0:T(8,128)(2,1)S(1)}, u32[]{:S(2)}, u32[]{:S(2)}) async-start(bf16[8,64,192]{2,1,0:T(8,128)(2,1)} %broadcast_in_dim.65), calls=%async_computation | async-start | bytes 524288 | tf_op jit(solution)/shard_map/all_to_all | solution.py:148
  7.7 0.7 broadcast_in_dim.68
  8.6 0.8 convert_convert_fusion
  9.4 0.7 fusion.58
  10.4 1.8 %fusion.6 = f32[67,320]{1,0:T(8,128)S(1)} fusion(s32[2048]{0:T(1024)S(1)} %eq.147, bf16[1,2048]{1,0:T(2,128)(2,1)S(1)} %get-tuple-element.16, bf16[1,2048]{1,0:T(2,128)(2,1)S(1)} %get-tuple-element.15, bf16[1,2048]{1,0:T(2,128)(2,1)S(1)} %convert_element_type.166, bf16[64,2048]{1,0:T(8,128)(2,1)} %convert_convert_fusion), kind=kOutput, calls=%fused_computation.10 | convolution fusion | flops 89571328 | bytes 368384 | tf_op jit(solution)/shard_map/dot_general | solution.py:54
  12.8 0.8 reshape.431
  14.4 0.8 copy.113
  16.9 0.8 add_compare_fusion
  18.0 0.9 reshape.477
  18.9 7.0 %all-to-all-start.1 = ((bf16[16,4,1536]{2,1,0:T(4,128)(2,1)}), bf16[16,4,1536]{2,1,0:T(4,128)(2,1)S(1)}, u32[]{:S(2)}, u32[]{:S(2)}) async-start(bf16[16,4,1536]{2,1,0:T(4,128)(2,1)} %reshape.477), calls=%async_computation.1 | async-start | bytes 393216 | tf_op jit(solution)/shard_map/all_to_all | solution.py:162
  26.5 8.1 %all-to-all-done.1 = bf16[16,4,1536]{2,1,0:T(4,128)(2,1)S(1)} async-done(((bf16[16,4,1536]{2,1,0:T(4,128)(2,1)}), bf16[16,4,1536]{2,1,0:T(4,128)(2,1)S(1)}, u32[]{:S(2)}, u32[]{:S(2)}) %all-to-all-start.1) | async-done | bytes 196640 | tf_op jit(solution)/shard_map/all_to_all | solution.py:162
  34.7 0.9 fusion.27
  35.6 1.6 %fusion.19 = bf16[64,1,320]{2,0,1:T(8,128)(2,1)S(1)} fusion(bf16[1,1536,320]{1,2,0:T(8,128)(2,1)} %param.19, bf16[64,1536]{1,0:T(8,128)(2,1)S(1)} %get-tuple-element.22, f32[1536]{0:T(1024)S(1)} %copy-done.5, f32[64]{0:T(128)S(1)} %add_rsqrt_fusion.1), kind=kOutput, calls=%fused_computation.26 | convolution fusion | flops 63328256 | bytes 1227008 | tf_op jit(solution)/shard_map/sd,hdc->shc/dot_general | solution.py:25
  37.3 0.7 fusion.55
  38.0 1.0 fusion.51
  39.0 0.9 copy.107
  39.9 5.6 %fusion.75 = (f32[320,3]{1,0:T(8,128)}, f32[320,3,128]{2,1,0:T(4,128)}) fusion(bf16[320,3,64]{2,1,0:T(4,128)(2,1)} %copy.107, bf16[320,1,128,128]{3,2,0,1:T(8,128)(2,1)} %bitcast.100, pred[320,128]{1,0:T(8,128)(4,1)} %add_compare_fusion), kind=kOutput, calls=%fused_computation.138 | convolution fusion | flops 16096320 | bytes 6106880 | tf_op jit(solution)/shard_map/pkgd,pkdt->pkgt/dot_general | solution.py:68
  45.6 1.0 copy.108
  47.8 1.9 %fusion.25 = (f32[320,3]{1,0:T(8,128)S(1)}, bf16[320,1,3,128]{3,2,0,1:T(4,128)(2,1)S(1)}) fusion(f32[320,3,128]{2,1,0:T(4,128)} %get-tuple-element.24, f32[320,3]{1,0:T(8,128)S(1)} %copy.109, pred[320,128]{1,0:T(8,128)(4,1)} %add_compare_fusion), kind=kLoop, calls=%fused_computation.39 | loop fusion | flops 490560 | bytes 785920 | tf_op jit(solution)/shard_map/reduce_sum | solution.py:92
  50.0 5.4 %fusion.2 = f32[320,3,64]{2,1,0:T(4,128)S(1)} fusion(bf16[320,1,128,128]{3,2,0,1:T(8,128)(2,1)} %bitcast.101, bf16[320,1,3,128]{3,2,0,1:T(4,128)(2,1)S(1)} %get-tuple-element.10), kind=kOutput, calls=%fused_computation.4 | convolution fusion | flops 15728640 | bytes 5734400 | tf_op jit(solution)/shard_map/pkgt,pkdt->pkgd/dot_general | solution.py:94
  55.8 2.0 %fusion.7 = bf16[8,8,1536]{2,1,0:T(8,128)(2,1)} fusion(bf16[64,192]{0,1:T(8,128)(2,1)S(1)} %bitcast.103, bf16[1,192,1536]{2,1,0:T(8,128)(2,1)} %param.20), kind=kOutput, calls=%fused_computation.13 | convolution fusion | flops 37847040 | bytes 811008 | tf_op jit(solution)/shard_map/dot_general | solution.py:179
  57.8 4.5 %all-to-all-start.2 = ((bf16[8,8,1536]{2,1,0:T(8,128)(2,1)}), bf16[8,8,1536]{2,1,0:T(8,128)(2,1)S(1)}, u32[]{:S(2)}, u32[]{:S(2)}) async-start(bf16[8,8,1536]{2,1,0:T(8,128)(2,1)} %fusion.7), calls=%async_computation.2 | async-start | bytes 393216 | tf_op jit(solution)/shard_map/all_to_all | solution.py:180
  63.0 6.2 %all-to-all-done.2 = bf16[8,8,1536]{2,1,0:T(8,128)(2,1)S(1)} async-done(((bf16[8,8,1536]{2,1,0:T(8,128)(2,1)}), bf16[8,8,1536]{2,1,0:T(8,128)(2,1)S(1)}, u32[]{:S(2)}, u32[]{:S(2)}) %all-to-all-start.2) | async-done | bytes 196640 | tf_op jit(solution)/shard_map/all_to_all | solution.py:180
  69.3 0.8 fusion.49
  70.1 0.9 fusion.76
  72.8 3.5 %all-to-all-start.3 = ((bf16[16,2,1536]{2,1,0:T(2,128)(2,1)}), bf16[16,2,1536]{2,1,0:T(2,128)(2,1)S(1)}, u32[]{:S(2)}, u32[]{:S(2)}) async-start(bf16[16,2,1536]{2,1,0:T(2,128)(2,1)} %reshape.449), calls=%async_computation.3 | async-start | bytes 196608 | tf_op jit(solution)/shard_map/all_to_all | solution.py:213
  76.4 7.7 %all-to-all-done.3 = bf16[16,2,1536]{2,1,0:T(2,128)(2,1)S(1)} async-done(((bf16[16,2,1536]{2,1,0:T(2,128)(2,1)}), bf16[16,2,1536]{2,1,0:T(2,128)(2,1)S(1)}, u32[]{:S(2)}, u32[]{:S(2)}) %all-to-all-start.3) | async-done | bytes 98336 | tf_op jit(solution)/shard_map/all_to_all | solution.py:213
  84.1 4.0 %fusion.8 = f32[1,32,2048]{2,1,0:T(8,128)S(1)} fusion(bf16[32,1536]{1,0:T(8,128)(2,1)S(1)} %reshape.450, bf16[1,1536,2048]{2,1,0:T(8,128)(2,1)} %param.24), kind=kOutput, calls=%fused_computation.14 | convolution fusion | flops 201326592 | bytes 6651904 | tf_op jit(solution)/shard_map/erd,edf->erf/dot_general | solution.py:115
  88.7 0.7 reshape_transpose_reshape.4
  89.4 3.5 %all-to-all-start.4 = ((bf16[16,2,1536]{2,1,0:T(2,128)(2,1)}), bf16[16,2,1536]{2,1,0:T(2,128)(2,1)S(1)}, u32[]{:S(2)}, u32[]{:S(2)}) async-start(bf16[16,2,1536]{2,1,0:T(2,128)(2,1)} %reshape_transpose_reshape.4), calls=%async_computation.4 | async-start | bytes 196608 | tf_op jit(solution)/shard_map/all_to_all | solution.py:217
  93.1 7.6 %all-to-all-done.4 = bf16[16,2,1536]{2,1,0:T(2,128)(2,1)S(1)} async-done(((bf16[16,2,1536]{2,1,0:T(2,128)(2,1)}), bf16[16,2,1536]{2,1,0:T(2,128)(2,1)S(1)}, u32[]{:S(2)}, u32[]{:S(2)}) %all-to-all-start.4) | async-done | bytes 98336 | tf_op jit(solution)/shard_map/all_to_all | solution.py:217
  (87 shorter events, 11.5 us)
Async XLA Ops:
  0.0 88.1 %copy-start = (bf16[1,1024,1536]{2,1,0:T(8,128)(2,1)S(1)}, bf16[1,1024,1536]{2,1,0:T(8,128)(2,1)}, u32[]{:S(2)}) copy-start(bf16[1,1024,1536]{2,1,0:T(8,128)(2,1)} %param.25) | copy-start | bytes 9437188
  0.0 35.6 %copy-start.5 = (f32[1536]{0:T(1024)S(1)}, f32[1536]{0:T(1024)}, u32[]{:S(2)}) copy-start(f32[1536]{0:T(1024)} %param.18) | copy-start | bytes 18436
  1.6 16.0 %all-to-all-start = ((bf16[8,64,192]{2,1,0:T(8,128)(2,1)}), bf16[8,64,192]{2,1,0:T(8,128)(2,1)S(1)}, u32[]{:S(2)}, u32[]{:S(2)}) async-start(bf16[8,64,192]{2,1,0:T(8,128)(2,1)} %broadcast_in_dim.65), calls=%async_computation | async-start | bytes 524288 | tf_op jit(solution)/shard_map/all_to_all | solution.py:148
  15.2 11.3 %copy-start.6 = (s32[16]{0:T(128)}, s32[16]{0:T(128)S(1)}, u32[]{:S(2)}) copy-start(s32[16]{0:T(128)S(1)} %eq.151) | copy-start | bytes 196
  15.5 0.5 copy-start.8
  18.9 15.7 %all-to-all-start.1 = ((bf16[16,4,1536]{2,1,0:T(4,128)(2,1)}), bf16[16,4,1536]{2,1,0:T(4,128)(2,1)S(1)}, u32[]{:S(2)}, u32[]{:S(2)}) async-start(bf16[16,4,1536]{2,1,0:T(4,128)(2,1)} %reshape.477), calls=%async_computation.1 | async-start | bytes 393216 | tf_op jit(solution)/shard_map/all_to_all | solution.py:162
  35.6 10.9 %copy-start.1 = (pred[64,320]{1,0:T(8,128)(4,1)S(1)}, pred[64,320]{1,0:T(8,128)(4,1)}, u32[]{:S(2)}) copy-start(pred[64,320]{1,0:T(8,128)(4,1)} %slice_compare_fusion) | copy-start | bytes 61444
  37.3 1.7 %copy-start.2 = (bf16[64,1,320]{2,0,1:T(8,128)(2,1)}, bf16[64,1,320]{2,0,1:T(8,128)(2,1)S(1)}, u32[]{:S(2)}) copy-start(bf16[64,1,320]{2,0,1:T(8,128)(2,1)S(1)} %fusion.19) | copy-start | bytes 122884
  39.9 6.8 %copy-start.3 = (f32[64,64]{1,0:T(8,128)S(1)}, f32[64,64]{1,0:T(8,128)}, u32[]{:S(2)}) copy-start(f32[64,64]{1,0:T(8,128)} %get-tuple-element.12) | copy-start | bytes 49156
  39.9 6.9 %slice-start = ((bf16[64,1,320]{2,0,1:T(8,128)(2,1)}), bf16[64,1,192]{2,0,1:T(8,128)(2,1)S(1)}, s32[]{:S(2)}) async-start(bf16[64,1,320]{2,0,1:T(8,128)(2,1)} %copy-done.2), calls=%async_computation.5 | async-start | bytes 65536 | tf_op jit(solution)/shard_map/slice | solution.py:27
  47.8 7.6 %copy-start.7 = (bf16[64,1,3]{0,2,1:T(4,128)(2,1)S(1)}, bf16[64,1,3]{0,2,1:T(4,128)(2,1)}, u32[]{:S(2)}) copy-start(bf16[64,1,3]{0,2,1:T(4,128)(2,1)} %get-tuple-element.19) | copy-start | bytes 1156
  47.8 7.6 %copy-start.4 = (f32[64,64]{1,0:T(8,128)S(1)}, f32[64,64]{1,0:T(8,128)}, u32[]{:S(2)}) copy-start(f32[64,64]{1,0:T(8,128)} %get-tuple-element.11) | copy-start | bytes 49156
  57.8 11.3 %all-to-all-start.2 = ((bf16[8,8,1536]{2,1,0:T(8,128)(2,1)}), bf16[8,8,1536]{2,1,0:T(8,128)(2,1)S(1)}, u32[]{:S(2)}, u32[]{:S(2)}) async-start(bf16[8,8,1536]{2,1,0:T(8,128)(2,1)} %fusion.7), calls=%async_computation.2 | async-start | bytes 393216 | tf_op jit(solution)/shard_map/all_to_all | solution.py:180
  72.8 11.3 %all-to-all-start.3 = ((bf16[16,2,1536]{2,1,0:T(2,128)(2,1)}), bf16[16,2,1536]{2,1,0:T(2,128)(2,1)S(1)}, u32[]{:S(2)}, u32[]{:S(2)}) async-start(bf16[16,2,1536]{2,1,0:T(2,128)(2,1)} %reshape.449), calls=%async_computation.3 | async-start | bytes 196608 | tf_op jit(solution)/shard_map/all_to_all | solution.py:213
  84.1 16.6 %copy-start.9 = (s32[8,2]{0,1:T(2,128)S(1)}, s32[8,2]{0,1:T(2,128)}, u32[]{:S(2)}) copy-start(s32[8,2]{0,1:T(2,128)} %copy.121) | copy-start | bytes 196
  89.4 11.3 %all-to-all-start.4 = ((bf16[16,2,1536]{2,1,0:T(2,128)(2,1)}), bf16[16,2,1536]{2,1,0:T(2,128)(2,1)S(1)}, u32[]{:S(2)}, u32[]{:S(2)}) async-start(bf16[16,2,1536]{2,1,0:T(2,128)(2,1)} %reshape_transpose_reshape.4), calls=%async_computation.4 | async-start | bytes 196608 | tf_op jit(solution)/shard_map/all_to_all | solution.py:217

commit v14 on v13

--- a/solution.py
+++ b/solution.py
@@ -185,39 +185,40 @@
     residual = (own_tokens.astype(jnp.float32) + attn_rows).astype(jnp.bfloat16)
     normed_ffn = rms_norm(residual, ffn_gain)
     logits = jnp.dot(normed_ffn, router, preferred_element_type=jnp.float32)
-    chosen = jnp.take_along_axis(logits, routes, axis=1)
+    expert_ids = jnp.arange(logits.shape[1], dtype=jnp.int32)
+    chosen = jnp.sum(
+        jnp.where(routes[:, :, None] == expert_ids[None, None, :], logits[:, None, :], 0.0), axis=2
+    )
     sigmoid_vals = jax.nn.sigmoid(chosen)
     gates = sigmoid_vals / jnp.sum(sigmoid_vals, axis=1, keepdims=True)
     experts_all = router.shape[1]
     local_experts = gate_up.shape[0]
     capacity = max(2, 2 * sub_rows // experts_all + 1)
-    flat_routes = routes.reshape(-1)
-    onehot_int = (flat_routes[:, None] == jnp.arange(experts_all, dtype=jnp.int32)[None, :]).astype(
-        jnp.int32
-    )
-    earlier = jnp.cumsum(onehot_int, axis=0) - onehot_int
-    rank_in = jnp.sum(earlier * onehot_int, axis=1)
+    entry_ids = jnp.arange(routes.size, dtype=jnp.int32).reshape(routes.shape)
+    same_expert = routes[:, :, None, None] == routes[None, None, :, :]
+    earlier = entry_ids[None, None, :, :] < entry_ids[:, :, None, None]
+    rank_in = jnp.sum((same_expert & earlier).astype(jnp.int32), axis=(2, 3))
     place_at = (
-        flat_routes // local_experts * capacity * local_experts
+        lax.div(routes, local_experts) * capacity * local_experts
         + rank_in * local_experts
-        + flat_routes % local_experts
-    )
-    placement_plan = (
-        place_at[:, None] == jnp.arange(experts_all * capacity, dtype=jnp.int32)[None, :]
-    ).astype(jnp.bfloat16)
-    paired_rows = jnp.repeat(normed_ffn, 2, axis=0)
+        + lax.rem(routes, local_experts)
+    )
+    slots_per_dest = capacity * local_experts
+    dest_slot = (
+        jnp.arange(n_req, dtype=jnp.int32)[:, None] * slots_per_dest
+        + jnp.arange(slots_per_dest, dtype=jnp.int32)[None, :]
+    )
+    placement_plan = (place_at[:, :, None, None] == dest_slot[None, None, :, :]).astype(jnp.bfloat16)
     outgoing = jnp.einsum(
-        "qe,qd->ed", placement_plan, paired_rows, preferred_element_type=jnp.float32
-    )
-    outgoing = outgoing.astype(jnp.bfloat16).reshape(n_req, capacity * local_experts, width)
+        "rjnc,rd->ncd", placement_plan, normed_ffn, preferred_element_type=jnp.float32
+    ).astype(jnp.bfloat16)
     arrived = lax.all_to_all(outgoing, "req", split_axis=0, concat_axis=0, tiled=True)
     expert_rows = expert_apply(
         arrived.reshape(n_req, capacity, local_experts, width), gate_up, down
-    ).reshape(n_req, capacity * local_experts, width)
+    ).reshape(n_req, slots_per_dest, width)
     returned = lax.all_to_all(expert_rows, "req", split_axis=0, concat_axis=0, tiled=True)
-    back_rows = returned.reshape(experts_all * capacity, width)
-    paired_output = jnp.dot(placement_plan, back_rows, preferred_element_type=jnp.float32).reshape(
-        sub_rows, 2, width
+    paired_output = jnp.einsum(
+        "rjnc,ncd->rjd", placement_plan, returned, preferred_element_type=jnp.float32
     )
     mixed = residual.astype(jnp.float32) + jnp.sum(gates[:, :, None] * paired_output, axis=1)
     return mixed.astype(jnp.bfloat16)

time: 103 us -> 101 us (0.981)
  local copies, waits for them, and re-layouts: 11.6 us -> 8.53 us
  other arithmetic: 11 us -> 12.2 us
    reduce_sum x1 -> x3, other arithmetic: 0.19 us -> 1.8 us  [the longest x1 0.94 us: shards(): rank_in = jnp.sum((same_expert & earlier).astype(jnp.int32), axis=(2, 3))]
    unnamed x22 -> x17, local copies, waits for them, and re-layouts: 1.31 us -> 0.11 us
    add x2, other arithmetic: 0.68 us -> 1.84 us  [the longest x1 1.23 us: shards(): lax.div(routes, local_experts) * capacity * local_experts]
  transfers between devices with their start and end apart: 5 -> 5, of which waited for: 4 -> 4; matrix products, arithmetic and copies ran while one was open for 11% -> 12% of each run, Pallas kernels for 0% -> 0%
where the time goes in v14:
time: 101 us; the launch traced here: 99.9 us
  waiting for transfers between devices  29.7 us (29%)
  matrix products  25.3 us (25%)
  starting transfers between devices  23.9 us (24%)
  other arithmetic  12.2 us (12%)
  local copies, waits for them, and re-layouts  8.53 us (8%)
    all_to_all x1, waiting for transfers between devices, shards(): lax.all_to_all(outgoing_rows.reshape(n_req, deal, width), 'req', split_ax...  8.63 us
    all_to_all x1, waiting for transfers between devices, shards(): lax.all_to_all(expert_rows, 'req', split_axis=0, concat_axis=0, tiled=True)  7.76 us
    all_to_all x1, waiting for transfers between devices, shards(): lax.all_to_all(outgoing, 'req', split_axis=0, concat_axis=0, tiled=True)  7.75 us
    all_to_all x1, starting transfers between devices, shards(): lax.all_to_all(outgoing_rows.reshape(n_req, deal, width), 'req', split_ax...  7.04 us
    dot_general x1, matrix products, attend(): jnp.einsum('pkgd,pkdt->pkgt', page_queries, kv_cache[:, :, :head_dim, :],...  5.62 us
    all_to_all x1, waiting for transfers between devices, shards(): lax.all_to_all(partial.reshape(n_kv, sub_rows, partial.shape[1]), 'kv', s...  5.51 us
    all_to_all x1, starting transfers between devices, shards(): lax.all_to_all(spread, 'kv', split_axis=0, concat_axis=0, tiled=True)  5.4 us
    dot_general x1, matrix products, attend(): jnp.einsum('pkgt,pkdt->pkgd', rounded_weights, kv_cache[:, :, head_dim:,...  5.36 us
  transfers between devices with their start and end apart: 5, of which 4 were waited for; matrix products, arithmetic and copies ran while one was open for 12% of the time, Pallas kernels for 0%

profile of v14, /device:TPU:0, one launch (start us, length us, event | category | flops | bytes accessed | tf_op | source)
XLA Modules:
  0.0 99.9 jit_solution(15242594686206733733)
XLA Ops:
  0.0 1.6 %broadcast_in_dim.78 = bf16[8,64,192]{2,1,0:T(8,128)(2,1)} broadcast(bf16[64,192]{1,0:T(8,128)(2,1)} %param.13), dimensions={1,2} | broadcast | bytes 221184 | tf_op jit(solution)/shard_map/broadcast_in_dim | solution.py:147
  1.6 5.4 %all-to-all-start = ((bf16[8,64,192]{2,1,0:T(8,128)(2,1)}), bf16[8,64,192]{2,1,0:T(8,128)(2,1)S(1)}, u32[]{:S(2)}, u32[]{:S(2)}) async-start(bf16[8,64,192]{2,1,0:T(8,128)(2,1)} %broadcast_in_dim.78), calls=%async_computation | async-start | bytes 524288 | tf_op jit(solution)/shard_map/all_to_all | solution.py:148
  7.7 0.7 broadcast_in_dim.81
  8.6 0.8 convert_convert_fusion
  9.4 0.7 fusion.63
  10.4 1.8 %fusion.6 = f32[67,320]{1,0:T(8,128)S(1)} fusion(s32[2048]{0:T(1024)S(1)} %eq.134, bf16[1,2048]{1,0:T(2,128)(2,1)S(1)} %get-tuple-element.16, bf16[1,2048]{1,0:T(2,128)(2,1)S(1)} %get-tuple-element.15, bf16[1,2048]{1,0:T(2,128)(2,1)S(1)} %convert_element_type.171, bf16[64,2048]{1,0:T(8,128)(2,1)} %convert_convert_fusion), kind=kOutput, calls=%fused_computation.9 | convolution fusion | flops 89571328 | bytes 368384 | tf_op jit(solution)/shard_map/dot_general | solution.py:54
  13.3 0.8 reshape.432
  14.9 0.8 add_compare_fusion
  15.7 0.9 convert_reduce_fusion.3
  16.6 1.2 %multiply_add_fusion.1 = s32[8,2]{0,1:T(2,128)} fusion(s32[8,2]{0,1:T(2,128)S(1)} %convert_reduce_fusion.3, s32[8,2]{0,1:T(2,128)} %param.23), kind=kLoop, calls=%fused_computation.127 | loop fusion | flops 32 | bytes 192 | tf_op jit(solution)/shard_map/add | solution.py:202
  18.1 0.9 reshape.465
  19.1 7.0 %all-to-all-start.1 = ((bf16[16,4,1536]{2,1,0:T(4,128)(2,1)}), bf16[16,4,1536]{2,1,0:T(4,128)(2,1)S(1)}, u32[]{:S(2)}, u32[]{:S(2)}) async-start(bf16[16,4,1536]{2,1,0:T(4,128)(2,1)} %reshape.465), calls=%async_computation.1 | async-start | bytes 393216 | tf_op jit(solution)/shard_map/all_to_all | solution.py:162
  26.1 8.6 %all-to-all-done.1 = bf16[16,4,1536]{2,1,0:T(4,128)(2,1)S(1)} async-done(((bf16[16,4,1536]{2,1,0:T(4,128)(2,1)}), bf16[16,4,1536]{2,1,0:T(4,128)(2,1)S(1)}, u32[]{:S(2)}, u32[]{:S(2)}) %all-to-all-start.1) | async-done | bytes 196640 | tf_op jit(solution)/shard_map/all_to_all | solution.py:162
  35.2 1.6 %fusion.20 = bf16[64,1,320]{2,0,1:T(8,128)(2,1)S(1)} fusion(bf16[1,1536,320]{1,2,0:T(8,128)(2,1)} %param.19, bf16[64,1536]{1,0:T(8,128)(2,1)S(1)} %get-tuple-element.20, f32[1536]{0:T(1024)S(1)} %copy-done.6, f32[64]{0:T(128)S(1)} %add_rsqrt_fusion.1), kind=kOutput, calls=%fused_computation.26 | convolution fusion | flops 63328256 | bytes 1227008 | tf_op jit(solution)/shard_map/sd,hdc->shc/dot_general | solution.py:25
  37.5 1.0 fusion.54
  38.5 0.9 copy.91
  39.5 5.6 %fusion.80 = (f32[320,3]{1,0:T(8,128)}, f32[320,3,128]{2,1,0:T(4,128)}) fusion(bf16[320,3,64]{2,1,0:T(4,128)(2,1)} %copy.91, bf16[320,1,128,128]{3,2,0,1:T(8,128)(2,1)} %bitcast.104, pred[320,128]{1,0:T(8,128)(4,1)} %add_compare_fusion), kind=kOutput, calls=%fused_computation.141 | convolution fusion | flops 16096320 | bytes 6106880 | tf_op jit(solution)/shard_map/pkgd,pkdt->pkgt/dot_general | solution.py:68
  45.1 1.0 copy.92
  46.8 1.9 %fusion.26 = (f32[320,3]{1,0:T(8,128)S(1)}, bf16[320,1,3,128]{3,2,0,1:T(4,128)(2,1)S(1)}) fusion(f32[320,3,128]{2,1,0:T(4,128)} %get-tuple-element.22, f32[320,3]{1,0:T(8,128)S(1)} %copy.93, pred[320,128]{1,0:T(8,128)(4,1)} %add_compare_fusion), kind=kLoop, calls=%fused_computation.39 | loop fusion | flops 490560 | bytes 785920 | tf_op jit(solution)/shard_map/reduce_sum | solution.py:92
  49.0 5.4 %fusion.2 = f32[320,3,64]{2,1,0:T(4,128)S(1)} fusion(bf16[320,1,128,128]{3,2,0,1:T(8,128)(2,1)} %bitcast.105, bf16[320,1,3,128]{3,2,0,1:T(4,128)(2,1)S(1)} %get-tuple-element.10), kind=kOutput, calls=%fused_computation.3 | convolution fusion | flops 15728640 | bytes 5734400 | tf_op jit(solution)/shard_map/pkgt,pkdt->pkgd/dot_general | solution.py:94
  54.8 2.0 %fusion.7 = bf16[8,8,1536]{2,1,0:T(8,128)(2,1)} fusion(bf16[64,192]{0,1:T(8,128)(2,1)S(1)} %bitcast.107, bf16[1,192,1536]{2,1,0:T(8,128)(2,1)} %param.20), kind=kOutput, calls=%fused_computation.12 | convolution fusion | flops 37847040 | bytes 811008 | tf_op jit(solution)/shard_map/dot_general | solution.py:179
  56.8 4.5 %all-to-all-start.2 = ((bf16[8,8,1536]{2,1,0:T(8,128)(2,1)}), bf16[8,8,1536]{2,1,0:T(8,128)(2,1)S(1)}, u32[]{:S(2)}, u32[]{:S(2)}) async-start(bf16[8,8,1536]{2,1,0:T(8,128)(2,1)} %fusion.7), calls=%async_computation.2 | async-start | bytes 393216 | tf_op jit(solution)/shard_map/all_to_all | solution.py:180
  61.9 0.7 convert_reduce_fusion.2
  62.6 5.5 %all-to-all-done.2 = bf16[8,8,1536]{2,1,0:T(8,128)(2,1)S(1)} async-done(((bf16[8,8,1536]{2,1,0:T(8,128)(2,1)}), bf16[8,8,1536]{2,1,0:T(8,128)(2,1)S(1)}, u32[]{:S(2)}, u32[]{:S(2)}) %all-to-all-start.2) | async-done | bytes 196640 | tf_op jit(solution)/shard_map/all_to_all | solution.py:180
  68.3 1.0 %fusion.69 = f32[8,16]{1,0:T(8,128)S(1)} fusion(bf16[1536,16]{0,1:T(8,128)(2,1)} %param.22, bf16[8,1536]{1,0:T(8,128)(2,1)S(1)} %get-tuple-element.8, f32[1536]{0:T(1024)} %param.21, f32[8]{0:T(128)S(1)} %add_rsqrt_fusion), kind=kOutput, calls=%fused_computation.111 | convolution fusion | flops 442368 | bytes 80416 | tf_op jit(solution)/shard_map/dot_general | solution.py:187
  69.5 0.9 convolution_convert_fusion.2
  70.4 0.7 copy.97
  71.1 3.5 %all-to-all-start.3 = ((bf16[16,2,1536]{2,1,0:T(2,128)(2,1)}), bf16[16,2,1536]{2,1,0:T(2,128)(2,1)S(1)}, u32[]{:S(2)}, u32[]{:S(2)}) async-start(bf16[16,2,1536]{2,1,0:T(2,128)(2,1)} %copy.97), calls=%async_computation.3 | async-start | bytes 196608 | tf_op jit(solution)/shard_map/all_to_all | solution.py:215
  74.7 7.8 %all-to-all-done.3 = bf16[16,2,1536]{2,1,0:T(2,128)(2,1)S(1)} async-done(((bf16[16,2,1536]{2,1,0:T(2,128)(2,1)}), bf16[16,2,1536]{2,1,0:T(2,128)(2,1)S(1)}, u32[]{:S(2)}, u32[]{:S(2)}) %all-to-all-start.3) | async-done | bytes 98336 | tf_op jit(solution)/shard_map/all_to_all | solution.py:215
  82.5 4.0 %fusion.8 = f32[1,32,2048]{2,1,0:T(8,128)S(1)} fusion(bf16[32,1536]{1,0:T(8,128)(2,1)S(1)} %reshape.448, bf16[1,1536,2048]{2,1,0:T(8,128)(2,1)} %param.24), kind=kOutput, calls=%fused_computation.13 | convolution fusion | flops 201326592 | bytes 6651904 | tf_op jit(solution)/shard_map/erd,edf->erf/dot_general | solution.py:115
  87.8 3.5 %all-to-all-start.4 = ((bf16[16,2,1536]{2,1,0:T(2,128)(2,1)}), bf16[16,2,1536]{2,1,0:T(2,128)(2,1)S(1)}, u32[]{:S(2)}, u32[]{:S(2)}) async-start(bf16[16,2,1536]{2,1,0:T(2,128)(2,1)} %reshape_transpose_reshape.4), calls=%async_computation.4 | async-start | bytes 196608 | tf_op jit(solution)/shard_map/all_to_all | solution.py:219
  91.3 7.8 %all-to-all-done.4 = bf16[16,2,1536]{2,1,0:T(2,128)(2,1)S(1)} async-done(((bf16[16,2,1536]{2,1,0:T(2,128)(2,1)}), bf16[16,2,1536]{2,1,0:T(2,128)(2,1)S(1)}, u32[]{:S(2)}, u32[]{:S(2)}) %all-to-all-start.4) | async-done | bytes 98336 | tf_op jit(solution)/shard_map/all_to_all | solution.py:219
  (70 shorter events, 9.0 us)
Async XLA Ops:
  0.0 86.4 %copy-start = (bf16[1,1024,1536]{2,1,0:T(8,128)(2,1)S(1)}, bf16[1,1024,1536]{2,1,0:T(8,128)(2,1)}, u32[]{:S(2)}) copy-start(bf16[1,1024,1536]{2,1,0:T(8,128)(2,1)} %param.25) | copy-start | bytes 9437188
  0.0 35.2 %copy-start.6 = (f32[1536]{0:T(1024)S(1)}, f32[1536]{0:T(1024)}, u32[]{:S(2)}) copy-start(f32[1536]{0:T(1024)} %param.18) | copy-start | bytes 18436
  1.6 16.2 %all-to-all-start = ((bf16[8,64,192]{2,1,0:T(8,128)(2,1)}), bf16[8,64,192]{2,1,0:T(8,128)(2,1)S(1)}, u32[]{:S(2)}, u32[]{:S(2)}) async-start(bf16[8,64,192]{2,1,0:T(8,128)(2,1)} %broadcast_in_dim.78), calls=%async_computation | async-start | bytes 524288 | tf_op jit(solution)/shard_map/all_to_all | solution.py:148
  19.1 15.7 %all-to-all-start.1 = ((bf16[16,4,1536]{2,1,0:T(4,128)(2,1)}), bf16[16,4,1536]{2,1,0:T(4,128)(2,1)S(1)}, u32[]{:S(2)}, u32[]{:S(2)}) async-start(bf16[16,4,1536]{2,1,0:T(4,128)(2,1)} %reshape.465), calls=%async_computation.1 | async-start | bytes 393216 | tf_op jit(solution)/shard_map/all_to_all | solution.py:162
  35.2 10.9 %copy-start.1 = (pred[64,320]{1,0:T(8,128)(4,1)S(1)}, pred[64,320]{1,0:T(8,128)(4,1)}, u32[]{:S(2)}) copy-start(pred[64,320]{1,0:T(8,128)(4,1)} %slice_compare_fusion) | copy-start | bytes 61444
  36.8 1.7 %copy-start.2 = (bf16[64,1,320]{2,0,1:T(8,128)(2,1)}, bf16[64,1,320]{2,0,1:T(8,128)(2,1)S(1)}, u32[]{:S(2)}) copy-start(bf16[64,1,320]{2,0,1:T(8,128)(2,1)S(1)} %fusion.20) | copy-start | bytes 122884
  39.5 6.8 %copy-start.3 = (f32[64,64]{1,0:T(8,128)S(1)}, f32[64,64]{1,0:T(8,128)}, u32[]{:S(2)}) copy-start(f32[64,64]{1,0:T(8,128)} %get-tuple-element.12) | copy-start | bytes 49156
  39.5 6.9 %slice-start = ((bf16[64,1,320]{2,0,1:T(8,128)(2,1)}), bf16[64,1,192]{2,0,1:T(8,128)(2,1)S(1)}, s32[]{:S(2)}) async-start(bf16[64,1,320]{2,0,1:T(8,128)(2,1)} %copy-done.2), calls=%async_computation.5 | async-start | bytes 65536 | tf_op jit(solution)/shard_map/slice | solution.py:27
  46.5 22.9 %copy-start.5 = (s32[8,2]{0,1:T(2,128)S(1)}, s32[8,2]{0,1:T(2,128)}, u32[]{:S(2)}) copy-start(s32[8,2]{0,1:T(2,128)} %param.23) | copy-start | bytes 196
  46.8 7.6 %copy-start.4 = (f32[64,64]{1,0:T(8,128)S(1)}, f32[64,64]{1,0:T(8,128)}, u32[]{:S(2)}) copy-start(f32[64,64]{1,0:T(8,128)} %get-tuple-element.11) | copy-start | bytes 49156
  56.8 11.3 %all-to-all-start.2 = ((bf16[8,8,1536]{2,1,0:T(8,128)(2,1)}), bf16[8,8,1536]{2,1,0:T(8,128)(2,1)S(1)}, u32[]{:S(2)}, u32[]{:S(2)}) async-start(bf16[8,8,1536]{2,1,0:T(8,128)(2,1)} %fusion.7), calls=%async_computation.2 | async-start | bytes 393216 | tf_op jit(solution)/shard_map/all_to_all | solution.py:180
  71.1 11.3 %all-to-all-start.3 = ((bf16[16,2,1536]{2,1,0:T(2,128)(2,1)}), bf16[16,2,1536]{2,1,0:T(2,128)(2,1)S(1)}, u32[]{:S(2)}, u32[]{:S(2)}) async-start(bf16[16,2,1536]{2,1,0:T(2,128)(2,1)} %copy.97), calls=%async_computation.3 | async-start | bytes 196608 | tf_op jit(solution)/shard_map/all_to_all | solution.py:215
  82.5 16.6 %copy-start.7 = (s32[8,2]{0,1:T(2,128)S(1)}, s32[8,2]{0,1:T(2,128)}, u32[]{:S(2)}) copy-start(s32[8,2]{0,1:T(2,128)} %multiply_add_fusion.1) | copy-start | bytes 196
  87.8 11.3 %all-to-all-start.4 = ((bf16[16,2,1536]{2,1,0:T(2,128)(2,1)}), bf16[16,2,1536]{2,1,0:T(2,128)(2,1)S(1)}, u32[]{:S(2)}, u32[]{:S(2)}) async-start(bf16[16,2,1536]{2,1,0:T(2,128)(2,1)} %reshape_transpose_reshape.4), calls=%async_computation.4 | async-start | bytes 196608 | tf_op jit(solution)/shard_map/all_to_all | solution.py:219

commit v15 on v14

--- a/solution.py
+++ b/solution.py
@@ -39,14 +39,10 @@
     ).reshape(-1)
     entry_page = jnp.where(in_use, page_table, -1).reshape(-1)
     entry_order = jnp.broadcast_to(page_ids[None, :], (slot_count, max_pages)).reshape(-1)
-    entry_len = jnp.broadcast_to(seq_lens[:, None], (slot_count, max_pages)).reshape(-1)
-    len_unit = 64
     facts = jnp.concatenate(
         [
             (entry_slot[None, :] == jnp.arange(slot_count, dtype=jnp.int32)[:, None]).astype(jnp.float32),
             entry_order[None, :].astype(jnp.float32),
-            lax.div(entry_len, len_unit)[None, :].astype(jnp.float32),
-            lax.rem(entry_len, len_unit)[None, :].astype(jnp.float32),
         ],
         axis=0,
     ).astype(jnp.bfloat16)
@@ -54,10 +50,7 @@
     page_facts = jnp.dot(facts, entry_hit, preferred_element_type=jnp.float32)
     belongs = page_facts[:slot_count] > 0.5
     page_order = page_facts[slot_count].astype(jnp.int32)
-    owner_len = (
-        page_facts[slot_count + 1].astype(jnp.int32) * len_unit
-        + page_facts[slot_count + 2].astype(jnp.int32)
-    )
+    owner_len = jnp.sum(jnp.where(belongs, seq_lens[:, None], 0), axis=0)
     position = page_order[:, None] * page_len + jnp.arange(page_len, dtype=jnp.int32)[None, :]
     live = position < owner_len[:, None]
     scale_factor = head_dim ** (-0.5)

time: 101 us -> 104 us (1.030)
  other arithmetic: 12.2 us -> 14.2 us
where the time goes in v15:
time: 104 us; the launch traced here: 103 us
  waiting for transfers between devices  29.6 us (28%)
  matrix products  26 us (25%)
  starting transfers between devices  23.9 us (23%)
  other arithmetic  14.2 us (14%)
  local copies, waits for them, and re-layouts  9.05 us (9%)
    all_to_all x1, waiting for transfers between devices, shards(): lax.all_to_all(outgoing_rows.reshape(n_req, deal, width), 'req', split_ax...  8.63 us
    all_to_all x1, waiting for transfers between devices, shards(): lax.all_to_all(expert_rows, 'req', split_axis=0, concat_axis=0, tiled=True)  7.76 us
    all_to_all x1, waiting for transfers between devices, shards(): lax.all_to_all(outgoing, 'req', split_axis=0, concat_axis=0, tiled=True)  7.75 us
    all_to_all x1, starting transfers between devices, shards(): lax.all_to_all(outgoing_rows.reshape(n_req, deal, width), 'req', split_ax...  7.03 us
    dot_general x1, matrix products, attend(): jnp.einsum('pkgd,pkdt->pkgt', page_queries, kv_cache[:, :, :head_dim, :],...  5.62 us
    all_to_all x1, waiting for transfers between devices, shards(): lax.all_to_all(partial.reshape(n_kv, sub_rows, partial.shape[1]), 'kv', s...  5.49 us
    all_to_all x1, starting transfers between devices, shards(): lax.all_to_all(spread, 'kv', split_axis=0, concat_axis=0, tiled=True)  5.4 us
    dot_general x1, matrix products, attend(): jnp.einsum('pkgt,pkdt->pkgd', rounded_weights, kv_cache[:, :, head_dim:,...  5.36 us
  transfers between devices with their start and end apart: 5, of which 4 were waited for; matrix products, arithmetic and copies ran while one was open for 12% of the time, Pallas kernels for 0%

profile of v15, /device:TPU:0, one launch (start us, length us, event | category | flops | bytes accessed | tf_op | source)
XLA Modules:
  0.0 103.1 jit_solution(8840244509297904236)
XLA Ops:
  0.0 1.6 %broadcast_in_dim.88 = bf16[8,64,192]{2,1,0:T(8,128)(2,1)} broadcast(bf16[64,192]{1,0:T(8,128)(2,1)} %param.13), dimensions={1,2} | broadcast | bytes 221184 | tf_op jit(solution)/shard_map/broadcast_in_dim | solution.py:140
  1.6 5.4 %all-to-all-start = ((bf16[8,64,192]{2,1,0:T(8,128)(2,1)}), bf16[8,64,192]{2,1,0:T(8,128)(2,1)S(1)}, u32[]{:S(2)}, u32[]{:S(2)}) async-start(bf16[8,64,192]{2,1,0:T(8,128)(2,1)} %broadcast_in_dim.88), calls=%async_computation | async-start | bytes 524288 | tf_op jit(solution)/shard_map/all_to_all | solution.py:141
  7.1 0.8 convert_convert_fusion
  9.5 1.7 %fusion.6 = f32[65,320]{1,0:T(8,128)S(1)} fusion(s32[2048]{0:T(1024)S(1)} %eq.134, bf16[1,2048]{1,0:T(2,128)(2,1)S(1)} %convert_element_type.133, bf16[64,2048]{1,0:T(8,128)(2,1)} %convert_convert_fusion), kind=kOutput, calls=%fused_computation.9 | convolution fusion | flops 86384640 | bytes 357632 | tf_op jit(solution)/shard_map/dot_general | solution.py:50
  11.3 0.8 select_reduce_fusion.2
  12.6 0.8 reshape.346
  14.7 0.8 add_compare_fusion
  15.5 0.9 convert_reduce_fusion.3
  16.4 1.3 %multiply_add_fusion.1 = s32[8,2]{0,1:T(2,128)} fusion(s32[8,2]{0,1:T(2,128)S(1)} %convert_reduce_fusion.3, s32[8,2]{0,1:T(2,128)} %param.23), kind=kLoop, calls=%fused_computation.114 | loop fusion | flops 32 | bytes 192 | tf_op jit(solution)/shard_map/add | solution.py:195
  18.0 0.9 reshape.377
  18.9 7.0 %all-to-all-start.1 = ((bf16[16,4,1536]{2,1,0:T(4,128)(2,1)}), bf16[16,4,1536]{2,1,0:T(4,128)(2,1)S(1)}, u32[]{:S(2)}, u32[]{:S(2)}) async-start(bf16[16,4,1536]{2,1,0:T(4,128)(2,1)} %reshape.377), calls=%async_computation.1 | async-start | bytes 393216 | tf_op jit(solution)/shard_map/all_to_all | solution.py:155
  26.0 8.6 %all-to-all-done.1 = bf16[16,4,1536]{2,1,0:T(4,128)(2,1)S(1)} async-done(((bf16[16,4,1536]{2,1,0:T(4,128)(2,1)}), bf16[16,4,1536]{2,1,0:T(4,128)(2,1)S(1)}, u32[]{:S(2)}, u32[]{:S(2)}) %all-to-all-start.1) | async-done | bytes 196640 | tf_op jit(solution)/shard_map/all_to_all | solution.py:155
  35.1 1.6 %fusion.20 = bf16[64,1,320]{2,0,1:T(8,128)(2,1)S(1)} fusion(bf16[1,1536,320]{1,2,0:T(8,128)(2,1)} %param.19, bf16[64,1536]{1,0:T(8,128)(2,1)S(1)} %get-tuple-element.18, f32[1536]{0:T(1024)} %param.18, f32[64]{0:T(128)S(1)} %add_rsqrt_fusion.1), kind=kOutput, calls=%fused_computation.26 | convolution fusion | flops 63328256 | bytes 1227008 | tf_op jit(solution)/shard_map/sd,hdc->shc/dot_general | solution.py:25
  36.7 1.0 %fusion.50 = f32[320,192]{0,1:S(1)} fusion(pred[64,320]{1,0:T(32,128)(4,1)} %copy-done.1, bf16[64,1,320]{2,0,1:T(8,128)(2,1)S(1)} %fusion.20), kind=kOutput, calls=%fused_computation.73 | convolution fusion | flops 7864320 | bytes 348160
  38.5 0.9 copy.91
  39.4 5.6 %fusion.73 = (f32[320,3]{1,0:T(8,128)}, f32[320,3,128]{2,1,0:T(4,128)}) fusion(bf16[320,3,64]{2,1,0:T(4,128)(2,1)} %copy.91, bf16[320,1,128,128]{3,2,0,1:T(8,128)(2,1)} %bitcast.104, pred[320,128]{1,0:T(8,128)(4,1)} %add_compare_fusion), kind=kOutput, calls=%fused_computation.128 | convolution fusion | flops 16096320 | bytes 6106880 | tf_op jit(solution)/shard_map/pkgd,pkdt->pkgt/dot_general | solution.py:61
  45.1 1.0 copy.92
  47.8 0.8 copy.93
  48.6 1.9 %fusion.26 = (f32[320,3]{1,0:T(8,128)S(1)}, bf16[320,1,3,128]{3,2,0,1:T(4,128)(2,1)S(1)}) fusion(f32[320,3,128]{2,1,0:T(4,128)} %get-tuple-element.20, f32[320,3]{1,0:T(8,128)S(1)} %copy.93, pred[320,128]{1,0:T(8,128)(4,1)} %add_compare_fusion), kind=kLoop, calls=%fused_computation.39 | loop fusion | flops 490560 | bytes 785920 | tf_op jit(solution)/shard_map/reduce_sum | solution.py:85
  50.5 0.9 convolution_add_fusion.1
  51.5 5.4 %fusion.2 = f32[320,3,64]{2,1,0:T(4,128)S(1)} fusion(bf16[320,1,128,128]{3,2,0,1:T(8,128)(2,1)} %bitcast.105, bf16[320,1,3,128]{3,2,0,1:T(4,128)(2,1)S(1)} %get-tuple-element.10), kind=kOutput, calls=%fused_computation.3 | convolution fusion | flops 15728640 | bytes 5734400 | tf_op jit(solution)/shard_map/pkgt,pkdt->pkgd/dot_general | solution.py:87
  57.3 2.0 %fusion.7 = bf16[8,8,1536]{2,1,0:T(8,128)(2,1)} fusion(bf16[64,192]{0,1:T(8,128)(2,1)S(1)} %bitcast.107, bf16[1,192,1536]{2,1,0:T(8,128)(2,1)} %param.20), kind=kOutput, calls=%fused_computation.12 | convolution fusion | flops 37847040 | bytes 811008 | tf_op jit(solution)/shard_map/dot_general | solution.py:172
  59.3 4.5 %all-to-all-start.2 = ((bf16[8,8,1536]{2,1,0:T(8,128)(2,1)}), bf16[8,8,1536]{2,1,0:T(8,128)(2,1)S(1)}, u32[]{:S(2)}, u32[]{:S(2)}) async-start(bf16[8,8,1536]{2,1,0:T(8,128)(2,1)} %fusion.7), calls=%async_computation.2 | async-start | bytes 393216 | tf_op jit(solution)/shard_map/all_to_all | solution.py:173
  65.1 5.5 %all-to-all-done.2 = bf16[8,8,1536]{2,1,0:T(8,128)(2,1)S(1)} async-done(((bf16[8,8,1536]{2,1,0:T(8,128)(2,1)}), bf16[8,8,1536]{2,1,0:T(8,128)(2,1)S(1)}, u32[]{:S(2)}, u32[]{:S(2)}) %all-to-all-start.2) | async-done | bytes 196640 | tf_op jit(solution)/shard_map/all_to_all | solution.py:173
  70.8 1.0 fusion.65
  71.8 0.8 select_reduce_fusion.3
  72.6 0.9 convolution_convert_fusion.2
  74.3 3.5 %all-to-all-start.3 = ((bf16[16,2,1536]{2,1,0:T(2,128)(2,1)}), bf16[16,2,1536]{2,1,0:T(2,128)(2,1)S(1)}, u32[]{:S(2)}, u32[]{:S(2)}) async-start(bf16[16,2,1536]{2,1,0:T(2,128)(2,1)} %copy.97), calls=%async_computation.3 | async-start | bytes 196608 | tf_op jit(solution)/shard_map/all_to_all | solution.py:208
  77.8 7.8 %all-to-all-done.3 = bf16[16,2,1536]{2,1,0:T(2,128)(2,1)S(1)} async-done(((bf16[16,2,1536]{2,1,0:T(2,128)(2,1)}), bf16[16,2,1536]{2,1,0:T(2,128)(2,1)S(1)}, u32[]{:S(2)}, u32[]{:S(2)}) %all-to-all-start.3) | async-done | bytes 98336 | tf_op jit(solution)/shard_map/all_to_all | solution.py:208
  85.6 4.0 %fusion.8 = f32[1,32,2048]{2,1,0:T(8,128)S(1)} fusion(bf16[32,1536]{1,0:T(8,128)(2,1)S(1)} %reshape.360, bf16[1,1536,2048]{2,1,0:T(8,128)(2,1)} %param.24), kind=kOutput, calls=%fused_computation.13 | convolution fusion | flops 201326592 | bytes 6651904 | tf_op jit(solution)/shard_map/erd,edf->erf/dot_general | solution.py:108
  90.9 3.5 %all-to-all-start.4 = ((bf16[16,2,1536]{2,1,0:T(2,128)(2,1)}), bf16[16,2,1536]{2,1,0:T(2,128)(2,1)S(1)}, u32[]{:S(2)}, u32[]{:S(2)}) async-start(bf16[16,2,1536]{2,1,0:T(2,128)(2,1)} %reshape_transpose_reshape.4), calls=%async_computation.4 | async-start | bytes 196608 | tf_op jit(solution)/shard_map/all_to_all | solution.py:212
  94.4 7.8 %all-to-all-done.4 = bf16[16,2,1536]{2,1,0:T(2,128)(2,1)S(1)} async-done(((bf16[16,2,1536]{2,1,0:T(2,128)(2,1)}), bf16[16,2,1536]{2,1,0:T(2,128)(2,1)S(1)}, u32[]{:S(2)}, u32[]{:S(2)}) %all-to-all-start.4) | async-done | bytes 98336 | tf_op jit(solution)/shard_map/all_to_all | solution.py:212
  (74 shorter events, 11.7 us)
Async XLA Ops:
  0.0 89.6 %copy-start = (bf16[1,1024,1536]{2,1,0:T(8,128)(2,1)S(1)}, bf16[1,1024,1536]{2,1,0:T(8,128)(2,1)}, u32[]{:S(2)}) copy-start(bf16[1,1024,1536]{2,1,0:T(8,128)(2,1)} %param.25) | copy-start | bytes 9437188
  1.6 16.1 %all-to-all-start = ((bf16[8,64,192]{2,1,0:T(8,128)(2,1)}), bf16[8,64,192]{2,1,0:T(8,128)(2,1)S(1)}, u32[]{:S(2)}, u32[]{:S(2)}) async-start(bf16[8,64,192]{2,1,0:T(8,128)(2,1)} %broadcast_in_dim.88), calls=%async_computation | async-start | bytes 524288 | tf_op jit(solution)/shard_map/all_to_all | solution.py:141
  12.0 14.0 %copy-start.1 = (pred[64,320]{1,0:T(32,128)(4,1)}, pred[64,320]{1,0:T(32,128)(4,1)S(1)}, u32[]{:S(2)}) copy-start(pred[64,320]{1,0:T(32,128)(4,1)S(1)} %get-tuple-element.8) | copy-start | bytes 61444
  18.9 15.7 %all-to-all-start.1 = ((bf16[16,4,1536]{2,1,0:T(4,128)(2,1)}), bf16[16,4,1536]{2,1,0:T(4,128)(2,1)S(1)}, u32[]{:S(2)}, u32[]{:S(2)}) async-start(bf16[16,4,1536]{2,1,0:T(4,128)(2,1)} %reshape.377), calls=%async_computation.1 | async-start | bytes 393216 | tf_op jit(solution)/shard_map/all_to_all | solution.py:155
  35.0 11.2 %copy-start.4 = (pred[64,320]{1,0:T(8,128)(4,1)S(1)}, pred[64,320]{1,0:T(8,128)(4,1)}, u32[]{:S(2)}) copy-start(pred[64,320]{1,0:T(8,128)(4,1)} %copy.124) | copy-start | bytes 61444
  36.7 1.8 %copy-start.3 = (bf16[64,1,320]{2,0,1:T(8,128)(2,1)}, bf16[64,1,320]{2,0,1:T(8,128)(2,1)S(1)}, u32[]{:S(2)}) copy-start(bf16[64,1,320]{2,0,1:T(8,128)(2,1)S(1)} %fusion.20) | copy-start | bytes 122884
  36.7 13.8 %copy-start.2 = (pred[64,320]{1,0:T(32,128)(4,1)S(1)}, pred[64,320]{1,0:T(32,128)(4,1)}, u32[]{:S(2)}) copy-start(pred[64,320]{1,0:T(32,128)(4,1)} %copy-done.1) | copy-start | bytes 61444
  39.4 6.6 %copy-start.6 = (f32[64,64]{1,0:T(8,128)S(1)}, f32[64,64]{1,0:T(8,128)}, u32[]{:S(2)}) copy-start(f32[64,64]{1,0:T(8,128)} %get-tuple-element.12) | copy-start | bytes 49156
  39.4 6.7 %slice-start = ((bf16[64,1,320]{2,0,1:T(8,128)(2,1)}), bf16[64,1,192]{2,0,1:T(8,128)(2,1)S(1)}, s32[]{:S(2)}) async-start(bf16[64,1,320]{2,0,1:T(8,128)(2,1)} %copy-done.3), calls=%async_computation.5 | async-start | bytes 65536 | tf_op jit(solution)/shard_map/slice | solution.py:27
  46.4 0.7 copy-start.7
  46.4 0.6 copy-start.8
  47.8 9.1 %copy-start.9 = (bf16[64,1,3]{0,2,1:T(4,128)(2,1)S(1)}, bf16[64,1,3]{0,2,1:T(4,128)(2,1)}, u32[]{:S(2)}) copy-start(bf16[64,1,3]{0,2,1:T(4,128)(2,1)} %get-tuple-element.15) | copy-start | bytes 1156
  48.6 8.3 %copy-start.5 = (f32[64,64]{1,0:T(8,128)S(1)}, f32[64,64]{1,0:T(8,128)}, u32[]{:S(2)}) copy-start(f32[64,64]{1,0:T(8,128)} %get-tuple-element.11) | copy-start | bytes 49156
  59.3 11.3 %all-to-all-start.2 = ((bf16[8,8,1536]{2,1,0:T(8,128)(2,1)}), bf16[8,8,1536]{2,1,0:T(8,128)(2,1)S(1)}, u32[]{:S(2)}, u32[]{:S(2)}) async-start(bf16[8,8,1536]{2,1,0:T(8,128)(2,1)} %fusion.7), calls=%async_computation.2 | async-start | bytes 393216 | tf_op jit(solution)/shard_map/all_to_all | solution.py:173
  74.3 11.3 %all-to-all-start.3 = ((bf16[16,2,1536]{2,1,0:T(2,128)(2,1)}), bf16[16,2,1536]{2,1,0:T(2,128)(2,1)S(1)}, u32[]{:S(2)}, u32[]{:S(2)}) async-start(bf16[16,2,1536]{2,1,0:T(2,128)(2,1)} %copy.97), calls=%async_computation.3 | async-start | bytes 196608 | tf_op jit(solution)/shard_map/all_to_all | solution.py:208
  85.6 16.6 %copy-start.10 = (s32[8,2]{0,1:T(2,128)S(1)}, s32[8,2]{0,1:T(2,128)}, u32[]{:S(2)}) copy-start(s32[8,2]{0,1:T(2,128)} %multiply_add_fusion.1) | copy-start | bytes 196
  90.9 11.3 %all-to-all-start.4 = ((bf16[16,2,1536]{2,1,0:T(2,128)(2,1)}), bf16[16,2,1536]{2,1,0:T(2,128)(2,1)S(1)}, u32[]{:S(2)}, u32[]{:S(2)}) async-start(bf16[16,2,1536]{2,1,0:T(2,128)(2,1)} %reshape_transpose_reshape.4), calls=%async_computation.4 | async-start | bytes 196608 | tf_op jit(solution)/shard_map/all_to_all | solution.py:212

commit v16 on v14

--- a/solution.py
+++ b/solution.py
@@ -112,11 +112,14 @@
 def expert_apply(piece, gate_up, down):
     n_source, slot_num, local_experts, width = piece.shape
     rows_in = piece.transpose(2, 0, 1, 3).reshape(local_experts, n_source * slot_num, width)
-    projected_up = jnp.einsum("erd,edf->erf", rows_in, gate_up, preferred_element_type=jnp.float32)
     hidden_units = gate_up.shape[2] // 2
-    acts = (
-        jax.nn.silu(projected_up[..., :hidden_units]) * projected_up[..., hidden_units:]
-    ).astype(jnp.bfloat16)
+    gate_part = jnp.einsum(
+        "erd,edf->erf", rows_in, gate_up[:, :, :hidden_units], preferred_element_type=jnp.float32
+    )
+    up_part = jnp.einsum(
+        "erd,edf->erf", rows_in, gate_up[:, :, hidden_units:], preferred_element_type=jnp.float32
+    )
+    acts = (jax.nn.silu(gate_part) * up_part).astype(jnp.bfloat16)
     result = jnp.einsum("erf,efd->erd", acts, down, preferred_element_type=jnp.float32).astype(
         jnp.bfloat16
     )

time: 101 us -> 102 us (level)
    dot_general x1, matrix products: 0.62 us -> 3.09 us  [expert_apply(): jnp.einsum('erf,efd->erd', acts, down, preferred_element_type=jnp.float32)]
    dot_general x1, matrix products: 3.97 us -> 2.53 us  [expert_apply(): jnp.einsum('erd,edf->erf', rows_in, gate_up[:, :, :hidden_units], preferr...]
where the time goes in v16:
time: 102 us; the launch traced here: 101 us
  waiting for transfers between devices  29.7 us (29%)
  matrix products  26.3 us (26%)
  starting transfers between devices  23.9 us (23%)
  other arithmetic  12.2 us (12%)
  local copies, waits for them, and re-layouts  8.52 us (8%)
    all_to_all x1, waiting for transfers between devices, shards(): lax.all_to_all(outgoing_rows.reshape(n_req, deal, width), 'req', split_ax...  8.63 us
    all_to_all x1, waiting for transfers between devices, shards(): lax.all_to_all(expert_rows, 'req', split_axis=0, concat_axis=0, tiled=True)  7.76 us
    all_to_all x1, waiting for transfers between devices, shards(): lax.all_to_all(outgoing, 'req', split_axis=0, concat_axis=0, tiled=True)  7.75 us
    all_to_all x1, starting transfers between devices, shards(): lax.all_to_all(outgoing_rows.reshape(n_req, deal, width), 'req', split_ax...  7.04 us
    dot_general x1, matrix products, attend(): jnp.einsum('pkgd,pkdt->pkgt', page_queries, kv_cache[:, :, :head_dim, :],...  5.62 us
    all_to_all x1, waiting for transfers between devices, shards(): lax.all_to_all(partial.reshape(n_kv, sub_rows, partial.shape[1]), 'kv', s...  5.51 us
    all_to_all x1, starting transfers between devices, shards(): lax.all_to_all(spread, 'kv', split_axis=0, concat_axis=0, tiled=True)  5.4 us
    dot_general x1, matrix products, attend(): jnp.einsum('pkgt,pkdt->pkgd', rounded_weights, kv_cache[:, :, head_dim:,...  5.36 us
  transfers between devices with their start and end apart: 5, of which 4 were waited for; matrix products, arithmetic and copies ran while one was open for 12% of the time, Pallas kernels for 0%

profile of v16, /device:TPU:0, one launch (start us, length us, event | category | flops | bytes accessed | tf_op | source)
XLA Modules:
  0.0 101.0 jit_solution(4161417179474318782)
XLA Ops:
  0.0 1.6 %broadcast_in_dim.78 = bf16[8,64,192]{2,1,0:T(8,128)(2,1)} broadcast(bf16[64,192]{1,0:T(8,128)(2,1)} %param.13), dimensions={1,2} | broadcast | bytes 221184 | tf_op jit(solution)/shard_map/broadcast_in_dim | solution.py:150
  1.6 5.4 %all-to-all-start = ((bf16[8,64,192]{2,1,0:T(8,128)(2,1)}), bf16[8,64,192]{2,1,0:T(8,128)(2,1)S(1)}, u32[]{:S(2)}, u32[]{:S(2)}) async-start(bf16[8,64,192]{2,1,0:T(8,128)(2,1)} %broadcast_in_dim.78), calls=%async_computation | async-start | bytes 524288 | tf_op jit(solution)/shard_map/all_to_all | solution.py:151
  7.7 0.7 broadcast_in_dim.81
  8.6 0.8 convert_convert_fusion
  9.4 0.7 fusion.75
  10.4 1.8 %fusion.10 = f32[67,320]{1,0:T(8,128)S(1)} fusion(s32[2048]{0:T(1024)S(1)} %eq.134, bf16[1,2048]{1,0:T(2,128)(2,1)S(1)} %get-tuple-element.16, bf16[1,2048]{1,0:T(2,128)(2,1)S(1)} %get-tuple-element.15, bf16[1,2048]{1,0:T(2,128)(2,1)S(1)} %convert_element_type.172, bf16[64,2048]{1,0:T(8,128)(2,1)} %convert_convert_fusion), kind=kOutput, calls=%fused_computation.13 | convolution fusion | flops 89571328 | bytes 368384 | tf_op jit(solution)/shard_map/dot_general | solution.py:54
  13.3 0.8 reshape.444
  14.9 0.8 add_compare_fusion
  15.7 0.9 convert_reduce_fusion.3
  16.6 1.2 %multiply_add_fusion.1 = s32[8,2]{0,1:T(2,128)} fusion(s32[8,2]{0,1:T(2,128)S(1)} %convert_reduce_fusion.3, s32[8,2]{0,1:T(2,128)} %param.23), kind=kLoop, calls=%fused_computation.135 | loop fusion | flops 32 | bytes 192 | tf_op jit(solution)/shard_map/add | solution.py:205
  18.1 0.9 reshape.477
  19.1 7.0 %all-to-all-start.1 = ((bf16[16,4,1536]{2,1,0:T(4,128)(2,1)}), bf16[16,4,1536]{2,1,0:T(4,128)(2,1)S(1)}, u32[]{:S(2)}, u32[]{:S(2)}) async-start(bf16[16,4,1536]{2,1,0:T(4,128)(2,1)} %reshape.477), calls=%async_computation.1 | async-start | bytes 393216 | tf_op jit(solution)/shard_map/all_to_all | solution.py:165
  26.1 8.6 %all-to-all-done.1 = bf16[16,4,1536]{2,1,0:T(4,128)(2,1)S(1)} async-done(((bf16[16,4,1536]{2,1,0:T(4,128)(2,1)}), bf16[16,4,1536]{2,1,0:T(4,128)(2,1)S(1)}, u32[]{:S(2)}, u32[]{:S(2)}) %all-to-all-start.1) | async-done | bytes 196640 | tf_op jit(solution)/shard_map/all_to_all | solution.py:165
  35.2 1.6 %fusion.27 = bf16[64,1,320]{2,0,1:T(8,128)(2,1)S(1)} fusion(bf16[1,1536,320]{1,2,0:T(8,128)(2,1)} %param.19, bf16[64,1536]{1,0:T(8,128)(2,1)S(1)} %get-tuple-element.20, f32[1536]{0:T(1024)S(1)} %copy-done.6, f32[64]{0:T(128)S(1)} %add_rsqrt_fusion.1), kind=kOutput, calls=%fused_computation.31 | convolution fusion | flops 63328256 | bytes 1227008 | tf_op jit(solution)/shard_map/sd,hdc->shc/dot_general | solution.py:25
  37.5 1.0 fusion.66
  38.5 0.9 copy.91
  39.5 5.6 %fusion.92 = (f32[320,3]{1,0:T(8,128)}, f32[320,3,128]{2,1,0:T(4,128)}) fusion(bf16[320,3,64]{2,1,0:T(4,128)(2,1)} %copy.91, bf16[320,1,128,128]{3,2,0,1:T(8,128)(2,1)} %bitcast.107, pred[320,128]{1,0:T(8,128)(4,1)} %add_compare_fusion), kind=kOutput, calls=%fused_computation.149 | convolution fusion | flops 16096320 | bytes 6106880 | tf_op jit(solution)/shard_map/pkgd,pkdt->pkgt/dot_general | solution.py:68
  45.1 1.0 copy.92
  46.8 1.9 %fusion.35 = (f32[320,3]{1,0:T(8,128)S(1)}, bf16[320,1,3,128]{3,2,0,1:T(4,128)(2,1)S(1)}) fusion(f32[320,3,128]{2,1,0:T(4,128)} %get-tuple-element.22, f32[320,3]{1,0:T(8,128)S(1)} %copy.93, pred[320,128]{1,0:T(8,128)(4,1)} %add_compare_fusion), kind=kLoop, calls=%fused_computation.44 | loop fusion | flops 490560 | bytes 785920 | tf_op jit(solution)/shard_map/reduce_sum | solution.py:92
  49.0 5.4 %fusion = f32[320,3,64]{2,1,0:T(4,128)S(1)} fusion(bf16[320,1,128,128]{3,2,0,1:T(8,128)(2,1)} %bitcast.108, bf16[320,1,3,128]{3,2,0,1:T(4,128)(2,1)S(1)} %get-tuple-element.10), kind=kOutput, calls=%fused_computation.1 | convolution fusion | flops 15728640 | bytes 5734400 | tf_op jit(solution)/shard_map/pkgt,pkdt->pkgd/dot_general | solution.py:94
  54.8 2.0 %fusion.11 = bf16[8,8,1536]{2,1,0:T(8,128)(2,1)} fusion(bf16[64,192]{0,1:T(8,128)(2,1)S(1)} %bitcast.110, bf16[1,192,1536]{2,1,0:T(8,128)(2,1)} %param.20), kind=kOutput, calls=%fused_computation.16 | convolution fusion | flops 37847040 | bytes 811008 | tf_op jit(solution)/shard_map/dot_general | solution.py:182
  56.8 4.5 %all-to-all-start.2 = ((bf16[8,8,1536]{2,1,0:T(8,128)(2,1)}), bf16[8,8,1536]{2,1,0:T(8,128)(2,1)S(1)}, u32[]{:S(2)}, u32[]{:S(2)}) async-start(bf16[8,8,1536]{2,1,0:T(8,128)(2,1)} %fusion.11), calls=%async_computation.2 | async-start | bytes 393216 | tf_op jit(solution)/shard_map/all_to_all | solution.py:183
  62.6 5.5 %all-to-all-done.2 = bf16[8,8,1536]{2,1,0:T(8,128)(2,1)S(1)} async-done(((bf16[8,8,1536]{2,1,0:T(8,128)(2,1)}), bf16[8,8,1536]{2,1,0:T(8,128)(2,1)S(1)}, u32[]{:S(2)}, u32[]{:S(2)}) %all-to-all-start.2) | async-done | bytes 196640 | tf_op jit(solution)/shard_map/all_to_all | solution.py:183
  68.3 1.0 %fusion.81 = f32[8,16]{1,0:T(8,128)S(1)} fusion(bf16[1536,16]{0,1:T(8,128)(2,1)} %param.22, bf16[8,1536]{1,0:T(8,128)(2,1)S(1)} %get-tuple-element.8, f32[1536]{0:T(1024)} %param.21, f32[8]{0:T(128)S(1)} %add_rsqrt_fusion), kind=kOutput, calls=%fused_computation.119 | convolution fusion | flops 442368 | bytes 80416 | tf_op jit(solution)/shard_map/dot_general | solution.py:190
  69.5 0.9 convolution_convert_fusion.2
  70.4 0.7 copy.97
  71.1 3.5 %all-to-all-start.3 = ((bf16[16,2,1536]{2,1,0:T(2,128)(2,1)}), bf16[16,2,1536]{2,1,0:T(2,128)(2,1)S(1)}, u32[]{:S(2)}, u32[]{:S(2)}) async-start(bf16[16,2,1536]{2,1,0:T(2,128)(2,1)} %copy.97), calls=%async_computation.3 | async-start | bytes 196608 | tf_op jit(solution)/shard_map/all_to_all | solution.py:218
  74.7 7.8 %all-to-all-done.3 = bf16[16,2,1536]{2,1,0:T(2,128)(2,1)S(1)} async-done(((bf16[16,2,1536]{2,1,0:T(2,128)(2,1)}), bf16[16,2,1536]{2,1,0:T(2,128)(2,1)S(1)}, u32[]{:S(2)}, u32[]{:S(2)}) %all-to-all-start.3) | async-done | bytes 98336 | tf_op jit(solution)/shard_map/all_to_all | solution.py:218
  82.5 2.5 %fusion.6 = f32[32,1024]{1,0:T(8,128)S(1)} fusion(bf16[32,1536]{1,0:T(8,128)(2,1)S(1)} %reshape.460, bf16[1,1536,2048]{2,1,0:T(8,128)(2,1)} %param.24), kind=kOutput, calls=%fused_computation.8 | convolution fusion | flops 100663296 | bytes 3375104 | tf_op jit(solution)/shard_map/erd,edf->erf/dot_general | solution.py:116
  85.0 3.1 %fusion.12 = bf16[32,1536]{1,0:T(8,128)(2,1)S(1)} fusion(bf16[1,1024,1536]{2,1,0:T(8,128)(2,1)S(1)} %copy-done, bf16[32,1536]{1,0:T(8,128)(2,1)S(1)} %reshape.460, bf16[1,1536,2048]{2,1,0:T(8,128)(2,1)} %param.24, f32[32,1024]{1,0:T(8,128)S(1)} %fusion.6), kind=kOutput, calls=%fused_computation.17 | convolution fusion | flops 201572352 | bytes 6619136 | tf_op jit(solution)/shard_map/erf,efd->erd/dot_general | solution.py:123
  88.8 3.5 %all-to-all-start.4 = ((bf16[16,2,1536]{2,1,0:T(2,128)(2,1)}), bf16[16,2,1536]{2,1,0:T(2,128)(2,1)S(1)}, u32[]{:S(2)}, u32[]{:S(2)}) async-start(bf16[16,2,1536]{2,1,0:T(2,128)(2,1)} %reshape_transpose_reshape.4), calls=%async_computation.4 | async-start | bytes 196608 | tf_op jit(solution)/shard_map/all_to_all | solution.py:222
  92.3 7.8 %all-to-all-done.4 = bf16[16,2,1536]{2,1,0:T(2,128)(2,1)S(1)} async-done(((bf16[16,2,1536]{2,1,0:T(2,128)(2,1)}), bf16[16,2,1536]{2,1,0:T(2,128)(2,1)S(1)}, u32[]{:S(2)}, u32[]{:S(2)}) %all-to-all-start.4) | async-done | bytes 98336 | tf_op jit(solution)/shard_map/all_to_all | solution.py:222
  (70 shorter events, 9.1 us)
Async XLA Ops:
  0.0 85.0 %copy-start = (bf16[1,1024,1536]{2,1,0:T(8,128)(2,1)S(1)}, bf16[1,1024,1536]{2,1,0:T(8,128)(2,1)}, u32[]{:S(2)}) copy-start(bf16[1,1024,1536]{2,1,0:T(8,128)(2,1)} %param.25) | copy-start | bytes 9437188
  0.0 35.2 %copy-start.6 = (f32[1536]{0:T(1024)S(1)}, f32[1536]{0:T(1024)}, u32[]{:S(2)}) copy-start(f32[1536]{0:T(1024)} %param.18) | copy-start | bytes 18436
  1.6 16.2 %all-to-all-start = ((bf16[8,64,192]{2,1,0:T(8,128)(2,1)}), bf16[8,64,192]{2,1,0:T(8,128)(2,1)S(1)}, u32[]{:S(2)}, u32[]{:S(2)}) async-start(bf16[8,64,192]{2,1,0:T(8,128)(2,1)} %broadcast_in_dim.78), calls=%async_computation | async-start | bytes 524288 | tf_op jit(solution)/shard_map/all_to_all | solution.py:151
  19.1 15.7 %all-to-all-start.1 = ((bf16[16,4,1536]{2,1,0:T(4,128)(2,1)}), bf16[16,4,1536]{2,1,0:T(4,128)(2,1)S(1)}, u32[]{:S(2)}, u32[]{:S(2)}) async-start(bf16[16,4,1536]{2,1,0:T(4,128)(2,1)} %reshape.477), calls=%async_computation.1 | async-start | bytes 393216 | tf_op jit(solution)/shard_map/all_to_all | solution.py:165
  35.2 10.9 %copy-start.1 = (pred[64,320]{1,0:T(8,128)(4,1)S(1)}, pred[64,320]{1,0:T(8,128)(4,1)}, u32[]{:S(2)}) copy-start(pred[64,320]{1,0:T(8,128)(4,1)} %slice_compare_fusion) | copy-start | bytes 61444
  36.8 1.7 %copy-start.2 = (bf16[64,1,320]{2,0,1:T(8,128)(2,1)}, bf16[64,1,320]{2,0,1:T(8,128)(2,1)S(1)}, u32[]{:S(2)}) copy-start(bf16[64,1,320]{2,0,1:T(8,128)(2,1)S(1)} %fusion.27) | copy-start | bytes 122884
  39.5 6.8 %copy-start.3 = (f32[64,64]{1,0:T(8,128)S(1)}, f32[64,64]{1,0:T(8,128)}, u32[]{:S(2)}) copy-start(f32[64,64]{1,0:T(8,128)} %get-tuple-element.12) | copy-start | bytes 49156
  39.5 6.9 %slice-start = ((bf16[64,1,320]{2,0,1:T(8,128)(2,1)}), bf16[64,1,192]{2,0,1:T(8,128)(2,1)S(1)}, s32[]{:S(2)}) async-start(bf16[64,1,320]{2,0,1:T(8,128)(2,1)} %copy-done.2), calls=%async_computation.5 | async-start | bytes 65536 | tf_op jit(solution)/shard_map/slice | solution.py:27
  46.5 22.9 %copy-start.5 = (s32[8,2]{0,1:T(2,128)S(1)}, s32[8,2]{0,1:T(2,128)}, u32[]{:S(2)}) copy-start(s32[8,2]{0,1:T(2,128)} %param.23) | copy-start | bytes 196
  46.8 7.6 %copy-start.4 = (f32[64,64]{1,0:T(8,128)S(1)}, f32[64,64]{1,0:T(8,128)}, u32[]{:S(2)}) copy-start(f32[64,64]{1,0:T(8,128)} %get-tuple-element.11) | copy-start | bytes 49156
  56.8 11.3 %all-to-all-start.2 = ((bf16[8,8,1536]{2,1,0:T(8,128)(2,1)}), bf16[8,8,1536]{2,1,0:T(8,128)(2,1)S(1)}, u32[]{:S(2)}, u32[]{:S(2)}) async-start(bf16[8,8,1536]{2,1,0:T(8,128)(2,1)} %fusion.11), calls=%async_computation.2 | async-start | bytes 393216 | tf_op jit(solution)/shard_map/all_to_all | solution.py:183
  71.1 11.3 %all-to-all-start.3 = ((bf16[16,2,1536]{2,1,0:T(2,128)(2,1)}), bf16[16,2,1536]{2,1,0:T(2,128)(2,1)S(1)}, u32[]{:S(2)}, u32[]{:S(2)}) async-start(bf16[16,2,1536]{2,1,0:T(2,128)(2,1)} %copy.97), calls=%async_computation.3 | async-start | bytes 196608 | tf_op jit(solution)/shard_map/all_to_all | solution.py:218
  82.5 17.6 %copy-start.7 = (s32[8,2]{0,1:T(2,128)S(1)}, s32[8,2]{0,1:T(2,128)}, u32[]{:S(2)}) copy-start(s32[8,2]{0,1:T(2,128)} %multiply_add_fusion.1) | copy-start | bytes 196
  88.8 11.3 %all-to-all-start.4 = ((bf16[16,2,1536]{2,1,0:T(2,128)(2,1)}), bf16[16,2,1536]{2,1,0:T(2,128)(2,1)S(1)}, u32[]{:S(2)}, u32[]{:S(2)}) async-start(bf16[16,2,1536]{2,1,0:T(2,128)(2,1)} %reshape_transpose_reshape.4), calls=%async_computation.4 | async-start | bytes 196608 | tf_op jit(solution)/shard_map/all_to_all | solution.py:222

commit v17 on v14

--- a/solution.py
+++ b/solution.py
@@ -159,18 +159,17 @@
     outgoing_rows = jnp.einsum(
         "dir,jrc->dijc", send_pick, block_parts, preferred_element_type=jnp.float32
     ).astype(hidden.dtype)
-    arrived_rows = lax.all_to_all(
-        outgoing_rows.reshape(n_req, deal, width), "req", split_axis=0, concat_axis=0, tiled=True
-    ).reshape(n_req * deal, width)
+    arrived_rows = lax.all_to_all(outgoing_rows, "req", split_axis=0, concat_axis=0, tiled=True)
     my_source = lax.dynamic_slice_in_dim(source_block, req_index, 1, 0).reshape(local_rows)
     slot_ids = jnp.arange(local_rows, dtype=jnp.int32)
     same_before = (my_source[None, :] == my_source[:, None]) & (slot_ids[None, :] < slot_ids[:, None])
     rank_got = jnp.sum(same_before.astype(jnp.int32), axis=1)
     take_key = my_source * deal + rank_got
     take_pick = (take_key[:, None] == slot_ids[None, :]).astype(hidden.dtype)
-    tokens = jnp.dot(take_pick, arrived_rows, preferred_element_type=jnp.float32).astype(
-        hidden.dtype
-    )
+    tokens = jnp.einsum(
+        "sri,rijc->sjc", take_pick.reshape(local_rows, n_req, deal), arrived_rows,
+        preferred_element_type=jnp.float32,
+    ).astype(hidden.dtype).reshape(local_rows, width)
     normed = rms_norm(tokens, attn_gain)
     head_out = attend(normed, seq_lens, page_table, kv_cache, qkv_weight)
     sub_rows = routes.shape[0]

time: 101 us -> 109 us (1.079)
  local copies, waits for them, and re-layouts: 8.53 us -> 18.1 us
  other arithmetic: 12.2 us -> 11.1 us
    convert_element_type x0 -> x4, local copies, waits for them, and re-layouts: none -> 4.39 us  [the longest x2 2.72 us: rms_norm(): return (values * factor * gain_vec).astype(jnp.bfloat16)]
    unnamed x17 -> x9, local copies, waits for them, and re-layouts: 0.11 us -> 1.49 us
    slice x3 -> x2, local copies, waits for them, and re-layouts: 0.11 us -> 1.47 us  [attend(): projected[:, :, :groups * head_dim]]
  transfers between devices with their start and end apart: 5 -> 5, of which waited for: 4 -> 4; matrix products, arithmetic and copies ran while one was open for 12% -> 10% of each run, Pallas kernels for 0% -> 0%
where the time goes in v17:
time: 109 us; the launch traced here: 108 us
  waiting for transfers between devices  29.7 us (27%)
  matrix products  24.8 us (23%)
  starting transfers between devices  23.9 us (22%)
  local copies, waits for them, and re-layouts  18.1 us (17%)
  other arithmetic  11.1 us (10%)
    all_to_all x1, waiting for transfers between devices, shards(): lax.all_to_all(outgoing_rows, 'req', split_axis=0, concat_axis=0, tiled=T...  9.38 us
    all_to_all x1, waiting for transfers between devices, shards(): lax.all_to_all(expert_rows, 'req', split_axis=0, concat_axis=0, tiled=True)  7.76 us
    all_to_all x1, waiting for transfers between devices, shards(): lax.all_to_all(outgoing, 'req', split_axis=0, concat_axis=0, tiled=True)  7.75 us
    all_to_all x1, starting transfers between devices, shards(): lax.all_to_all(outgoing_rows, 'req', split_axis=0, concat_axis=0, tiled=T...  7.09 us
    dot_general x1, matrix products, attend(): jnp.einsum('pkgd,pkdt->pkgt', page_queries, kv_cache[:, :, :head_dim, :],...  5.62 us
    all_to_all x1, starting transfers between devices, shards(): lax.all_to_all(spread, 'kv', split_axis=0, concat_axis=0, tiled=True)  5.4 us
    dot_general x1, matrix products, attend(): jnp.einsum('pkgt,pkdt->pkgd', rounded_weights, kv_cache[:, :, head_dim:,...  5.36 us
    all_to_all x1, waiting for transfers between devices, shards(): lax.all_to_all(partial.reshape(n_kv, sub_rows, partial.shape[1]), 'kv', s...  4.82 us
  transfers between devices with their start and end apart: 5, of which 4 were waited for; matrix products, arithmetic and copies ran while one was open for 10% of the time, Pallas kernels for 0%

profile of v17, /device:TPU:0, one launch (start us, length us, event | category | flops | bytes accessed | tf_op | source)
XLA Modules:
  0.0 108.0 jit_solution(18207975390608812974)
XLA Ops:
  0.0 1.6 %broadcast_in_dim.78 = bf16[8,64,192]{2,1,0:T(8,128)(2,1)} broadcast(bf16[64,192]{1,0:T(8,128)(2,1)} %param.13), dimensions={1,2} | broadcast | bytes 221184 | tf_op jit(solution)/shard_map/broadcast_in_dim | solution.py:147
  1.6 5.4 %all-to-all-start = ((bf16[8,64,192]{2,1,0:T(8,128)(2,1)}), bf16[8,64,192]{2,1,0:T(8,128)(2,1)S(1)}, u32[]{:S(2)}, u32[]{:S(2)}) async-start(bf16[8,64,192]{2,1,0:T(8,128)(2,1)} %broadcast_in_dim.78), calls=%async_computation | async-start | bytes 524288 | tf_op jit(solution)/shard_map/all_to_all | solution.py:148
  9.7 0.8 fusion.6
  12.9 0.9 convert_reduce_fusion.3
  15.5 0.8 copy.91
  16.4 7.1 %all-to-all-start.1 = ((bf16[16,4,8,192]{3,1,2,0:T(4,128)(2,1)}), bf16[16,4,8,192]{3,1,2,0:T(4,128)(2,1)}, u32[]{:S(2)}, u32[]{:S(2)}) async-start(bf16[16,4,8,192]{3,1,2,0:T(4,128)(2,1)} %copy.91), calls=%async_computation.1 | async-start | bytes 524288 | tf_op jit(solution)/shard_map/all_to_all | solution.py:162
  23.5 9.4 %all-to-all-done.1 = bf16[16,4,8,192]{3,1,2,0:T(4,128)(2,1)} async-done(((bf16[16,4,8,192]{3,1,2,0:T(4,128)(2,1)}), bf16[16,4,8,192]{3,1,2,0:T(4,128)(2,1)}, u32[]{:S(2)}, u32[]{:S(2)}) %all-to-all-start.1) | async-done | bytes 196640 | tf_op jit(solution)/shard_map/all_to_all | solution.py:162
  32.9 1.4 %fusion.26 = (f32[64]{0:T(128)S(1)}, bf16[64,8,192]{2,0,1:T(8,128)(2,1)S(1)}) fusion(bf16[16,4,8,192]{3,1,2,0:T(4,128)(2,1)} %all-to-all-done.1, s32[16,4]{0,1:T(4,128)S(1)} %multiply_add_fusion, s32[64]{0:T(128)S(1)} %multiply_add_fusion.3), kind=kOutput, calls=%fused_computation.37 | convolution fusion | flops 12980160 | bytes 393984 | tf_op jit(solution)/shard_map/sri,rijc->sjc/dot_general | solution.py:169
  34.4 0.8 copy.95
  35.3 1.9 %convert_element_type.184 = bf16[64,1536]{1,0:T(8,128)(2,1)} reshape(bf16[64,8,192]{2,1,0:T(8,128)(2,1)} %copy.95) | data formatting | bytes 393216 | tf_op jit(solution)/shard_map/convert_element_type | solution.py:16
  37.1 1.7 %fusion.21 = bf16[64,1,320]{2,0,1:T(8,128)(2,1)S(1)} fusion(bf16[64,1536]{1,0:T(8,128)(2,1)} %convert_element_type.184, bf16[1,1536,320]{1,2,0:T(8,128)(2,1)} %param.19), kind=kOutput, calls=%fused_computation.27 | convolution fusion | flops 62935040 | bytes 1220608 | tf_op jit(solution)/shard_map/sd,hdc->shc/dot_general | solution.py:25
  40.2 0.9 copy.96
  41.0 1.5 %copy.116 = f32[64,64]{0,1:T(8,128)} copy(f32[64,64]{1,0:T(8,128)} %get-tuple-element.12) | data formatting | bytes 32768
  43.4 1.8 %copy.98 = bf16[320,3,64]{2,1,0:T(4,128)(2,1)} copy(bf16[320,3,64]{0,2,1:T(8,128)(2,1)} %convert_element_type.186) | data formatting | bytes 245760 | tf_op jit(solution)/shard_map/convert_element_type | solution.py:66
  45.2 5.6 %fusion.83 = (f32[320,3]{1,0:T(8,128)}, f32[320,3,128]{2,1,0:T(4,128)}) fusion(bf16[320,3,64]{2,1,0:T(4,128)(2,1)} %copy.98, bf16[320,1,128,128]{3,2,0,1:T(8,128)(2,1)} %bitcast.116, pred[320,128]{1,0:T(8,128)(4,1)} %add_compare_fusion), kind=kOutput, calls=%fused_computation.145 | convolution fusion | flops 16096320 | bytes 6106880 | tf_op jit(solution)/shard_map/pkgd,pkdt->pkgt/dot_general | solution.py:68
  50.9 1.0 copy.99
  52.9 0.8 copy.100
  53.8 2.0 %fusion.30 = (f32[320,3]{1,0:T(8,128)S(1)}, bf16[320,1,3,128]{3,2,0,1:T(4,128)(2,1)S(1)}) fusion(f32[320,3,128]{2,1,0:T(4,128)} %get-tuple-element.22, f32[320,3]{1,0:T(8,128)} %copy.100, pred[320,128]{1,0:T(8,128)(4,1)S(1)} %copy-done.1), kind=kLoop, calls=%fused_computation.43 | loop fusion | flops 490560 | bytes 785920 | tf_op jit(solution)/shard_map/reduce_sum | solution.py:92
  56.0 5.4 %fusion.2 = f32[320,3,64]{2,1,0:T(4,128)S(1)} fusion(bf16[320,1,128,128]{3,2,0,1:T(8,128)(2,1)} %bitcast.117, bf16[320,1,3,128]{3,2,0,1:T(4,128)(2,1)S(1)} %get-tuple-element.10), kind=kOutput, calls=%fused_computation.3 | convolution fusion | flops 15728640 | bytes 5734400 | tf_op jit(solution)/shard_map/pkgt,pkdt->pkgd/dot_general | solution.py:94
  61.3 1.1 %fusion.19 = bf16[64,3,64]{2,0,1:T(8,128)(2,1)S(1)} fusion(f32[320,3,64]{2,1,0:T(4,128)S(1)} %fusion.2, pred[64,320]{1,0:T(8,128)(4,1)S(1)} %slice_compare_fusion, f32[64,3]{0,1:T(4,128)S(1)} %convolution_add_fusion.1, f32[64,64]{1,0:T(8,128)} %get-tuple-element.11, f32[64,3]{0,1:T(4,128)S(1)} %bitcast_convert_fusion), kind=kOutput, calls=%fused_computation.24 | convolution fusion | flops 47235072 | bytes 308736 | tf_op jit(solution)/shard_map/sp,pkgd->skgd/dot_general | solution.py:102
  62.6 2.0 %fusion.7 = bf16[8,8,1536]{2,1,0:T(8,128)(2,1)} fusion(bf16[64,192]{0,1:T(8,128)(2,1)S(1)} %bitcast.119, bf16[1,192,1536]{2,1,0:T(8,128)(2,1)} %param.20), kind=kOutput, calls=%fused_computation.11 | convolution fusion | flops 37847040 | bytes 811008 | tf_op jit(solution)/shard_map/dot_general | solution.py:178
  64.6 4.4 %all-to-all-start.2 = ((bf16[8,8,1536]{2,1,0:T(8,128)(2,1)}), bf16[8,8,1536]{2,1,0:T(8,128)(2,1)}, u32[]{:S(2)}, u32[]{:S(2)}) async-start(bf16[8,8,1536]{2,1,0:T(8,128)(2,1)} %fusion.7), calls=%async_computation.2 | async-start | bytes 393216 | tf_op jit(solution)/shard_map/all_to_all | solution.py:179
  69.1 0.8 copy.93
  69.9 1.2 %reshape.459 = bf16[64,1536]{1,0:T(8,128)(2,1)S(1)} reshape(bf16[64,8,192]{2,1,0:T(8,128)(2,1)} %copy.93) | data formatting | bytes 393216 | tf_op jit(solution)/shard_map/reshape | solution.py:172
  71.1 4.8 %all-to-all-done.2 = bf16[8,8,1536]{2,1,0:T(8,128)(2,1)} async-done(((bf16[8,8,1536]{2,1,0:T(8,128)(2,1)}), bf16[8,8,1536]{2,1,0:T(8,128)(2,1)}, u32[]{:S(2)}, u32[]{:S(2)}) %all-to-all-start.2) | async-done | bytes 196640 | tf_op jit(solution)/shard_map/all_to_all | solution.py:179
  75.9 1.0 convert_reduce_fusion
  77.1 1.0 fusion.72
  79.2 3.5 %all-to-all-start.3 = ((bf16[16,2,1536]{2,1,0:T(2,128)(2,1)}), bf16[16,2,1536]{2,1,0:T(2,128)(2,1)S(1)}, u32[]{:S(2)}, u32[]{:S(2)}) async-start(bf16[16,2,1536]{2,1,0:T(2,128)(2,1)} %copy.104), calls=%async_computation.3 | async-start | bytes 196608 | tf_op jit(solution)/shard_map/all_to_all | solution.py:214
  82.7 7.8 %all-to-all-done.3 = bf16[16,2,1536]{2,1,0:T(2,128)(2,1)S(1)} async-done(((bf16[16,2,1536]{2,1,0:T(2,128)(2,1)}), bf16[16,2,1536]{2,1,0:T(2,128)(2,1)S(1)}, u32[]{:S(2)}, u32[]{:S(2)}) %all-to-all-start.3) | async-done | bytes 98336 | tf_op jit(solution)/shard_map/all_to_all | solution.py:214
  90.5 4.0 %fusion.8 = f32[1,32,2048]{2,1,0:T(8,128)S(1)} fusion(bf16[32,1536]{1,0:T(8,128)(2,1)S(1)} %reshape.470, bf16[1,1536,2048]{2,1,0:T(8,128)(2,1)} %param.24), kind=kOutput, calls=%fused_computation.12 | convolution fusion | flops 201326592 | bytes 6651904 | tf_op jit(solution)/shard_map/erd,edf->erf/dot_general | solution.py:115
  95.8 3.5 %all-to-all-start.4 = ((bf16[16,2,1536]{2,1,0:T(2,128)(2,1)}), bf16[16,2,1536]{2,1,0:T(2,128)(2,1)S(1)}, u32[]{:S(2)}, u32[]{:S(2)}) async-start(bf16[16,2,1536]{2,1,0:T(2,128)(2,1)} %reshape_transpose_reshape.4), calls=%async_computation.4 | async-start | bytes 196608 | tf_op jit(solution)/shard_map/all_to_all | solution.py:218
  99.3 7.8 %all-to-all-done.4 = bf16[16,2,1536]{2,1,0:T(2,128)(2,1)S(1)} async-done(((bf16[16,2,1536]{2,1,0:T(2,128)(2,1)}), bf16[16,2,1536]{2,1,0:T(2,128)(2,1)S(1)}, u32[]{:S(2)}, u32[]{:S(2)}) %all-to-all-start.4) | async-done | bytes 98336 | tf_op jit(solution)/shard_map/all_to_all | solution.py:218
  (66 shorter events, 14.0 us)
Async XLA Ops:
  0.0 94.5 %copy-start = (bf16[1,1024,1536]{2,1,0:T(8,128)(2,1)S(1)}, bf16[1,1024,1536]{2,1,0:T(8,128)(2,1)}, u32[]{:S(2)}) copy-start(bf16[1,1024,1536]{2,1,0:T(8,128)(2,1)} %param.25) | copy-start | bytes 9437188
  1.6 13.7 %all-to-all-start = ((bf16[8,64,192]{2,1,0:T(8,128)(2,1)}), bf16[8,64,192]{2,1,0:T(8,128)(2,1)S(1)}, u32[]{:S(2)}, u32[]{:S(2)}) async-start(bf16[8,64,192]{2,1,0:T(8,128)(2,1)} %broadcast_in_dim.78), calls=%async_computation | async-start | bytes 524288 | tf_op jit(solution)/shard_map/all_to_all | solution.py:148
  16.4 16.5 %all-to-all-start.1 = ((bf16[16,4,8,192]{3,1,2,0:T(4,128)(2,1)}), bf16[16,4,8,192]{3,1,2,0:T(4,128)(2,1)}, u32[]{:S(2)}, u32[]{:S(2)}) async-start(bf16[16,4,8,192]{3,1,2,0:T(4,128)(2,1)} %copy.91), calls=%async_computation.1 | async-start | bytes 524288 | tf_op jit(solution)/shard_map/all_to_all | solution.py:162
  42.7 11.0 %copy-start.1 = (pred[320,128]{1,0:T(8,128)(4,1)S(1)}, pred[320,128]{1,0:T(8,128)(4,1)}, u32[]{:S(2)}) copy-start(pred[320,128]{1,0:T(8,128)(4,1)} %add_compare_fusion) | copy-start | bytes 122884
  53.7 23.3 %copy-start.3 = (f32[1536]{0:T(1024)S(1)}, f32[1536]{0:T(1024)}, u32[]{:S(2)}) copy-start(f32[1536]{0:T(1024)} %param.21) | copy-start | bytes 18436
  55.7 22.3 %copy-start.2 = (s32[8,2]{0,1:T(2,128)S(1)}, s32[8,2]{0,1:T(2,128)}, u32[]{:S(2)}) copy-start(s32[8,2]{0,1:T(2,128)} %param.23) | copy-start | bytes 196
  64.6 11.4 %all-to-all-start.2 = ((bf16[8,8,1536]{2,1,0:T(8,128)(2,1)}), bf16[8,8,1536]{2,1,0:T(8,128)(2,1)}, u32[]{:S(2)}, u32[]{:S(2)}) async-start(bf16[8,8,1536]{2,1,0:T(8,128)(2,1)} %fusion.7), calls=%async_computation.2 | async-start | bytes 393216 | tf_op jit(solution)/shard_map/all_to_all | solution.py:179
  79.2 11.3 %all-to-all-start.3 = ((bf16[16,2,1536]{2,1,0:T(2,128)(2,1)}), bf16[16,2,1536]{2,1,0:T(2,128)(2,1)S(1)}, u32[]{:S(2)}, u32[]{:S(2)}) async-start(bf16[16,2,1536]{2,1,0:T(2,128)(2,1)} %copy.104), calls=%async_computation.3 | async-start | bytes 196608 | tf_op jit(solution)/shard_map/all_to_all | solution.py:214
  95.8 11.3 %all-to-all-start.4 = ((bf16[16,2,1536]{2,1,0:T(2,128)(2,1)}), bf16[16,2,1536]{2,1,0:T(2,128)(2,1)S(1)}, u32[]{:S(2)}, u32[]{:S(2)}) async-start(bf16[16,2,1536]{2,1,0:T(2,128)(2,1)} %reshape_transpose_reshape.4), calls=%async_computation.4 | async-start | bytes 196608 | tf_op jit(solution)/shard_map/all_to_all | solution.py:218
